TPU v7x, 512 devices: a whole 4x4x16 slice. The times are simulated.
512 devices in a mesh: dp: 8 (over x, core), expert: 64 (over y, z).
Axes of the slice: x: 4, y: 4, z: 16, core: 2. Of those that a mesh axis runs over, the one named last changes fastest.
Arguments:
- query_rows: bfloat16 [65536, 2048], P(('dp', 'expert')), may hold values from -40 to 40
- key_rows: bfloat16 [65536, 256], P(('dp', 'expert')), may hold values from -40 to 40
- value_rows: bfloat16 [65536, 256], P(('dp', 'expert')), may hold values from -6 to 6
- residual: bfloat16 [65536, 1024], P(('dp', 'expert')), may hold values from -25 to 25
- document_owner: int32 [512, 8], P(('dp', 'expert')), may hold values from 0 to 7, as said below
- document_length: int32 [512, 8], P(('dp', 'expert')), may hold values from 8 to 24, as said below
- document_offset: int32 [512, 8], P(('dp', 'expert')), may hold values from 0 to 120, as said below
- query_gain: float32 [128], replicated, may hold values from 0.3 to 5.5
- key_gain: float32 [128], replicated, may hold values from 0.3 to 5.5
- output_weight: bfloat16 [2048, 1024], P('expert'), may hold values from -0.125 to 0.125
- post_gain: float32 [1024], replicated, may hold values from 0.5 to 2
- routes: int32 [65536, 8], P(('dp', 'expert')), may hold values from 0 to 63, all different within a row; in each aligned block of 128 rows (0 to 127, 128 to 255, ...) at most 20 rows name the same one
- route_weight: float32 [65536, 8], P(('dp', 'expert')), may hold values from 0.1 to 1
- gate_weight: bfloat16 [64, 768, 1024], P('expert', 'dp'), may hold values from -0.1875 to 0.1875
- up_weight: bfloat16 [64, 768, 1024], P('expert', 'dp'), may hold values from -0.1875 to 0.1875
- down_weight: bfloat16 [64, 768, 1024], P('expert', 'dp'), may hold values from -0.21875 to 0.21875
Outputs:
- layer_out: bfloat16 [65536, 1024], P(('dp', 'expert'))
Inputs may be any that keep to these rules, and one draw needn't show every extreme that they name: `document_owner`: each device's row names every dp index once, so a device sends exactly one document to each pack owner of its expert column. `document_length`: A device's lengths sum to 128; the documents that all devices of an expert column send to one owner also sum to 128; no device sends more than 24 rows to one owner, and some device does in every column. `document_offset`: the documents that reach one owner cover its 128 pack rows exactly once. `routes`: at most 20 of one device's rows name one expert; a row names 8 different experts.
All inputs are finite; a program needn't handle non-finite values.
Results may differ from a plain program's by a relative error of at most 0.012.
The roundings to bfloat16 on the way count: a program that leaves them out, or rounds other values in their place, can miss the bound.
Values may be sent and summed in bfloat16 or wider, within the bound.
No kernel may reach another device: no remote copies, remote signals or barrier semaphores. Data moves between devices by JAX's collectives and lax.ppermute only.
A program may use at most 64 MiB of HBM per device.

v0:
```python
import jax
import jax.numpy as jnp
from jax import lax
from jax.sharding import PartitionSpec as P

norm_epsilon = 1e-06
rope_base = 1000000.0


def rms_scale(values, gain):
    mean_square = jnp.mean(values * values, axis=-1, keepdims=True)
    return values * lax.rsqrt(mean_square + norm_epsilon) * gain


def rotary(values, positions):
    head_width = values.shape[-1]
    half_width = head_width // 2
    frequency = rope_base ** (-2.0 * jnp.arange(half_width, dtype=jnp.float32) / head_width)
    angles = positions.astype(jnp.float32)[:, None] * frequency[None, :]
    cosine_part = jnp.cos(angles)[:, None, :]
    sine_part = jnp.sin(angles)[:, None, :]
    leading = values[..., :half_width]
    trailing = values[..., half_width:]
    return jnp.concatenate(
        [
            leading * cosine_part - trailing * sine_part,
            trailing * cosine_part + leading * sine_part,
        ],
        axis=-1,
    )


def attend(query_part, key_part, value_part, identity, position, query_gain, key_gain):
    row_total = query_part.shape[0]
    head_width = query_gain.shape[0]
    head_count = query_part.shape[1] // head_width
    key_heads = key_part.shape[1] // head_width
    group_size = head_count // key_heads
    queries = rotary(
        rms_scale(
            query_part.reshape(row_total, head_count, head_width).astype(jnp.float32), query_gain
        ),
        position,
    ).astype(jnp.bfloat16)
    keys_normed = rotary(
        rms_scale(key_part.reshape(row_total, key_heads, head_width).astype(jnp.float32), key_gain),
        position,
    ).astype(jnp.bfloat16)
    queries = queries.reshape(row_total, key_heads, group_size, head_width)
    scores = jnp.einsum(
        "pkgd,qkd->kgpq", queries, keys_normed, preferred_element_type=jnp.float32
    ) * head_width ** (-0.5)
    allowed = (identity[:, None] == identity[None, :]) & (position[None, :] <= position[:, None])
    scores = jnp.where(allowed, scores, -jnp.inf)
    largest = jnp.max(scores, axis=-1, keepdims=True)
    powers = jnp.exp(scores - largest)
    weights = (powers / jnp.sum(powers, axis=-1, keepdims=True)).astype(jnp.bfloat16)
    values_heads = value_part.reshape(row_total, key_heads, head_width)
    mixed = jnp.einsum("kgpq,qkd->pkgd", weights, values_heads, preferred_element_type=jnp.float32)
    return mixed.astype(jnp.bfloat16).reshape(row_total, head_count * head_width)


def project_heads(attended, output_weight):
    return jnp.dot(
        attended,
        lax.all_gather(output_weight, "expert", axis=0, tiled=True),
        preferred_element_type=jnp.float32,
    )


def hidden_product(block, gate_part, up_part, down_part):
    contract = (((1,), (1,)), ((), ()))
    gate_value = lax.dot_general(block, gate_part, contract, preferred_element_type=jnp.float32)
    up_value = lax.dot_general(block, up_part, contract, preferred_element_type=jnp.float32)
    active = (jax.nn.silu(gate_value) * up_value).astype(jnp.bfloat16)
    return jnp.dot(active, down_part, preferred_element_type=jnp.float32)


def expert_output(work_rows, gate_part, up_part, down_part):
    return hidden_product(work_rows, gate_part, up_part, down_part)


def local(
    query_rows,
    key_rows,
    value_rows,
    residual,
    document_owner,
    document_length,
    document_offset,
    query_gain,
    key_gain,
    output_weight,
    post_gain,
    routes,
    route_weight,
    gate_weight,
    up_weight,
    down_weight,
):
    owner_total = lax.axis_size("dp")
    expert_total = lax.axis_size("expert")
    row_total = query_rows.shape[0]
    capacity = row_total * 3 // (2 * owner_total)
    owners = document_owner[0]
    lengths = document_length[0]
    offsets = document_offset[0]
    starts = jnp.cumsum(lengths) - lengths
    owner_ids = jnp.arange(owner_total, dtype=jnp.int32)
    matches = owners[None, :] == owner_ids[:, None]
    start_of = jnp.sum(jnp.where(matches, starts[None, :], 0), axis=1)
    length_of = jnp.sum(jnp.where(matches, lengths[None, :], 0), axis=1)
    offset_of = jnp.sum(jnp.where(matches, offsets[None, :], 0), axis=1)
    slot_ids = jnp.arange(capacity, dtype=jnp.int32)
    source_rows = jnp.minimum(start_of[:, None] + slot_ids[None, :], row_total - 1).reshape(-1)
    pack_slot = jnp.where(
        slot_ids[None, :] < length_of[:, None], offset_of[:, None] + slot_ids[None, :], -1
    )
    total_slots = owner_total * capacity
    flat_slots = jnp.arange(total_slots, dtype=jnp.int32)
    pack_ids = jnp.arange(row_total, dtype=jnp.int32)
    got_query, got_key, got_value, got_residual, got_slot = (
        lax.all_to_all(
            query_rows[source_rows].reshape(owner_total, capacity, -1),
            "dp",
            split_axis=0,
            concat_axis=0,
            tiled=True,
        ),
        lax.all_to_all(
            key_rows[source_rows].reshape(owner_total, capacity, -1),
            "dp",
            split_axis=0,
            concat_axis=0,
            tiled=True,
        ),
        lax.all_to_all(
            value_rows[source_rows].reshape(owner_total, capacity, -1),
            "dp",
            split_axis=0,
            concat_axis=0,
            tiled=True,
        ),
        lax.all_to_all(
            residual[source_rows].reshape(owner_total, capacity, -1),
            "dp",
            split_axis=0,
            concat_axis=0,
            tiled=True,
        ),
        lax.all_to_all(pack_slot, "dp", split_axis=0, concat_axis=0, tiled=True),
    )
    placed = got_slot.reshape(-1)[None, :] == pack_ids[:, None]
    slot_of = jnp.sum(jnp.where(placed, flat_slots[None, :], 0), axis=1)
    pack_query = got_query.reshape(total_slots, -1)[slot_of]
    pack_key = got_key.reshape(total_slots, -1)[slot_of]
    pack_value = got_value.reshape(total_slots, -1)[slot_of]
    pack_residual = got_residual.reshape(total_slots, -1)[slot_of]
    identity = slot_of // capacity
    position = slot_of % capacity
    attended = attend(pack_query, pack_key, pack_value, identity, position, query_gain, key_gain)
    hidden_state = pack_residual.astype(jnp.float32) + project_heads(attended, output_weight)
    normed = rms_scale(hidden_state, post_gain).astype(jnp.bfloat16)
    top_total = routes.shape[1]
    most = row_total * top_total * 5 // (4 * expert_total)
    expert_ids = jnp.arange(expert_total, dtype=jnp.int32)
    routed = routes[:, :, None] == expert_ids[None, None, :]
    chosen = jnp.sum(routed.astype(jnp.int32), axis=1)
    earlier = (pack_ids[None, :] < pack_ids[:, None]).astype(jnp.int32)
    rank = jnp.dot(earlier, chosen)
    ranked = jnp.where(chosen > 0, rank, -1)
    place_ids = jnp.arange(most, dtype=jnp.int32)
    hits = ranked.T[:, :, None] == place_ids[None, None, :]
    source_token = jnp.sum(jnp.where(hits, pack_ids[None, :, None], 0), axis=1)
    outgoing = normed[source_token.reshape(-1)].reshape(expert_total, most, -1)
    total_rows = expert_total * most
    received = lax.all_to_all(outgoing, "expert", split_axis=0, concat_axis=0, tiled=True)
    work_rows = received.reshape(total_rows, -1)
    gate_whole, up_whole, down_whole = (
        lax.all_gather(gate_weight, "dp", axis=1, tiled=True),
        lax.all_gather(up_weight, "dp", axis=1, tiled=True),
        lax.all_gather(down_weight, "dp", axis=1, tiled=True),
    )
    produced = expert_output(work_rows, gate_whole[0], up_whole[0], down_whole[0])
    produced = produced.astype(jnp.bfloat16)
    out_slots = produced.reshape(expert_total, most, -1)
    returned = lax.all_to_all(out_slots, "expert", split_axis=0, concat_axis=0, tiled=True)
    flat_back = returned.reshape(total_rows, -1)
    copy_rank = jnp.sum(jnp.where(routed, rank[:, None, :], 0), axis=2)
    copy_index = routes * most + copy_rank
    gates = route_weight / jnp.sum(route_weight, axis=1, keepdims=True)
    mixture = jnp.zeros(hidden_state.shape, jnp.float32)
    for route_slot in range(top_total):
        mixture = mixture + gates[:, route_slot : route_slot + 1] * flat_back[
            copy_index[:, route_slot]
        ].astype(jnp.float32)
    return (hidden_state + mixture).astype(jnp.bfloat16)


def solution(mesh):
    placed = (
        P(("dp", "expert"), None),
        P(("dp", "expert"), None),
        P(("dp", "expert"), None),
        P(("dp", "expert"), None),
        P(("dp", "expert"), None),
        P(("dp", "expert"), None),
        P(("dp", "expert"), None),
        P(),
        P(),
        P("expert", None),
        P(),
        P(("dp", "expert"), None),
        P(("dp", "expert"), None),
        P("expert", "dp", None),
        P("expert", "dp", None),
        P("expert", "dp", None),
    )
    return jax.shard_map(
        local, mesh=mesh, in_specs=placed, out_specs=P(("dp", "expert"), None), check_vma=False
    )
```

profile of v0, /device:TPU:6, one launch (start us, length us, event | category | flops | bytes accessed | tf_op | source)
XLA Modules:
  0.0 507.4 jit_solution(4077008279144218235)
XLA Ops:
  11.1 9.1 %all-to-all-start.1 = ((s32[8,1,24]{2,1,0:T(1,128)}), s32[8,1,24]{2,1,0:T(1,128)S(1)}, u32[]{:S(2)}, u32[]{:S(2)}) async-start(s32[8,1,24]{2,1,0:T(1,128)} %compare_select_fusion.1), calls=%async_computation.1 | async-start | bytes 8192 | tf_op jit(solution)/shard_map/all_to_all | solution.py:151
  23.2 2.0 gather_fusion.6
  30.3 4.9 all-to-all-start.3
  36.7 2.2 all-to-all-done.3
  38.9 5.4 %all-to-all-start.2 = ((bf16[8,24,256]{2,1,0:T(8,128)(2,1)}), bf16[8,24,256]{2,1,0:T(8,128)(2,1)S(1)}, u32[]{:S(2)}, u32[]{:S(2)}) async-start(bf16[8,24,256]{2,1,0:T(8,128)(2,1)} %bitcast.9), calls=%async_computation.2 | async-start | bytes 196608 | tf_op jit(solution)/shard_map/all_to_all | solution.py:137
  44.3 3.7 all-to-all-done.2
  48.0 5.5 %all-to-all-start = ((bf16[8,24,1024]{2,1,0:T(8,128)(2,1)}), bf16[8,24,1024]{2,1,0:T(8,128)(2,1)S(1)}, u32[]{:S(2)}, u32[]{:S(2)}) async-start(bf16[8,24,1024]{2,1,0:T(8,128)(2,1)} %bitcast.3), calls=%async_computation | async-start | bytes 786432 | tf_op jit(solution)/shard_map/all_to_all | solution.py:144
  56.4 3.8 all-to-all-done
  60.3 5.6 %all-to-all-start.4 = ((bf16[8,24,2048]{2,1,0:T(8,128)(2,1)}), bf16[8,24,2048]{2,1,0:T(8,128)(2,1)S(1)}, u32[]{:S(2)}, u32[]{:S(2)}) async-start(bf16[8,24,2048]{2,1,0:T(8,128)(2,1)} %bitcast.19), calls=%async_computation.4 | async-start | bytes 1572864 | tf_op jit(solution)/shard_map/all_to_all | solution.py:123
  67.0 9.9 %all-to-all-done.4 = bf16[8,24,2048]{2,1,0:T(8,128)(2,1)S(1)} async-done(((bf16[8,24,2048]{2,1,0:T(8,128)(2,1)}), bf16[8,24,2048]{2,1,0:T(8,128)(2,1)S(1)}, u32[]{:S(2)}, u32[]{:S(2)}) %all-to-all-start.4) | async-done | bytes 786464 | tf_op jit(solution)/shard_map/all_to_all | solution.py:123
  82.3 79.4 %all-gather.5.cloned.1.call-done = bf16[2048,1024]{1,0:T(8,128)(2,1)} async-done(((bf16[32,1024]{1,0:T(8,128)(2,1)}), bf16[2048,1024]{1,0:T(8,128)(2,1)}) %all-gather.5.cloned.1.call-update) | async-done | bytes 4194320 | tf_op jit(solution)/shard_map/all_gather | solution.py:66
  161.7 3.0 multiply_reduce_fusion.1
  165.7 4.3 gather_fusion.8
  170.0 2.3 reshape.331
  172.3 9.2 %all-to-all-start.5 = ((bf16[64,20,1024]{2,1,0:T(8,128)(2,1)}), bf16[64,20,1024]{2,1,0:T(8,128)(2,1)}, u32[]{:S(2)}, u32[]{:S(2)}) async-start(bf16[64,20,1024]{2,1,0:T(8,128)(2,1)} %reshape.331), calls=%async_computation.5 | async-start | bytes 6291456 | tf_op jit(solution)/shard_map/all_to_all | solution.py:177
  183.3 131.7 %all-to-all-done.5 = bf16[64,20,1024]{2,1,0:T(8,128)(2,1)} async-done(((bf16[64,20,1024]{2,1,0:T(8,128)(2,1)}), bf16[64,20,1024]{2,1,0:T(8,128)(2,1)}, u32[]{:S(2)}, u32[]{:S(2)}) %all-to-all-start.5) | async-done | bytes 2621472 | tf_op jit(solution)/shard_map/all_to_all | solution.py:177
  315.0 3.6 reshape.332
  318.7 5.5 %fusion.4 = f32[1280,768]{1,0:T(8,128)} fusion(bf16[1280,1024]{1,0:T(8,128)(2,1)S(1)} %reshape.332, bf16[1,768,1024]{2,1,0:T(8,128)(2,1)} %all-gather.7.cloned.1.call-done), kind=kOutput, calls=%fused_computation.23 | convolution fusion | flops 2013265920 | bytes 8126464 | tf_op jit(solution)/shard_map/dot_general | solution.py:73
  324.2 10.0 %convolution_convert_fusion = bf16[1280,1024]{1,0:T(8,128)(2,1)} fusion(bf16[1,768,1024]{2,1,0:T(8,128)(2,1)} %all-gather.11.cloned.1.call-done, bf16[1280,1024]{1,0:T(8,128)(2,1)S(1)} %reshape.332, f32[1280,768]{1,0:T(8,128)} %fusion.4, bf16[1,768,1024]{2,1,0:T(8,128)(2,1)} %all-gather.9.cloned.1.call-done), kind=kOutput, calls=%fused_computation.19 | convolution fusion | flops 4033740800 | bytes 12320768 | tf_op jit(solution)/shard_map/dot_general | solution.py:76
  334.2 5.2 %reshape.333 = bf16[64,20,1024]{2,1,0:T(8,128)(2,1)} reshape(bf16[1280,1024]{1,0:T(8,128)(2,1)} %convolution_convert_fusion) | data formatting | bytes 5242880 | tf_op jit(solution)/shard_map/reshape | solution.py:186
  339.4 7.9 %all-to-all-start.6 = ((bf16[64,20,1024]{2,1,0:T(8,128)(2,1)}), bf16[64,20,1024]{2,1,0:T(8,128)(2,1)}, u32[]{:S(2)}, u32[]{:S(2)}) async-start(bf16[64,20,1024]{2,1,0:T(8,128)(2,1)} %reshape.333), calls=%async_computation.6 | async-start | bytes 6291456 | tf_op jit(solution)/shard_map/all_to_all | solution.py:187
  347.5 134.1 %all-to-all-done.6 = bf16[64,20,1024]{2,1,0:T(8,128)(2,1)} async-done(((bf16[64,20,1024]{2,1,0:T(8,128)(2,1)}), bf16[64,20,1024]{2,1,0:T(8,128)(2,1)}, u32[]{:S(2)}, u32[]{:S(2)}) %all-to-all-start.6) | async-done | bytes 2621472 | tf_op jit(solution)/shard_map/all_to_all | solution.py:187
  481.7 3.6 reshape.334
  497.1 2.8 add_convert_fusion.1
  (117 shorter events, 37.1 us)
Async XLA Ops:
  7.4 15.8 %copy-start = (bf16[128,2048]{1,0:T(8,128)(2,1)S(1)}, bf16[128,2048]{1,0:T(8,128)(2,1)}, u32[]{:S(2)}) copy-start(bf16[128,2048]{1,0:T(8,128)(2,1)} %param.16) | copy-start | bytes 1572868
  7.4 154.3 %all-gather.5.cloned.1.call-start = ((), (), s32[]{:S(2)}) async-start(), calls=%async_computation.7 | async-start | bytes 4259840 | tf_op jit(solution)/shard_map/all_gather | solution.py:66
  11.1 19.2 %all-to-all-start.1 = ((s32[8,1,24]{2,1,0:T(1,128)}), s32[8,1,24]{2,1,0:T(1,128)S(1)}, u32[]{:S(2)}, u32[]{:S(2)}) async-start(s32[8,1,24]{2,1,0:T(1,128)} %compare_select_fusion.1), calls=%async_computation.1 | async-start | bytes 8192 | tf_op jit(solution)/shard_map/all_to_all | solution.py:151
  23.2 2.0 copy-start.2
  23.2 3.7 copy-start.3
  25.2 3.3 copy-start.1
  30.2 35.6 %copy-start.14 = (f32[128]{0:T(128)S(1)}, f32[128]{0:T(128)}, u32[]{:S(2)}) copy-start(f32[128]{0:T(128)} %param.24) | copy-start | bytes 1540
  30.3 8.7 %all-to-all-start.3 = ((bf16[8,24,256]{2,1,0:T(8,128)(2,1)}), bf16[8,24,256]{2,1,0:T(8,128)(2,1)S(1)}, u32[]{:S(2)}, u32[]{:S(2)}) async-start(bf16[8,24,256]{2,1,0:T(8,128)(2,1)} %bitcast.14), calls=%async_computation.3 | async-start | bytes 196608 | tf_op jit(solution)/shard_map/all_to_all | solution.py:130
  38.9 9.1 %all-to-all-start.2 = ((bf16[8,24,256]{2,1,0:T(8,128)(2,1)}), bf16[8,24,256]{2,1,0:T(8,128)(2,1)S(1)}, u32[]{:S(2)}, u32[]{:S(2)}) async-start(bf16[8,24,256]{2,1,0:T(8,128)(2,1)} %bitcast.9), calls=%async_computation.2 | async-start | bytes 196608 | tf_op jit(solution)/shard_map/all_to_all | solution.py:137
  48.0 12.3 %all-to-all-start = ((bf16[8,24,1024]{2,1,0:T(8,128)(2,1)}), bf16[8,24,1024]{2,1,0:T(8,128)(2,1)S(1)}, u32[]{:S(2)}, u32[]{:S(2)}) async-start(bf16[8,24,1024]{2,1,0:T(8,128)(2,1)} %bitcast.3), calls=%async_computation | async-start | bytes 786432 | tf_op jit(solution)/shard_map/all_to_all | solution.py:144
  60.3 16.6 %all-to-all-start.4 = ((bf16[8,24,2048]{2,1,0:T(8,128)(2,1)}), bf16[8,24,2048]{2,1,0:T(8,128)(2,1)S(1)}, u32[]{:S(2)}, u32[]{:S(2)}) async-start(bf16[8,24,2048]{2,1,0:T(8,128)(2,1)} %bitcast.19), calls=%async_computation.4 | async-start | bytes 1572864 | tf_op jit(solution)/shard_map/all_to_all | solution.py:123
  66.1 13.8 %copy-start.7 = (bf16[128,2,64]{2,0,1:T(8,128)(2,1)}, bf16[128,2,64]{2,0,1:T(8,128)(2,1)S(1)}, u32[]{:S(2)}) copy-start(bf16[128,2,64]{2,0,1:T(8,128)(2,1)S(1)} %get-tuple-element.12) | copy-start | bytes 98308
  66.1 13.8 %copy-start.8 = (bf16[128,2,64]{2,0,1:T(8,128)(2,1)}, bf16[128,2,64]{2,0,1:T(8,128)(2,1)S(1)}, u32[]{:S(2)}) copy-start(bf16[128,2,64]{2,0,1:T(8,128)(2,1)S(1)} %get-tuple-element.13) | copy-start | bytes 98308
  79.8 2.0 copy-start.9
  161.7 3.8 copy-start.13
  161.7 3.9 copy-start.11
  172.3 142.7 %all-to-all-start.5 = ((bf16[64,20,1024]{2,1,0:T(8,128)(2,1)}), bf16[64,20,1024]{2,1,0:T(8,128)(2,1)}, u32[]{:S(2)}, u32[]{:S(2)}) async-start(bf16[64,20,1024]{2,1,0:T(8,128)(2,1)} %reshape.331), calls=%async_computation.5 | async-start | bytes 6291456 | tf_op jit(solution)/shard_map/all_to_all | solution.py:177
  181.5 137.1 %all-gather.7.cloned.1.call-start = ((), (), s32[]{:S(2)}) async-start(), calls=%async_computation.8 | async-start | bytes 1769472 | tf_op jit(solution)/shard_map/all_gather | solution.py:180
  182.1 142.1 %all-gather.11.cloned.1.call-start = ((), (), s32[]{:S(2)}) async-start(), calls=%async_computation.10 | async-start | bytes 1769472 | tf_op jit(solution)/shard_map/all_gather | solution.py:182
  182.7 141.5 %all-gather.9.cloned.1.call-start = ((), (), s32[]{:S(2)}) async-start(), calls=%async_computation.9 | async-start | bytes 1769472 | tf_op jit(solution)/shard_map/all_gather | solution.py:181
  339.4 8.0 %copy-start.12 = (f32[128,8]{0,1:T(8,128)S(1)}, f32[128,8]{0,1:T(8,128)}, u32[]{:S(2)}) copy-start(f32[128,8]{0,1:T(8,128)} %param.28) | copy-start | bytes 12292
  339.4 8.0 %copy-start.6 = (s32[128,64]{0,1:T(8,128)S(1)}, s32[128,64]{0,1:T(8,128)}, u32[]{:S(2)}) copy-start(s32[128,64]{0,1:T(8,128)} %copy-done.5) | copy-start | bytes 98308
  339.4 8.0 %copy-start.10 = (s32[128,8]{0,1:T(8,128)S(1)}, s32[128,8]{0,1:T(8,128)}, u32[]{:S(2)}) copy-start(s32[128,8]{0,1:T(8,128)} %param.27) | copy-start | bytes 12292
  339.4 142.3 %all-to-all-start.6 = ((bf16[64,20,1024]{2,1,0:T(8,128)(2,1)}), bf16[64,20,1024]{2,1,0:T(8,128)(2,1)}, u32[]{:S(2)}, u32[]{:S(2)}) async-start(bf16[64,20,1024]{2,1,0:T(8,128)(2,1)} %reshape.333), calls=%async_computation.6 | async-start | bytes 6291456 | tf_op jit(solution)/shard_map/all_to_all | solution.py:187
  (3 other events, 2.2 us)
Sparse Core Ops, SparseCore 0:
  11.1 150.5 all-gather.4
Sparse Core Ops, SparseCore 1:
  184.1 31.0 all-gather.6
  217.2 32.1 all-gather.10
  251.3 32.0 all-gather.8
where the time goes:
time: 509 us; the launch traced here: 507 us
  waiting for transfers between devices  367 us (72%)
  starting transfers between devices  47.7 us (9%)
  local copies, waits for them, and re-layouts  45.3 us (9%)
  matrix products  21.2 us (4%)
  between operations  15.5 us (3%)
  other arithmetic  10.6 us (2%)
    all_to_all x1, waiting for transfers between devices, local(): lax.all_to_all(out_slots, 'expert', split_axis=0, concat_axis=0, tiled=True)  134 us
    all_to_all x1, waiting for transfers between devices, local(): lax.all_to_all(outgoing, 'expert', split_axis=0, concat_axis=0, tiled=True)  132 us
    all_gather x1, waiting for transfers between devices, project_heads(): lax.all_gather(output_weight, 'expert', axis=0, tiled=True)  79.4 us
    gather x8, local copies, waits for them, and re-layouts, local(): flat_back[copy_index[:, route_slot]].astype(jnp.float32)  11.8 us
  transfers between devices with their start and end apart: 11, of which 7 were waited for; matrix products, arithmetic and copies ran while one was open for 6% of the time, Pallas kernels for 0%

commit v1 on v0

--- a/solution.py
+++ b/solution.py
@@ -60,10 +60,54 @@
     return mixed.astype(jnp.bfloat16).reshape(row_total, head_count * head_width)
 
 
+def ring_pairs(rows, cols, step_row, step_col):
+    return [
+        (r * cols + c, ((r + step_row) % rows) * cols + (c + step_col) % cols)
+        for r in range(rows)
+        for c in range(cols)
+    ]
+
+
+def ring_gather(block, rows, cols):
+    up = lax.ppermute(block, "expert", ring_pairs(rows, cols, 1, 0))
+    down = lax.ppermute(block, "expert", ring_pairs(rows, cols, -1, 0))
+    up_two = lax.ppermute(up, "expert", ring_pairs(rows, cols, 1, 0))
+    by_row = jnp.stack([block, down, up_two, up])
+    relative = {0: by_row}
+    right = by_row
+    left = by_row
+    half = cols // 2
+    for step in range(1, half + 1):
+        right = lax.ppermute(right, "expert", ring_pairs(rows, cols, 0, 1))
+        relative[-step % cols] = right
+        if step < half:
+            left = lax.ppermute(left, "expert", ring_pairs(rows, cols, 0, -1))
+            relative[step] = left
+    return jnp.stack([relative[k] for k in range(cols)], axis=1)
+
+
 def project_heads(attended, output_weight):
+    expert_total = lax.axis_size("expert")
+    cols = 16
+    rows = expert_total // cols
+    if rows != 4 or expert_total % cols:
+        return jnp.dot(
+            attended,
+            lax.all_gather(output_weight, "expert", axis=0, tiled=True),
+            preferred_element_type=jnp.float32,
+        )
+    own = lax.axis_index("expert")
+    own_row = own // cols
+    own_col = own % cols
+    gathered = ring_gather(output_weight, rows, cols)
+    block = output_weight.shape[0]
+    row_order = (own_row + jnp.arange(rows, dtype=jnp.int32)) % rows
+    col_order = (own_col + jnp.arange(cols, dtype=jnp.int32)) % cols
+    split = attended.reshape(attended.shape[0], rows, cols, block)
+    split = jnp.take(jnp.take(split, row_order, axis=1), col_order, axis=2)
     return jnp.dot(
-        attended,
-        lax.all_gather(output_weight, "expert", axis=0, tiled=True),
+        split.reshape(attended.shape[0], -1),
+        gathered.reshape(rows * cols * block, -1),
         preferred_element_type=jnp.float32,
     )
 
@@ -119,43 +163,30 @@
     total_slots = owner_total * capacity
     flat_slots = jnp.arange(total_slots, dtype=jnp.int32)
     pack_ids = jnp.arange(row_total, dtype=jnp.int32)
-    got_query, got_key, got_value, got_residual, got_slot = (
-        lax.all_to_all(
-            query_rows[source_rows].reshape(owner_total, capacity, -1),
-            "dp",
-            split_axis=0,
-            concat_axis=0,
-            tiled=True,
-        ),
-        lax.all_to_all(
-            key_rows[source_rows].reshape(owner_total, capacity, -1),
-            "dp",
-            split_axis=0,
-            concat_axis=0,
-            tiled=True,
-        ),
-        lax.all_to_all(
-            value_rows[source_rows].reshape(owner_total, capacity, -1),
-            "dp",
-            split_axis=0,
-            concat_axis=0,
-            tiled=True,
-        ),
-        lax.all_to_all(
-            residual[source_rows].reshape(owner_total, capacity, -1),
-            "dp",
-            split_axis=0,
-            concat_axis=0,
-            tiled=True,
-        ),
-        lax.all_to_all(pack_slot, "dp", split_axis=0, concat_axis=0, tiled=True),
-    )
-    placed = got_slot.reshape(-1)[None, :] == pack_ids[:, None]
+    whole_rows = jnp.concatenate([query_rows, key_rows, value_rows, residual], axis=1)
+    widths = [query_rows.shape[1], key_rows.shape[1], value_rows.shape[1], residual.shape[1]]
+    data_width = sum(widths)
+    slot_column = jnp.broadcast_to(
+        pack_slot.reshape(-1, 1).astype(jnp.bfloat16), (total_slots, 128)
+    )
+    outgoing_pack = jnp.concatenate([whole_rows[source_rows], slot_column], axis=1)
+    got = lax.all_to_all(
+        outgoing_pack.reshape(owner_total, capacity, -1),
+        "dp",
+        split_axis=0,
+        concat_axis=0,
+        tiled=True,
+    ).reshape(total_slots, -1)
+    got_slot = got[:, data_width].astype(jnp.int32)
+    placed = got_slot[None, :] == pack_ids[:, None]
     slot_of = jnp.sum(jnp.where(placed, flat_slots[None, :], 0), axis=1)
-    pack_query = got_query.reshape(total_slots, -1)[slot_of]
-    pack_key = got_key.reshape(total_slots, -1)[slot_of]
-    pack_value = got_value.reshape(total_slots, -1)[slot_of]
-    pack_residual = got_residual.reshape(total_slots, -1)[slot_of]
+    packed = got[slot_of]
+    bounds = [0]
+    for width in widths:
+        bounds.append(bounds[-1] + width)
+    pack_query, pack_key, pack_value, pack_residual = (
+        packed[:, bounds[i] : bounds[i + 1]] for i in range(4)
+    )
     identity = slot_of // capacity
     position = slot_of % capacity
     attended = attend(pack_query, pack_key, pack_value, identity, position, query_gain, key_gain)

time: 509 us -> 480 us (0.943)
  waiting for transfers between devices: 367 us -> 290 us
  starting transfers between devices: 47.7 us -> 88.3 us
  local copies, waits for them, and re-layouts: 45.3 us -> 52.4 us
    all_gather x1 -> x0, waiting for transfers between devices: 79.4 us -> none  [project_heads(): lax.all_gather(output_weight, 'expert', axis=0, tiled=True)]
    ppermute x0 -> x18, starting transfers between devices: none -> 64 us  [the longest x7 39.7 us: ring_gather(): left = lax.ppermute(left, 'expert', ring_pairs(rows, cols, 0, -1))]
    ppermute x0 -> x18, waiting for transfers between devices: none -> 22.7 us  [the longest x8 11.5 us: ring_gather(): right = lax.ppermute(right, 'expert', ring_pairs(rows, cols, 0, 1))]
    all_to_all x5 -> x1, starting transfers between devices: 30.4 us -> 9.33 us  [local(): lax.all_to_all(outgoing_pack.reshape(owner_total, capacity, -1), 'dp', sp...]
    all_to_all x5 -> x1, waiting for transfers between devices: 19.7 us -> 0.01 us  [local(): lax.all_to_all(outgoing_pack.reshape(owner_total, capacity, -1), 'dp', sp...]
    unnamed x33 -> x45, local copies, waits for them, and re-layouts: 1.61 us -> 17 us
    gather x8 -> x4, local copies, waits for them, and re-layouts: 10.5 us -> 3.93 us  [the longest x1 1.42 us: local(): whole_rows[source_rows]]
  transfers between devices with their start and end apart: 11 -> 24, of which waited for: 7 -> 11; matrix products, arithmetic and copies ran while one was open for 6% -> 7% of each run, Pallas kernels for 0% -> 0%
where the time goes in v1:
time: 480 us; the launch traced here: 478 us
  waiting for transfers between devices  290 us (60%)
  starting transfers between devices  88.3 us (18%)
  local copies, waits for them, and re-layouts  52.4 us (11%)
  matrix products  21.3 us (4%)
  between operations  13.9 us (3%)
  other arithmetic  11.4 us (2%)
    all_to_all x1, waiting for transfers between devices, local(): lax.all_to_all(out_slots, 'expert', split_axis=0, concat_axis=0, tiled=True)  134 us
    all_to_all x1, waiting for transfers between devices, local(): lax.all_to_all(outgoing, 'expert', split_axis=0, concat_axis=0, tiled=True)  132 us
    ppermute x7, starting transfers between devices, ring_gather(): left = lax.ppermute(left, 'expert', ring_pairs(rows, cols, 0, -1))  39.7 us
    unnamed x45, local copies, waits for them, and re-layouts  17 us
    ppermute x8, starting transfers between devices, ring_gather(): right = lax.ppermute(right, 'expert', ring_pairs(rows, cols, 0, 1))  15.3 us
    gather x8, local copies, waits for them, and re-layouts, local(): flat_back[copy_index[:, route_slot]].astype(jnp.float32)  11.8 us
    ppermute x8, waiting for transfers between devices, ring_gather(): right = lax.ppermute(right, 'expert', ring_pairs(rows, cols, 0, 1))  11.5 us
    dot_general x1, matrix products, hidden_product(): return jnp.dot(active, down_part, preferred_element_type=jnp.float32)  10 us
  transfers between devices with their start and end apart: 24, of which 11 were waited for; matrix products, arithmetic and copies ran while one was open for 7% of the time, Pallas kernels for 0%

profile of v1, /device:TPU:6, one launch (start us, length us, event | category | flops | bytes accessed | tf_op | source)
XLA Modules:
  0.0 477.8 jit_solution(16440372000938107225)
XLA Ops:
  6.5 3.5 collective-permute-start.1
  10.0 3.6 collective-permute-start
  20.2 9.3 %all-to-all-start = ((bf16[8,24,3712]{2,1,0:T(8,128)(2,1)}), bf16[8,24,3712]{2,1,0:T(8,128)(2,1)S(1)}, u32[]{:S(2)}, u32[]{:S(2)}) async-start(bf16[8,24,3712]{2,1,0:T(8,128)(2,1)} %bitcast.5), calls=%async_computation | async-start | bytes 2850816 | tf_op jit(solution)/shard_map/all_to_all | solution.py:173
  32.3 5.4 %collective-permute-done.2 = bf16[32,1024]{1,0:T(8,128)(2,1)S(1)} collective-permute-done((bf16[32,1024]{1,0:T(8,128)(2,1)S(1)}, bf16[32,1024]{1,0:T(8,128)(2,1)S(1)}, u32[]{:S(2)}, u32[]{:S(2)}) %collective-permute-start.2) | collective-permute-done | bytes 65568 | tf_op jit(solution)/shard_map/ppermute | solution.py:74
  37.7 6.8 %collective-permute-start.3 = (bf16[4,32,1024]{2,1,0:T(8,128)(2,1)S(1)}, bf16[4,32,1024]{2,1,0:T(8,128)(2,1)S(1)}, u32[]{:S(2)}, u32[]{:S(2)}) collective-permute-start(bf16[4,32,1024]{2,1,0:T(8,128)(2,1)S(1)} %pad_maximum_fusion.2), channel_id=1, source_target_pairs={{0,15},{1,0},{2,1},{3,2},{4,3},{5,4},{6,5},{7,6},{8,7},{9,8},{10,9... | collective-permute-start | bytes 786440 | tf_op jit(solution)/shard_map/ppermute | solution.py:84
  46.8 2.8 collective-permute-done.3
  49.5 5.6 %collective-permute-start.4 = (bf16[4,32,1024]{2,1,0:T(8,128)(2,1)S(1)}, bf16[4,32,1024]{2,1,0:T(8,128)(2,1)S(1)}, u32[]{:S(2)}, u32[]{:S(2)}) collective-permute-start(bf16[4,32,1024]{2,1,0:T(8,128)(2,1)S(1)} %collective-permute-done.3), channel_id=1, source_target_pairs={{0,15},{1,0},{2,1},{3,2},{4,3},{5,4},{6,5},{7,6},{8,7},{9,8},{10,9... | collective-permute-start | bytes 786440 | tf_op jit(solution)/shard_map/ppermute | solution.py:84
  59.2 5.6 %collective-permute-start.5 = (bf16[4,32,1024]{2,1,0:T(8,128)(2,1)S(1)}, bf16[4,32,1024]{2,1,0:T(8,128)(2,1)S(1)}, u32[]{:S(2)}, u32[]{:S(2)}) collective-permute-start(bf16[4,32,1024]{2,1,0:T(8,128)(2,1)S(1)} %collective-permute-done.4), channel_id=1, source_target_pairs={{0,15},{1,0},{2,1},{3,2},{4,3},{5,4},{6,5},{7,6},{8,7},{9,8},{10,9... | collective-permute-start | bytes 786440 | tf_op jit(solution)/shard_map/ppermute | solution.py:84
  68.7 5.6 %collective-permute-start.6 = (bf16[4,32,1024]{2,1,0:T(8,128)(2,1)S(1)}, bf16[4,32,1024]{2,1,0:T(8,128)(2,1)}, u32[]{:S(2)}, u32[]{:S(2)}) collective-permute-start(bf16[4,32,1024]{2,1,0:T(8,128)(2,1)S(1)} %collective-permute-done.5), channel_id=1, source_target_pairs={{0,15},{1,0},{2,1},{3,2},{4,3},{5,4},{6,5},{7,6},{8,7},{9,8},{10,9... | collective-permute-start | bytes 786440 | tf_op jit(solution)/shard_map/ppermute | solution.py:84
  78.2 5.7 %collective-permute-start.7 = (bf16[4,32,1024]{2,1,0:T(8,128)(2,1)}, bf16[4,32,1024]{2,1,0:T(8,128)(2,1)}, u32[]{:S(2)}, u32[]{:S(2)}) collective-permute-start(bf16[4,32,1024]{2,1,0:T(8,128)(2,1)} %collective-permute-done.6), channel_id=1, source_target_pairs={{0,15},{1,0},{2,1},{3,2},{4,3},{5,4},{6,5},{7,6},{8,7},{9,8},{10,9... | collective-permute-start | bytes 786440 | tf_op jit(solution)/shard_map/ppermute | solution.py:84
  96.5 5.1 %collective-permute-start.8 = (bf16[4,32,1024]{2,1,0:T(8,128)(2,1)}, bf16[4,32,1024]{2,1,0:T(8,128)(2,1)}, u32[]{:S(2)}, u32[]{:S(2)}) collective-permute-start(bf16[4,32,1024]{2,1,0:T(8,128)(2,1)} %collective-permute-done.7), channel_id=1, source_target_pairs={{0,15},{1,0},{2,1},{3,2},{4,3},{5,4},{6,5},{7,6},{8,7},{9,8},{10,9... | collective-permute-start | bytes 786440 | tf_op jit(solution)/shard_map/ppermute | solution.py:84
  107.7 5.3 %collective-permute-start.9 = (bf16[4,32,1024]{2,1,0:T(8,128)(2,1)}, bf16[4,32,1024]{2,1,0:T(8,128)(2,1)S(1)}, u32[]{:S(2)}, u32[]{:S(2)}) collective-permute-start(bf16[4,32,1024]{2,1,0:T(8,128)(2,1)} %collective-permute-done.8), channel_id=1, source_target_pairs={{0,15},{1,0},{2,1},{3,2},{4,3},{5,4},{6,5},{7,6},{8,7},{9,8},{10,9... | collective-permute-start | bytes 786440 | tf_op jit(solution)/shard_map/ppermute | solution.py:84
  114.7 2.7 collective-permute-done.16
  121.8 5.1 %collective-permute-done.17 = bf16[4,32,1024]{2,1,0:T(8,128)(2,1)S(1)} collective-permute-done((bf16[4,32,1024]{2,1,0:T(8,128)(2,1)S(1)}, bf16[4,32,1024]{2,1,0:T(8,128)(2,1)S(1)}, u32[]{:S(2)}, u32[]{:S(2)}) %collective-permute-start.17) | collective-permute-done | bytes 262176 | tf_op jit(solution)/shard_map/ppermute | solution.py:81
  135.6 3.1 multiply_reduce_fusion.1
  139.7 4.3 gather_fusion.4
  146.4 6.9 %all-to-all-start.1 = ((bf16[64,20,1024]{2,1,0:T(8,128)(2,1)}), bf16[64,20,1024]{2,1,0:T(8,128)(2,1)S(1)}, u32[]{:S(2)}, u32[]{:S(2)}) async-start(bf16[64,20,1024]{2,1,0:T(8,128)(2,1)} %reshape.393), calls=%async_computation.1 | async-start | bytes 6291456 | tf_op jit(solution)/shard_map/all_to_all | solution.py:208
  155.5 131.6 %all-to-all-done.1 = bf16[64,20,1024]{2,1,0:T(8,128)(2,1)S(1)} async-done(((bf16[64,20,1024]{2,1,0:T(8,128)(2,1)}), bf16[64,20,1024]{2,1,0:T(8,128)(2,1)S(1)}, u32[]{:S(2)}, u32[]{:S(2)}) %all-to-all-start.1) | async-done | bytes 2621472 | tf_op jit(solution)/shard_map/all_to_all | solution.py:208
  289.3 6.4 %fusion.4 = f32[1280,768]{1,0:T(8,128)} fusion(bf16[1280,1024]{1,0:T(8,128)(2,1)} %reshape.394, bf16[1,768,1024]{2,1,0:T(8,128)(2,1)} %all-gather.4.cloned.1.call-done), kind=kOutput, calls=%fused_computation.19 | convolution fusion | flops 2013265920 | bytes 8126464 | tf_op jit(solution)/shard_map/dot_general | solution.py:117
  295.7 10.0 %convolution_convert_fusion = bf16[1280,1024]{1,0:T(8,128)(2,1)} fusion(bf16[1,768,1024]{2,1,0:T(8,128)(2,1)} %all-gather.8.cloned.1.call-done, bf16[1280,1024]{1,0:T(8,128)(2,1)S(1)} %copy-done.2, f32[1280,768]{1,0:T(8,128)} %fusion.4, bf16[1,768,1024]{2,1,0:T(8,128)(2,1)} %all-gather.6.cloned.1.call-done), kind=kOutput, calls=%fused_computation.15 | convolution fusion | flops 4033740800 | bytes 12320768 | tf_op jit(solution)/shard_map/dot_general | solution.py:120
  305.7 5.2 %reshape.395 = bf16[64,20,1024]{2,1,0:T(8,128)(2,1)} reshape(bf16[1280,1024]{1,0:T(8,128)(2,1)} %convolution_convert_fusion) | data formatting | bytes 5242880 | tf_op jit(solution)/shard_map/reshape | solution.py:217
  310.9 7.9 %all-to-all-start.2 = ((bf16[64,20,1024]{2,1,0:T(8,128)(2,1)}), bf16[64,20,1024]{2,1,0:T(8,128)(2,1)}, u32[]{:S(2)}, u32[]{:S(2)}) async-start(bf16[64,20,1024]{2,1,0:T(8,128)(2,1)} %reshape.395), calls=%async_computation.2 | async-start | bytes 6291456 | tf_op jit(solution)/shard_map/all_to_all | solution.py:218
  319.0 134.1 %all-to-all-done.2 = bf16[64,20,1024]{2,1,0:T(8,128)(2,1)} async-done(((bf16[64,20,1024]{2,1,0:T(8,128)(2,1)}), bf16[64,20,1024]{2,1,0:T(8,128)(2,1)}, u32[]{:S(2)}, u32[]{:S(2)}) %all-to-all-start.2) | async-done | bytes 2621472 | tf_op jit(solution)/shard_map/all_to_all | solution.py:218
  453.2 3.6 reshape.396
  (161 shorter events, 78.5 us)
Async XLA Ops:
  6.5 23.8 %collective-permute-start.1 = (bf16[32,1024]{1,0:T(8,128)(2,1)}, bf16[32,1024]{1,0:T(8,128)(2,1)S(1)}, u32[]{:S(2)}, u32[]{:S(2)}) collective-permute-start(bf16[32,1024]{1,0:T(8,128)(2,1)} %param.25), channel_id=1, source_target_pairs={{0,16},{1,17},{2,18},{3,19},{4,20},{5,21},{6,22},{7,23},{8,24},{9,... | collective-permute-start | bytes 196616 | tf_op jit(solution)/shard_map/ppermute | solution.py:72
  10.0 22.2 %collective-permute-start = (bf16[32,1024]{1,0:T(8,128)(2,1)}, bf16[32,1024]{1,0:T(8,128)(2,1)S(1)}, u32[]{:S(2)}, u32[]{:S(2)}) collective-permute-start(bf16[32,1024]{1,0:T(8,128)(2,1)} %param.25), channel_id=1, source_target_pairs={{0,48},{1,49},{2,50},{3,51},{4,52},{5,53},{6,54},{7,55},{8,56},{9,... | collective-permute-start | bytes 196616 | tf_op jit(solution)/shard_map/ppermute | solution.py:73
  20.2 67.3 %all-to-all-start = ((bf16[8,24,3712]{2,1,0:T(8,128)(2,1)}), bf16[8,24,3712]{2,1,0:T(8,128)(2,1)S(1)}, u32[]{:S(2)}, u32[]{:S(2)}) async-start(bf16[8,24,3712]{2,1,0:T(8,128)(2,1)} %bitcast.5), calls=%async_computation | async-start | bytes 2850816 | tf_op jit(solution)/shard_map/all_to_all | solution.py:173
  30.3 7.4 %collective-permute-start.2 = (bf16[32,1024]{1,0:T(8,128)(2,1)S(1)}, bf16[32,1024]{1,0:T(8,128)(2,1)S(1)}, u32[]{:S(2)}, u32[]{:S(2)}) collective-permute-start(bf16[32,1024]{1,0:T(8,128)(2,1)S(1)} %collective-permute-done.1), channel_id=1, source_target_pairs={{0,16},{1,17},{2,18},{3,19},{4,20},{5,21},{6,22},{7,23},{8,24},{9,... | collective-permute-start | bytes 196616 | tf_op jit(solution)/shard_map/ppermute | solution.py:74
  37.7 11.8 %collective-permute-start.3 = (bf16[4,32,1024]{2,1,0:T(8,128)(2,1)S(1)}, bf16[4,32,1024]{2,1,0:T(8,128)(2,1)S(1)}, u32[]{:S(2)}, u32[]{:S(2)}) collective-permute-start(bf16[4,32,1024]{2,1,0:T(8,128)(2,1)S(1)} %pad_maximum_fusion.2), channel_id=1, source_target_pairs={{0,15},{1,0},{2,1},{3,2},{4,3},{5,4},{6,5},{7,6},{8,7},{9,8},{10,9... | collective-permute-start | bytes 786440 | tf_op jit(solution)/shard_map/ppermute | solution.py:84
  44.6 10.6 %collective-permute-start.10 = (bf16[4,32,1024]{2,1,0:T(8,128)(2,1)S(1)}, bf16[4,32,1024]{2,1,0:T(8,128)(2,1)S(1)}, u32[]{:S(2)}, u32[]{:S(2)}) collective-permute-start(bf16[4,32,1024]{2,1,0:T(8,128)(2,1)S(1)} %pad_maximum_fusion.2), channel_id=1, source_target_pairs={{0,1},{1,2},{2,3},{3,4},{4,5},{5,6},{6,7},{7,8},{8,9},{9,10},{10,1... | collective-permute-start | bytes 786440 | tf_op jit(solution)/shard_map/ppermute | solution.py:81
  49.5 9.7 %collective-permute-start.4 = (bf16[4,32,1024]{2,1,0:T(8,128)(2,1)S(1)}, bf16[4,32,1024]{2,1,0:T(8,128)(2,1)S(1)}, u32[]{:S(2)}, u32[]{:S(2)}) collective-permute-start(bf16[4,32,1024]{2,1,0:T(8,128)(2,1)S(1)} %collective-permute-done.3), channel_id=1, source_target_pairs={{0,15},{1,0},{2,1},{3,2},{4,3},{5,4},{6,5},{7,6},{8,7},{9,8},{10,9... | collective-permute-start | bytes 786440 | tf_op jit(solution)/shard_map/ppermute | solution.py:84
  55.1 9.7 %collective-permute-start.11 = (bf16[4,32,1024]{2,1,0:T(8,128)(2,1)S(1)}, bf16[4,32,1024]{2,1,0:T(8,128)(2,1)S(1)}, u32[]{:S(2)}, u32[]{:S(2)}) collective-permute-start(bf16[4,32,1024]{2,1,0:T(8,128)(2,1)S(1)} %collective-permute-done.10), channel_id=1, source_target_pairs={{0,1},{1,2},{2,3},{3,4},{4,5},{5,6},{6,7},{7,8},{8,9},{9,10},{10,1... | collective-permute-start | bytes 786440 | tf_op jit(solution)/shard_map/ppermute | solution.py:81
  59.2 9.5 %collective-permute-start.5 = (bf16[4,32,1024]{2,1,0:T(8,128)(2,1)S(1)}, bf16[4,32,1024]{2,1,0:T(8,128)(2,1)S(1)}, u32[]{:S(2)}, u32[]{:S(2)}) collective-permute-start(bf16[4,32,1024]{2,1,0:T(8,128)(2,1)S(1)} %collective-permute-done.4), channel_id=1, source_target_pairs={{0,15},{1,0},{2,1},{3,2},{4,3},{5,4},{6,5},{7,6},{8,7},{9,8},{10,9... | collective-permute-start | bytes 786440 | tf_op jit(solution)/shard_map/ppermute | solution.py:84
  64.9 9.5 %collective-permute-start.12 = (bf16[4,32,1024]{2,1,0:T(8,128)(2,1)S(1)}, bf16[4,32,1024]{2,1,0:T(8,128)(2,1)S(1)}, u32[]{:S(2)}, u32[]{:S(2)}) collective-permute-start(bf16[4,32,1024]{2,1,0:T(8,128)(2,1)S(1)} %collective-permute-done.11), channel_id=1, source_target_pairs={{0,1},{1,2},{2,3},{3,4},{4,5},{5,6},{6,7},{7,8},{8,9},{9,10},{10,1... | collective-permute-start | bytes 786440 | tf_op jit(solution)/shard_map/ppermute | solution.py:81
  68.7 9.5 %collective-permute-start.6 = (bf16[4,32,1024]{2,1,0:T(8,128)(2,1)S(1)}, bf16[4,32,1024]{2,1,0:T(8,128)(2,1)}, u32[]{:S(2)}, u32[]{:S(2)}) collective-permute-start(bf16[4,32,1024]{2,1,0:T(8,128)(2,1)S(1)} %collective-permute-done.5), channel_id=1, source_target_pairs={{0,15},{1,0},{2,1},{3,2},{4,3},{5,4},{6,5},{7,6},{8,7},{9,8},{10,9... | collective-permute-start | bytes 786440 | tf_op jit(solution)/shard_map/ppermute | solution.py:84
  74.3 9.6 %collective-permute-start.13 = (bf16[4,32,1024]{2,1,0:T(8,128)(2,1)S(1)}, bf16[4,32,1024]{2,1,0:T(8,128)(2,1)}, u32[]{:S(2)}, u32[]{:S(2)}) collective-permute-start(bf16[4,32,1024]{2,1,0:T(8,128)(2,1)S(1)} %collective-permute-done.12), channel_id=1, source_target_pairs={{0,1},{1,2},{2,3},{3,4},{4,5},{5,6},{6,7},{7,8},{8,9},{9,10},{10,1... | collective-permute-start | bytes 786440 | tf_op jit(solution)/shard_map/ppermute | solution.py:81
  78.2 18.4 %collective-permute-start.7 = (bf16[4,32,1024]{2,1,0:T(8,128)(2,1)}, bf16[4,32,1024]{2,1,0:T(8,128)(2,1)}, u32[]{:S(2)}, u32[]{:S(2)}) collective-permute-start(bf16[4,32,1024]{2,1,0:T(8,128)(2,1)} %collective-permute-done.6), channel_id=1, source_target_pairs={{0,15},{1,0},{2,1},{3,2},{4,3},{5,4},{6,5},{7,6},{8,7},{9,8},{10,9... | collective-permute-start | bytes 786440 | tf_op jit(solution)/shard_map/ppermute | solution.py:84
  83.9 10.0 %collective-permute-start.14 = (bf16[4,32,1024]{2,1,0:T(8,128)(2,1)}, bf16[4,32,1024]{2,1,0:T(8,128)(2,1)}, u32[]{:S(2)}, u32[]{:S(2)}) collective-permute-start(bf16[4,32,1024]{2,1,0:T(8,128)(2,1)} %collective-permute-done.13), channel_id=1, source_target_pairs={{0,1},{1,2},{2,3},{3,4},{4,5},{5,6},{6,7},{7,8},{8,9},{9,10},{10,1... | collective-permute-start | bytes 786440 | tf_op jit(solution)/shard_map/ppermute | solution.py:81
  93.9 11.1 %collective-permute-start.15 = (bf16[4,32,1024]{2,1,0:T(8,128)(2,1)}, bf16[4,32,1024]{2,1,0:T(8,128)(2,1)}, u32[]{:S(2)}, u32[]{:S(2)}) collective-permute-start(bf16[4,32,1024]{2,1,0:T(8,128)(2,1)} %collective-permute-done.14), channel_id=1, source_target_pairs={{0,1},{1,2},{2,3},{3,4},{4,5},{5,6},{6,7},{7,8},{8,9},{9,10},{10,1... | collective-permute-start | bytes 786440 | tf_op jit(solution)/shard_map/ppermute | solution.py:81
  96.5 11.2 %collective-permute-start.8 = (bf16[4,32,1024]{2,1,0:T(8,128)(2,1)}, bf16[4,32,1024]{2,1,0:T(8,128)(2,1)}, u32[]{:S(2)}, u32[]{:S(2)}) collective-permute-start(bf16[4,32,1024]{2,1,0:T(8,128)(2,1)} %collective-permute-done.7), channel_id=1, source_target_pairs={{0,15},{1,0},{2,1},{3,2},{4,3},{5,4},{6,5},{7,6},{8,7},{9,8},{10,9... | collective-permute-start | bytes 786440 | tf_op jit(solution)/shard_map/ppermute | solution.py:84
  105.0 12.5 %collective-permute-start.16 = (bf16[4,32,1024]{2,1,0:T(8,128)(2,1)}, bf16[4,32,1024]{2,1,0:T(8,128)(2,1)S(1)}, u32[]{:S(2)}, u32[]{:S(2)}) collective-permute-start(bf16[4,32,1024]{2,1,0:T(8,128)(2,1)} %collective-permute-done.15), channel_id=1, source_target_pairs={{0,1},{1,2},{2,3},{3,4},{4,5},{5,6},{6,7},{7,8},{8,9},{9,10},{10,1... | collective-permute-start | bytes 786440 | tf_op jit(solution)/shard_map/ppermute | solution.py:81
  107.7 13.3 %collective-permute-start.9 = (bf16[4,32,1024]{2,1,0:T(8,128)(2,1)}, bf16[4,32,1024]{2,1,0:T(8,128)(2,1)S(1)}, u32[]{:S(2)}, u32[]{:S(2)}) collective-permute-start(bf16[4,32,1024]{2,1,0:T(8,128)(2,1)} %collective-permute-done.8), channel_id=1, source_target_pairs={{0,15},{1,0},{2,1},{3,2},{4,3},{5,4},{6,5},{7,6},{8,7},{9,8},{10,9... | collective-permute-start | bytes 786440 | tf_op jit(solution)/shard_map/ppermute | solution.py:84
  117.4 9.5 %collective-permute-start.17 = (bf16[4,32,1024]{2,1,0:T(8,128)(2,1)S(1)}, bf16[4,32,1024]{2,1,0:T(8,128)(2,1)S(1)}, u32[]{:S(2)}, u32[]{:S(2)}) collective-permute-start(bf16[4,32,1024]{2,1,0:T(8,128)(2,1)S(1)} %collective-permute-done.16), channel_id=1, source_target_pairs={{0,1},{1,2},{2,3},{3,4},{4,5},{5,6},{6,7},{7,8},{8,9},{9,10},{10,1... | collective-permute-start | bytes 786440 | tf_op jit(solution)/shard_map/ppermute | solution.py:81
  146.4 140.7 %all-to-all-start.1 = ((bf16[64,20,1024]{2,1,0:T(8,128)(2,1)}), bf16[64,20,1024]{2,1,0:T(8,128)(2,1)S(1)}, u32[]{:S(2)}, u32[]{:S(2)}) async-start(bf16[64,20,1024]{2,1,0:T(8,128)(2,1)} %reshape.393), calls=%async_computation.1 | async-start | bytes 6291456 | tf_op jit(solution)/shard_map/all_to_all | solution.py:208
  153.3 136.0 %all-gather.4.cloned.1.call-start = ((), (), s32[]{:S(2)}) async-start(), calls=%async_computation.3 | async-start | bytes 1769472 | tf_op jit(solution)/shard_map/all_gather | solution.py:211
  154.0 141.7 %all-gather.6.cloned.1.call-start = ((), (), s32[]{:S(2)}) async-start(), calls=%async_computation.4 | async-start | bytes 1769472 | tf_op jit(solution)/shard_map/all_gather | solution.py:212
  154.7 141.0 %all-gather.8.cloned.1.call-start = ((), (), s32[]{:S(2)}) async-start(), calls=%async_computation.5 | async-start | bytes 1769472 | tf_op jit(solution)/shard_map/all_gather | solution.py:213
  310.9 142.3 %all-to-all-start.2 = ((bf16[64,20,1024]{2,1,0:T(8,128)(2,1)}), bf16[64,20,1024]{2,1,0:T(8,128)(2,1)}, u32[]{:S(2)}, u32[]{:S(2)}) async-start(bf16[64,20,1024]{2,1,0:T(8,128)(2,1)} %reshape.395), calls=%async_computation.2 | async-start | bytes 6291456 | tf_op jit(solution)/shard_map/all_to_all | solution.py:218
  (15 other events, 205.8 us)
Sparse Core Ops, SparseCore 0:
  156.2 31.1 all-gather.3
  189.5 32.2 all-gather.5
  224.0 32.3 all-gather.7

commit v2 on v1

--- a/solution.py
+++ b/solution.py
@@ -86,28 +86,55 @@
     return jnp.stack([relative[k] for k in range(cols)], axis=1)
 
 
+def spread_over_dp(piece, ring, cores):
+    dp_pairs = lambda shift: [
+        (r * cores + c, ((r + shift) % ring) * cores + c) for r in range(ring) for c in range(cores)
+    ]
+    other = lax.ppermute(piece, "dp", [(i, i ^ 1) for i in range(ring * cores)])
+    pair = jnp.stack([piece, other])
+    up = lax.ppermute(pair, "dp", dp_pairs(1))
+    down = lax.ppermute(pair, "dp", dp_pairs(-1))
+    up_two = lax.ppermute(up, "dp", dp_pairs(1))
+    return jnp.stack([pair, down, up_two, up])
+
+
 def project_heads(attended, output_weight):
     expert_total = lax.axis_size("expert")
+    owner_total = lax.axis_size("dp")
     cols = 16
     rows = expert_total // cols
-    if rows != 4 or expert_total % cols:
+    block = output_weight.shape[0]
+    if rows != 4 or expert_total % cols or owner_total != 8 or block % owner_total:
         return jnp.dot(
             attended,
             lax.all_gather(output_weight, "expert", axis=0, tiled=True),
             preferred_element_type=jnp.float32,
         )
+    ring, cores = 4, 2
+    share = block // owner_total
     own = lax.axis_index("expert")
     own_row = own // cols
     own_col = own % cols
-    gathered = ring_gather(output_weight, rows, cols)
-    block = output_weight.shape[0]
-    row_order = (own_row + jnp.arange(rows, dtype=jnp.int32)) % rows
-    col_order = (own_col + jnp.arange(cols, dtype=jnp.int32)) % cols
-    split = attended.reshape(attended.shape[0], rows, cols, block)
-    split = jnp.take(jnp.take(split, row_order, axis=1), col_order, axis=2)
+    own_dp = lax.axis_index("dp")
+    own_x = own_dp // cores
+    own_core = own_dp % cores
+    piece = lax.dynamic_slice_in_dim(output_weight, own_dp * share, share, 0)
+    gathered = spread_over_dp(ring_gather(piece, rows, cols), ring, cores)
+    steps = jnp.arange
+    x_src = (own_x + steps(ring, dtype=jnp.int32)) % ring
+    core_src = own_core ^ steps(cores, dtype=jnp.int32)
+    row_src = (own_row + steps(rows, dtype=jnp.int32)) % rows
+    col_src = (own_col + steps(cols, dtype=jnp.int32)) % cols
+    dp_src = x_src[:, None] * cores + core_src[None, :]
+    block_src = row_src[:, None] * cols + col_src[None, :]
+    column = (
+        block_src[None, None, :, :, None] * block
+        + dp_src[:, :, None, None, None] * share
+        + steps(share, dtype=jnp.int32)[None, None, None, None, :]
+    ).reshape(-1)
     return jnp.dot(
-        split.reshape(attended.shape[0], -1),
-        gathered.reshape(rows * cols * block, -1),
+        jnp.take(attended, column, axis=1),
+        gathered.reshape(column.shape[0], -1),
         preferred_element_type=jnp.float32,
     )
 

time: 480 us -> 541 us (1.13)
  waiting for transfers between devices: 290 us -> 329 us
  starting transfers between devices: 88.3 us -> 97.3 us
  other arithmetic: 11.4 us -> 20.4 us
    ppermute x0 -> x4, waiting for transfers between devices: none -> 29.9 us  [the longest x1 15 us: spread_over_dp(): up_two = lax.ppermute(up, 'dp', dp_pairs(1))]
    unnamed x45 -> x39, local copies, waits for them, and re-layouts: 17 us -> 2.16 us
    ppermute x0 -> x4, starting transfers between devices: none -> 11.3 us  [the longest x1 3.91 us: spread_over_dp(): down = lax.ppermute(pair, 'dp', dp_pairs(-1))]
    all_to_all x1, waiting for transfers between devices: 134 us -> 143 us  [local(): lax.all_to_all(out_slots, 'expert', split_axis=0, concat_axis=0, tiled=True)]
    all_to_all x1, waiting for transfers between devices: 132 us -> 140 us  [local(): lax.all_to_all(outgoing, 'expert', split_axis=0, concat_axis=0, tiled=True)]
    another operation x3 -> x5, other arithmetic: 1.48 us -> 8.41 us  [the longest x2 6.93 us: spread_over_dp(): return jnp.stack([pair, down, up_two, up])]
    reshape x0 -> x1, local copies, waits for them, and re-layouts: none -> 6.9 us  [project_heads(): gathered.reshape(column.shape[0], -1)]
    ppermute x7, waiting for transfers between devices: 5.81 us -> 0.02 us  [ring_gather(): left = lax.ppermute(left, 'expert', ring_pairs(rows, cols, 0, -1))]
  transfers between devices with their start and end apart: 24 -> 28, of which waited for: 11 -> 8; matrix products, arithmetic and copies ran while one was open for 7% -> 7% of each run, Pallas kernels for 0% -> 0%
where the time goes in v2:
time: 541 us; the launch traced here: 538 us
  waiting for transfers between devices  329 us (61%)
  starting transfers between devices  97.3 us (18%)
  local copies, waits for them, and re-layouts  54.8 us (10%)
  matrix products  21.8 us (4%)
  other arithmetic  20.4 us (4%)
  between operations  14 us (3%)
    all_to_all x1, waiting for transfers between devices, local(): lax.all_to_all(out_slots, 'expert', split_axis=0, concat_axis=0, tiled=True)  143 us
    all_to_all x1, waiting for transfers between devices, local(): lax.all_to_all(outgoing, 'expert', split_axis=0, concat_axis=0, tiled=True)  140 us
    ppermute x7, starting transfers between devices, ring_gather(): left = lax.ppermute(left, 'expert', ring_pairs(rows, cols, 0, -1))  37.6 us
    ppermute x8, starting transfers between devices, ring_gather(): right = lax.ppermute(right, 'expert', ring_pairs(rows, cols, 0, 1))  15.4 us
    ppermute x1, waiting for transfers between devices, spread_over_dp(): up_two = lax.ppermute(up, 'dp', dp_pairs(1))  15 us
    ppermute x1, waiting for transfers between devices, spread_over_dp(): up = lax.ppermute(pair, 'dp', dp_pairs(1))  13.1 us
    gather x8, local copies, waits for them, and re-layouts, local(): flat_back[copy_index[:, route_slot]].astype(jnp.float32)  11.8 us
  transfers between devices with their start and end apart: 28, of which 8 were waited for; matrix products, arithmetic and copies ran while one was open for 7% of the time, Pallas kernels for 0%

profile of v2, /device:TPU:6, one launch (start us, length us, event | category | flops | bytes accessed | tf_op | source)
XLA Modules:
  0.0 537.6 jit_solution(1717597363065791161)
XLA Ops:
  21.1 9.3 %all-to-all-start = ((bf16[8,24,3712]{2,1,0:T(8,128)(2,1)}), bf16[8,24,3712]{2,1,0:T(8,128)(2,1)S(1)}, u32[]{:S(2)}, u32[]{:S(2)}) async-start(bf16[8,24,3712]{2,1,0:T(8,128)(2,1)} %bitcast.5), calls=%async_computation | async-start | bytes 2850816 | tf_op jit(solution)/shard_map/all_to_all | solution.py:200
  34.1 4.6 collective-permute-done.2
  38.8 6.8 %collective-permute-start.3 = (bf16[4,4,1024]{2,1,0:T(4,128)(2,1)S(1)}, bf16[4,4,1024]{2,1,0:T(4,128)(2,1)S(1)}, u32[]{:S(2)}, u32[]{:S(2)}) collective-permute-start(bf16[4,4,1024]{2,1,0:T(4,128)(2,1)S(1)} %pad_maximum_fusion.4), channel_id=1, source_target_pairs={{0,15},{1,0},{2,1},{3,2},{4,3},{5,4},{6,5},{7,6},{8,7},{9,8},{10,9... | collective-permute-start | bytes 98312 | tf_op jit(solution)/shard_map/ppermute | solution.py:84
  47.6 5.1 collective-permute-start.4
  54.7 5.1 collective-permute-start.5
  61.8 5.1 collective-permute-start.6
  69.0 5.1 collective-permute-start.7
  76.1 5.1 collective-permute-start.8
  83.2 5.1 collective-permute-start.9
  90.3 5.1 collective-permute-done.16
  97.3 5.1 collective-permute-done.17
  122.5 13.1 %collective-permute-done.20 = bf16[2,4,16,4,1024]{4,3,1,2,0:T(4,128)(2,1)} collective-permute-done((bf16[2,4,16,4,1024]{4,3,1,2,0:T(4,128)(2,1)}, bf16[2,4,16,4,1024]{4,3,1,2,0:T(4,128)(2,1)}, u32[]{:S(2)}, u32[]{:S(2)}) %collective-permute-start.20) | collective-permute-done | bytes 1048608 | tf_op jit(solution)/shard_map/ppermute | solution.py:95
  141.0 6.2 %gather_fusion.2 = bf16[2048,128]{1,0:T(8,128)(2,1)S(1)} fusion(bf16[128,2048]{0,1:T(8,128)(2,1)S(1)} %bitcast.147, s32[2048]{0:T(1024)S(1)} %broadcast_clamp_fusion), kind=kCustom, calls=%fused_computation.2 | custom fusion | bytes 1056768 | tf_op jit(solution)/shard_map/jit(_take)/gather | solution.py:136
  147.2 15.0 %collective-permute-done.21 = bf16[2,4,16,4,1024]{4,3,1,2,0:T(4,128)(2,1)} collective-permute-done((bf16[2,4,16,4,1024]{4,3,1,2,0:T(4,128)(2,1)}, bf16[2,4,16,4,1024]{4,3,1,2,0:T(4,128)(2,1)}, u32[]{:S(2)}, u32[]{:S(2)}) %collective-permute-start.21) | collective-permute-done | bytes 1048608 | tf_op jit(solution)/shard_map/ppermute | solution.py:97
  162.1 5.1 pad_maximum_fusion
  171.5 6.9 %reshape.449 = bf16[2048,1024]{1,0:T(8,128)(2,1)} reshape(bf16[4,2,4,16,4,1024]{5,4,3,2,1,0:T(4,128)(2,1)} %copy.55) | data formatting | bytes 8388608 | tf_op jit(solution)/shard_map/reshape | solution.py:137
  182.9 4.3 gather_fusion.3
  189.6 6.9 %all-to-all-start.1 = ((bf16[64,20,1024]{2,1,0:T(8,128)(2,1)}), bf16[64,20,1024]{2,1,0:T(8,128)(2,1)S(1)}, u32[]{:S(2)}, u32[]{:S(2)}) async-start(bf16[64,20,1024]{2,1,0:T(8,128)(2,1)} %reshape.451), calls=%async_computation.1 | async-start | bytes 6291456 | tf_op jit(solution)/shard_map/all_to_all | solution.py:235
  198.7 139.9 %all-to-all-done.1 = bf16[64,20,1024]{2,1,0:T(8,128)(2,1)S(1)} async-done(((bf16[64,20,1024]{2,1,0:T(8,128)(2,1)}), bf16[64,20,1024]{2,1,0:T(8,128)(2,1)S(1)}, u32[]{:S(2)}, u32[]{:S(2)}) %all-to-all-start.1) | async-done | bytes 2621472 | tf_op jit(solution)/shard_map/all_to_all | solution.py:235
  340.8 6.4 %fusion.4 = f32[1280,768]{1,0:T(8,128)} fusion(bf16[1280,1024]{1,0:T(8,128)(2,1)} %reshape.452, bf16[1,768,1024]{2,1,0:T(8,128)(2,1)} %all-gather.4.cloned.1.call-done), kind=kOutput, calls=%fused_computation.19 | convolution fusion | flops 2013265920 | bytes 8126464 | tf_op jit(solution)/shard_map/dot_general | solution.py:144
  347.3 10.0 %convolution_convert_fusion = bf16[1280,1024]{1,0:T(8,128)(2,1)} fusion(bf16[1,768,1024]{2,1,0:T(8,128)(2,1)} %all-gather.8.cloned.1.call-done, bf16[1280,1024]{1,0:T(8,128)(2,1)S(1)} %copy-done.4, f32[1280,768]{1,0:T(8,128)} %fusion.4, bf16[1,768,1024]{2,1,0:T(8,128)(2,1)} %all-gather.6.cloned.1.call-done), kind=kOutput, calls=%fused_computation.15 | convolution fusion | flops 4033740800 | bytes 12320768 | tf_op jit(solution)/shard_map/dot_general | solution.py:147
  357.3 5.2 reshape.453
  362.4 7.4 %all-to-all-start.2 = ((bf16[64,20,1024]{2,1,0:T(8,128)(2,1)}), bf16[64,20,1024]{2,1,0:T(8,128)(2,1)}, u32[]{:S(2)}, u32[]{:S(2)}) async-start(bf16[64,20,1024]{2,1,0:T(8,128)(2,1)} %reshape.453), calls=%async_computation.2 | async-start | bytes 6291456 | tf_op jit(solution)/shard_map/all_to_all | solution.py:245
  370.1 142.9 %all-to-all-done.2 = bf16[64,20,1024]{2,1,0:T(8,128)(2,1)} async-done(((bf16[64,20,1024]{2,1,0:T(8,128)(2,1)}), bf16[64,20,1024]{2,1,0:T(8,128)(2,1)}, u32[]{:S(2)}, u32[]{:S(2)}) %all-to-all-start.2) | async-done | bytes 2621472 | tf_op jit(solution)/shard_map/all_to_all | solution.py:245
  (175 shorter events, 92.5 us)
Async XLA Ops:
  7.4 24.6 %collective-permute-start.1 = (bf16[4,1024]{1,0:T(4,128)(2,1)S(1)}, bf16[4,1024]{1,0:T(4,128)(2,1)S(1)}, u32[]{:S(2)}, u32[]{:S(2)}) collective-permute-start(bf16[4,1024]{1,0:T(4,128)(2,1)S(1)} %constant_dynamic-slice_fusion), channel_id=1, source_target_pairs={{0,16},{1,17},{2,18},{3,19},{4,20},{5,21},{6,22},{7,23},{8,24},{9,... | collective-permute-start | bytes 24584 | tf_op jit(solution)/shard_map/ppermute | solution.py:72
  10.9 23.2 %collective-permute-start = (bf16[4,1024]{1,0:T(4,128)(2,1)S(1)}, bf16[4,1024]{1,0:T(4,128)(2,1)S(1)}, u32[]{:S(2)}, u32[]{:S(2)}) collective-permute-start(bf16[4,1024]{1,0:T(4,128)(2,1)S(1)} %constant_dynamic-slice_fusion), channel_id=1, source_target_pairs={{0,48},{1,49},{2,50},{3,51},{4,52},{5,53},{6,54},{7,55},{8,56},{9,... | collective-permute-start | bytes 24584 | tf_op jit(solution)/shard_map/ppermute | solution.py:73
  21.1 93.0 %all-to-all-start = ((bf16[8,24,3712]{2,1,0:T(8,128)(2,1)}), bf16[8,24,3712]{2,1,0:T(8,128)(2,1)S(1)}, u32[]{:S(2)}, u32[]{:S(2)}) async-start(bf16[8,24,3712]{2,1,0:T(8,128)(2,1)} %bitcast.5), calls=%async_computation | async-start | bytes 2850816 | tf_op jit(solution)/shard_map/all_to_all | solution.py:200
  38.8 8.8 %collective-permute-start.3 = (bf16[4,4,1024]{2,1,0:T(4,128)(2,1)S(1)}, bf16[4,4,1024]{2,1,0:T(4,128)(2,1)S(1)}, u32[]{:S(2)}, u32[]{:S(2)}) collective-permute-start(bf16[4,4,1024]{2,1,0:T(4,128)(2,1)S(1)} %pad_maximum_fusion.4), channel_id=1, source_target_pairs={{0,15},{1,0},{2,1},{3,2},{4,3},{5,4},{6,5},{7,6},{8,7},{9,8},{10,9... | collective-permute-start | bytes 98312 | tf_op jit(solution)/shard_map/ppermute | solution.py:84
  45.6 7.1 %collective-permute-start.10 = (bf16[4,4,1024]{2,1,0:T(4,128)(2,1)S(1)}, bf16[4,4,1024]{2,1,0:T(4,128)(2,1)S(1)}, u32[]{:S(2)}, u32[]{:S(2)}) collective-permute-start(bf16[4,4,1024]{2,1,0:T(4,128)(2,1)S(1)} %pad_maximum_fusion.4), channel_id=1, source_target_pairs={{0,1},{1,2},{2,3},{3,4},{4,5},{5,6},{6,7},{7,8},{8,9},{9,10},{10,1... | collective-permute-start | bytes 98312 | tf_op jit(solution)/shard_map/ppermute | solution.py:81
  47.6 7.1 %collective-permute-start.4 = (bf16[4,4,1024]{2,1,0:T(4,128)(2,1)S(1)}, bf16[4,4,1024]{2,1,0:T(4,128)(2,1)S(1)}, u32[]{:S(2)}, u32[]{:S(2)}) collective-permute-start(bf16[4,4,1024]{2,1,0:T(4,128)(2,1)S(1)} %collective-permute-done.3), channel_id=1, source_target_pairs={{0,15},{1,0},{2,1},{3,2},{4,3},{5,4},{6,5},{7,6},{8,7},{9,8},{10,9... | collective-permute-start | bytes 98312 | tf_op jit(solution)/shard_map/ppermute | solution.py:84
  52.8 7.1 %collective-permute-start.11 = (bf16[4,4,1024]{2,1,0:T(4,128)(2,1)S(1)}, bf16[4,4,1024]{2,1,0:T(4,128)(2,1)S(1)}, u32[]{:S(2)}, u32[]{:S(2)}) collective-permute-start(bf16[4,4,1024]{2,1,0:T(4,128)(2,1)S(1)} %collective-permute-done.10), channel_id=1, source_target_pairs={{0,1},{1,2},{2,3},{3,4},{4,5},{5,6},{6,7},{7,8},{8,9},{9,10},{10,1... | collective-permute-start | bytes 98312 | tf_op jit(solution)/shard_map/ppermute | solution.py:81
  54.7 7.1 %collective-permute-start.5 = (bf16[4,4,1024]{2,1,0:T(4,128)(2,1)S(1)}, bf16[4,4,1024]{2,1,0:T(4,128)(2,1)S(1)}, u32[]{:S(2)}, u32[]{:S(2)}) collective-permute-start(bf16[4,4,1024]{2,1,0:T(4,128)(2,1)S(1)} %collective-permute-done.4), channel_id=1, source_target_pairs={{0,15},{1,0},{2,1},{3,2},{4,3},{5,4},{6,5},{7,6},{8,7},{9,8},{10,9... | collective-permute-start | bytes 98312 | tf_op jit(solution)/shard_map/ppermute | solution.py:84
  59.9 7.1 %collective-permute-start.12 = (bf16[4,4,1024]{2,1,0:T(4,128)(2,1)S(1)}, bf16[4,4,1024]{2,1,0:T(4,128)(2,1)S(1)}, u32[]{:S(2)}, u32[]{:S(2)}) collective-permute-start(bf16[4,4,1024]{2,1,0:T(4,128)(2,1)S(1)} %collective-permute-done.11), channel_id=1, source_target_pairs={{0,1},{1,2},{2,3},{3,4},{4,5},{5,6},{6,7},{7,8},{8,9},{9,10},{10,1... | collective-permute-start | bytes 98312 | tf_op jit(solution)/shard_map/ppermute | solution.py:81
  61.8 7.1 %collective-permute-start.6 = (bf16[4,4,1024]{2,1,0:T(4,128)(2,1)S(1)}, bf16[4,4,1024]{2,1,0:T(4,128)(2,1)S(1)}, u32[]{:S(2)}, u32[]{:S(2)}) collective-permute-start(bf16[4,4,1024]{2,1,0:T(4,128)(2,1)S(1)} %collective-permute-done.5), channel_id=1, source_target_pairs={{0,15},{1,0},{2,1},{3,2},{4,3},{5,4},{6,5},{7,6},{8,7},{9,8},{10,9... | collective-permute-start | bytes 98312 | tf_op jit(solution)/shard_map/ppermute | solution.py:84
  67.0 7.1 %collective-permute-start.13 = (bf16[4,4,1024]{2,1,0:T(4,128)(2,1)S(1)}, bf16[4,4,1024]{2,1,0:T(4,128)(2,1)S(1)}, u32[]{:S(2)}, u32[]{:S(2)}) collective-permute-start(bf16[4,4,1024]{2,1,0:T(4,128)(2,1)S(1)} %collective-permute-done.12), channel_id=1, source_target_pairs={{0,1},{1,2},{2,3},{3,4},{4,5},{5,6},{6,7},{7,8},{8,9},{9,10},{10,1... | collective-permute-start | bytes 98312 | tf_op jit(solution)/shard_map/ppermute | solution.py:81
  69.0 7.1 %collective-permute-start.7 = (bf16[4,4,1024]{2,1,0:T(4,128)(2,1)S(1)}, bf16[4,4,1024]{2,1,0:T(4,128)(2,1)S(1)}, u32[]{:S(2)}, u32[]{:S(2)}) collective-permute-start(bf16[4,4,1024]{2,1,0:T(4,128)(2,1)S(1)} %collective-permute-done.6), channel_id=1, source_target_pairs={{0,15},{1,0},{2,1},{3,2},{4,3},{5,4},{6,5},{7,6},{8,7},{9,8},{10,9... | collective-permute-start | bytes 98312 | tf_op jit(solution)/shard_map/ppermute | solution.py:84
  74.1 7.1 %collective-permute-start.14 = (bf16[4,4,1024]{2,1,0:T(4,128)(2,1)S(1)}, bf16[4,4,1024]{2,1,0:T(4,128)(2,1)S(1)}, u32[]{:S(2)}, u32[]{:S(2)}) collective-permute-start(bf16[4,4,1024]{2,1,0:T(4,128)(2,1)S(1)} %collective-permute-done.13), channel_id=1, source_target_pairs={{0,1},{1,2},{2,3},{3,4},{4,5},{5,6},{6,7},{7,8},{8,9},{9,10},{10,1... | collective-permute-start | bytes 98312 | tf_op jit(solution)/shard_map/ppermute | solution.py:81
  76.1 7.1 %collective-permute-start.8 = (bf16[4,4,1024]{2,1,0:T(4,128)(2,1)S(1)}, bf16[4,4,1024]{2,1,0:T(4,128)(2,1)S(1)}, u32[]{:S(2)}, u32[]{:S(2)}) collective-permute-start(bf16[4,4,1024]{2,1,0:T(4,128)(2,1)S(1)} %collective-permute-done.7), channel_id=1, source_target_pairs={{0,15},{1,0},{2,1},{3,2},{4,3},{5,4},{6,5},{7,6},{8,7},{9,8},{10,9... | collective-permute-start | bytes 98312 | tf_op jit(solution)/shard_map/ppermute | solution.py:84
  81.2 7.1 %collective-permute-start.15 = (bf16[4,4,1024]{2,1,0:T(4,128)(2,1)S(1)}, bf16[4,4,1024]{2,1,0:T(4,128)(2,1)S(1)}, u32[]{:S(2)}, u32[]{:S(2)}) collective-permute-start(bf16[4,4,1024]{2,1,0:T(4,128)(2,1)S(1)} %collective-permute-done.14), channel_id=1, source_target_pairs={{0,1},{1,2},{2,3},{3,4},{4,5},{5,6},{6,7},{7,8},{8,9},{9,10},{10,1... | collective-permute-start | bytes 98312 | tf_op jit(solution)/shard_map/ppermute | solution.py:81
  83.2 14.1 %collective-permute-start.9 = (bf16[4,4,1024]{2,1,0:T(4,128)(2,1)S(1)}, bf16[4,4,1024]{2,1,0:T(4,128)(2,1)S(1)}, u32[]{:S(2)}, u32[]{:S(2)}) collective-permute-start(bf16[4,4,1024]{2,1,0:T(4,128)(2,1)S(1)} %collective-permute-done.8), channel_id=1, source_target_pairs={{0,15},{1,0},{2,1},{3,2},{4,3},{5,4},{6,5},{7,6},{8,7},{9,8},{10,9... | collective-permute-start | bytes 98312 | tf_op jit(solution)/shard_map/ppermute | solution.py:84
  108.2 27.4 %collective-permute-start.20 = (bf16[2,4,16,4,1024]{4,3,1,2,0:T(4,128)(2,1)}, bf16[2,4,16,4,1024]{4,3,1,2,0:T(4,128)(2,1)}, u32[]{:S(2)}, u32[]{:S(2)}) collective-permute-start(bf16[2,4,16,4,1024]{4,3,1,2,0:T(4,128)(2,1)} %get-tuple-element.13), channel_id=1, source_target_pairs={{0,128},{64,192},{128,256},{192,320},{256,384},{320,448},{384,0},{... | collective-permute-start | bytes 3145736 | tf_op jit(solution)/shard_map/ppermute | solution.py:95
  110.1 37.0 %collective-permute-start.19 = (bf16[2,4,16,4,1024]{4,3,1,2,0:T(4,128)(2,1)}, bf16[2,4,16,4,1024]{4,3,1,2,0:T(4,128)(2,1)}, u32[]{:S(2)}, u32[]{:S(2)}) collective-permute-start(bf16[2,4,16,4,1024]{4,3,1,2,0:T(4,128)(2,1)} %get-tuple-element.13), channel_id=1, source_target_pairs={{0,384},{64,448},{128,0},{192,64},{256,128},{320,192},{384,256},{4... | collective-permute-start | bytes 3145736 | tf_op jit(solution)/shard_map/ppermute | solution.py:96
  135.6 26.5 %collective-permute-start.21 = (bf16[2,4,16,4,1024]{4,3,1,2,0:T(4,128)(2,1)}, bf16[2,4,16,4,1024]{4,3,1,2,0:T(4,128)(2,1)}, u32[]{:S(2)}, u32[]{:S(2)}) collective-permute-start(bf16[2,4,16,4,1024]{4,3,1,2,0:T(4,128)(2,1)} %collective-permute-done.20), channel_id=1, source_target_pairs={{0,128},{64,192},{128,256},{192,320},{256,384},{320,448},{384,0},{... | collective-permute-start | bytes 3145736 | tf_op jit(solution)/shard_map/ppermute | solution.py:97
  189.6 149.0 %all-to-all-start.1 = ((bf16[64,20,1024]{2,1,0:T(8,128)(2,1)}), bf16[64,20,1024]{2,1,0:T(8,128)(2,1)S(1)}, u32[]{:S(2)}, u32[]{:S(2)}) async-start(bf16[64,20,1024]{2,1,0:T(8,128)(2,1)} %reshape.451), calls=%async_computation.1 | async-start | bytes 6291456 | tf_op jit(solution)/shard_map/all_to_all | solution.py:235
  196.5 144.3 %all-gather.4.cloned.1.call-start = ((), (), s32[]{:S(2)}) async-start(), calls=%async_computation.3 | async-start | bytes 1769472 | tf_op jit(solution)/shard_map/all_gather | solution.py:238
  197.2 150.0 %all-gather.6.cloned.1.call-start = ((), (), s32[]{:S(2)}) async-start(), calls=%async_computation.4 | async-start | bytes 1769472 | tf_op jit(solution)/shard_map/all_gather | solution.py:239
  198.0 149.3 %all-gather.8.cloned.1.call-start = ((), (), s32[]{:S(2)}) async-start(), calls=%async_computation.5 | async-start | bytes 1769472 | tf_op jit(solution)/shard_map/all_gather | solution.py:240
  362.4 150.5 %all-to-all-start.2 = ((bf16[64,20,1024]{2,1,0:T(8,128)(2,1)}), bf16[64,20,1024]{2,1,0:T(8,128)(2,1)}, u32[]{:S(2)}, u32[]{:S(2)}) async-start(bf16[64,20,1024]{2,1,0:T(8,128)(2,1)} %reshape.453), calls=%async_computation.2 | async-start | bytes 6291456 | tf_op jit(solution)/shard_map/all_to_all | solution.py:245
  (16 other events, 68.8 us)
Sparse Core Ops, SparseCore 0:
  199.4 31.2 all-gather.3
  232.8 32.2 all-gather.5
  267.3 32.3 all-gather.7

commit v3 on v1

--- a/solution.py
+++ b/solution.py
@@ -205,17 +205,35 @@
     source_token = jnp.sum(jnp.where(hits, pack_ids[None, :, None], 0), axis=1)
     outgoing = normed[source_token.reshape(-1)].reshape(expert_total, most, -1)
     total_rows = expert_total * most
-    received = lax.all_to_all(outgoing, "expert", split_axis=0, concat_axis=0, tiled=True)
-    work_rows = received.reshape(total_rows, -1)
     gate_whole, up_whole, down_whole = (
         lax.all_gather(gate_weight, "dp", axis=1, tiled=True),
         lax.all_gather(up_weight, "dp", axis=1, tiled=True),
         lax.all_gather(down_weight, "dp", axis=1, tiled=True),
     )
-    produced = expert_output(work_rows, gate_whole[0], up_whole[0], down_whole[0])
-    produced = produced.astype(jnp.bfloat16)
-    out_slots = produced.reshape(expert_total, most, -1)
-    returned = lax.all_to_all(out_slots, "expert", split_axis=0, concat_axis=0, tiled=True)
+    chunks = 2
+    chunk = most // chunks
+    pieces = []
+    for part in range(chunks):
+        received = lax.all_to_all(
+            outgoing[:, part * chunk : (part + 1) * chunk],
+            "expert",
+            split_axis=0,
+            concat_axis=0,
+            tiled=True,
+        )
+        produced = expert_output(
+            received.reshape(expert_total * chunk, -1), gate_whole[0], up_whole[0], down_whole[0]
+        ).astype(jnp.bfloat16)
+        pieces.append(
+            lax.all_to_all(
+                produced.reshape(expert_total, chunk, -1),
+                "expert",
+                split_axis=0,
+                concat_axis=0,
+                tiled=True,
+            )
+        )
+    returned = jnp.concatenate(pieces, axis=1)
     flat_back = returned.reshape(total_rows, -1)
     copy_rank = jnp.sum(jnp.where(routed, rank[:, None, :], 0), axis=2)
     copy_index = routes * most + copy_rank

time: 480 us -> 575 us (1.20)
  waiting for transfers between devices: 290 us -> 352 us
  starting transfers between devices: 88.3 us -> 108 us
  local copies, waits for them, and re-layouts: 52.4 us -> 58.3 us
    all_to_all x2 -> x4, waiting for transfers between devices: 266 us -> 298 us  [the longest x2 164 us: local(): lax.all_to_all(produced.reshape(expert_total, chunk, -1), 'expert', split...]
    all_gather x1, waiting for transfers between devices: 0.01 us -> 28.7 us  [local(): lax.all_gather(up_weight, 'dp', axis=1, tiled=True)]
    all_to_all x2 -> x4, starting transfers between devices: 14.8 us -> 34.4 us  [the longest x2 18.7 us: local(): lax.all_to_all(produced.reshape(expert_total, chunk, -1), 'expert', split...]
    dot_general x1 -> x2, matrix products: 10 us -> 11.8 us  [hidden_product(): return jnp.dot(active, down_part, preferred_element_type=jnp.float32)]
    unnamed x45 -> x43, local copies, waits for them, and re-layouts: 17 us -> 17 us
  transfers between devices with their start and end apart: 24 -> 26, of which waited for: 11 -> 14; matrix products, arithmetic and copies ran while one was open for 7% -> 9% of each run, Pallas kernels for 0% -> 0%
where the time goes in v3:
time: 575 us; the launch traced here: 572 us
  waiting for transfers between devices  352 us (61%)
  starting transfers between devices  108 us (19%)
  local copies, waits for them, and re-layouts  58.3 us (10%)
  matrix products  24.5 us (4%)
  other arithmetic  15.8 us (3%)
  between operations  13.9 us (2%)
    all_to_all x2, waiting for transfers between devices, local(): lax.all_to_all(produced.reshape(expert_total, chunk, -1), 'expert', split...  164 us
    all_to_all x2, waiting for transfers between devices, local(): lax.all_to_all(outgoing[:, part * chunk:(part + 1) * chunk], 'expert', sp...  134 us
    ppermute x7, starting transfers between devices, ring_gather(): left = lax.ppermute(left, 'expert', ring_pairs(rows, cols, 0, -1))  39.6 us
    all_gather x1, waiting for transfers between devices, local(): lax.all_gather(up_weight, 'dp', axis=1, tiled=True)  28.7 us
    all_to_all x2, starting transfers between devices, local(): lax.all_to_all(produced.reshape(expert_total, chunk, -1), 'expert', split...  18.7 us
    unnamed x43, local copies, waits for them, and re-layouts  17 us
    all_to_all x2, starting transfers between devices, local(): lax.all_to_all(outgoing[:, part * chunk:(part + 1) * chunk], 'expert', sp...  15.8 us
    ppermute x8, starting transfers between devices, ring_gather(): right = lax.ppermute(right, 'expert', ring_pairs(rows, cols, 0, 1))  15.5 us
  transfers between devices with their start and end apart: 26, of which 14 were waited for; matrix products, arithmetic and copies ran while one was open for 9% of the time, Pallas kernels for 0%

profile of v3, /device:TPU:6, one launch (start us, length us, event | category | flops | bytes accessed | tf_op | source)
XLA Modules:
  0.0 572.3 jit_solution(3027014787140592997)
XLA Ops:
  20.2 9.5 %all-to-all-start = ((bf16[8,24,3712]{2,1,0:T(8,128)(2,1)}), bf16[8,24,3712]{2,1,0:T(8,128)(2,1)S(1)}, u32[]{:S(2)}, u32[]{:S(2)}) async-start(bf16[8,24,3712]{2,1,0:T(8,128)(2,1)} %bitcast.5), calls=%async_computation | async-start | bytes 2850816 | tf_op jit(solution)/shard_map/all_to_all | solution.py:173
  32.4 5.4 collective-permute-done.2
  37.8 6.8 %collective-permute-start.3 = (bf16[4,32,1024]{2,1,0:T(8,128)(2,1)S(1)}, bf16[4,32,1024]{2,1,0:T(8,128)(2,1)S(1)}, u32[]{:S(2)}, u32[]{:S(2)}) collective-permute-start(bf16[4,32,1024]{2,1,0:T(8,128)(2,1)S(1)} %pad_maximum_fusion.3), channel_id=1, source_target_pairs={{0,15},{1,0},{2,1},{3,2},{4,3},{5,4},{6,5},{7,6},{8,7},{9,8},{10,9... | collective-permute-start | bytes 786440 | tf_op jit(solution)/shard_map/ppermute | solution.py:84
  49.6 5.6 collective-permute-start.4
  59.3 5.6 collective-permute-start.5
  68.8 5.6 collective-permute-start.6
  78.3 5.7 collective-permute-start.7
  96.6 5.1 collective-permute-start.8
  107.8 5.2 collective-permute-start.9
  122.0 5.0 collective-permute-done.17
  139.8 5.1 gather_fusion.4
  151.6 6.9 %all-to-all-start.3 = ((bf16[64,10,1024]{2,1,0:T(8,128)(2,1)}), bf16[64,10,1024]{2,1,0:T(8,128)(2,1)S(1)}, u32[]{:S(2)}, u32[]{:S(2)}) async-start(bf16[64,10,1024]{2,1,0:T(8,128)(2,1)} %get-tuple-element.11), calls=%async_computation.3 | async-start | bytes 4194304 | tf_op jit(solution)/shard_map/all_to_all | solution.py:217
  160.0 86.3 %all-to-all-done.3 = bf16[64,10,1024]{2,1,0:T(8,128)(2,1)S(1)} async-done(((bf16[64,10,1024]{2,1,0:T(8,128)(2,1)}), bf16[64,10,1024]{2,1,0:T(8,128)(2,1)S(1)}, u32[]{:S(2)}, u32[]{:S(2)}) %all-to-all-start.3) | async-done | bytes 1310752 | tf_op jit(solution)/shard_map/all_to_all | solution.py:217
  246.3 8.9 %all-to-all-start.1 = ((bf16[64,10,1024]{2,1,0:T(8,128)(2,1)}), bf16[64,10,1024]{2,1,0:T(8,128)(2,1)}, u32[]{:S(2)}, u32[]{:S(2)}) async-start(bf16[64,10,1024]{2,1,0:T(8,128)(2,1)} %get-tuple-element.10), calls=%async_computation.1 | async-start | bytes 4194304 | tf_op jit(solution)/shard_map/all_to_all | solution.py:217
  256.4 3.9 fusion.5
  260.3 28.7 %all-gather.6.cloned.1.call-done = bf16[1,768,1024]{2,1,0:T(8,128)(2,1)} async-done(((bf16[1,96,1024]{2,1,0:T(8,128)(2,1)}), bf16[1,768,1024]{2,1,0:T(8,128)(2,1)}) %all-gather.6.cloned.1.call-update) | async-done | bytes 1572880 | tf_op jit(solution)/shard_map/all_gather | solution.py:210
  289.1 5.3 convolution_convert_fusion
  296.0 47.8 %all-to-all-done.1 = bf16[64,10,1024]{2,1,0:T(8,128)(2,1)} async-done(((bf16[64,10,1024]{2,1,0:T(8,128)(2,1)}), bf16[64,10,1024]{2,1,0:T(8,128)(2,1)}, u32[]{:S(2)}, u32[]{:S(2)}) %all-to-all-start.1) | async-done | bytes 1310752 | tf_op jit(solution)/shard_map/all_to_all | solution.py:217
  343.8 9.2 %all-to-all-start.4 = ((bf16[64,10,1024]{2,1,0:T(8,128)(2,1)}), bf16[64,10,1024]{2,1,0:T(8,128)(2,1)S(1)}, u32[]{:S(2)}, u32[]{:S(2)}) async-start(bf16[64,10,1024]{2,1,0:T(8,128)(2,1)} %reshape.403), calls=%async_computation.4 | async-start | bytes 4194304 | tf_op jit(solution)/shard_map/all_to_all | solution.py:228
  359.5 6.5 %convolution_convert_fusion.1 = bf16[640,1024]{1,0:T(8,128)(2,1)} fusion(bf16[1,768,1024]{2,1,0:T(8,128)(2,1)} %all-gather.8.cloned.1.call-done, f32[640,768]{1,0:T(8,128)} %fusion.7, bf16[640,1024]{1,0:T(8,128)(2,1)S(1)} %reshape.400, bf16[1,768,1024]{2,1,0:T(8,128)(2,1)} %all-gather.6.cloned.1.call-done), kind=kOutput, calls=%fused_computation.18 | convolution fusion | flops 2016870400 | bytes 7733248 | tf_op jit(solution)/shard_map/dot_general | solution.py:120
  369.6 73.0 %all-to-all-done.4 = bf16[64,10,1024]{2,1,0:T(8,128)(2,1)S(1)} async-done(((bf16[64,10,1024]{2,1,0:T(8,128)(2,1)}), bf16[64,10,1024]{2,1,0:T(8,128)(2,1)S(1)}, u32[]{:S(2)}, u32[]{:S(2)}) %all-to-all-start.4) | async-done | bytes 1310752 | tf_op jit(solution)/shard_map/all_to_all | solution.py:228
  442.5 9.4 %all-to-all-start.2 = ((bf16[64,10,1024]{2,1,0:T(8,128)(2,1)}), bf16[64,10,1024]{2,1,0:T(8,128)(2,1)}, u32[]{:S(2)}, u32[]{:S(2)}) async-start(bf16[64,10,1024]{2,1,0:T(8,128)(2,1)} %reshape.401), calls=%async_computation.2 | async-start | bytes 4194304 | tf_op jit(solution)/shard_map/all_to_all | solution.py:228
  452.2 91.1 %all-to-all-done.2 = bf16[64,10,1024]{2,1,0:T(8,128)(2,1)} async-done(((bf16[64,10,1024]{2,1,0:T(8,128)(2,1)}), bf16[64,10,1024]{2,1,0:T(8,128)(2,1)}, u32[]{:S(2)}, u32[]{:S(2)}) %all-to-all-start.2) | async-done | bytes 1310752 | tf_op jit(solution)/shard_map/all_to_all | solution.py:228
  543.3 4.4 pad_maximum_fusion
  (169 shorter events, 112.3 us)
Async XLA Ops:
  6.5 23.9 %collective-permute-start.1 = (bf16[32,1024]{1,0:T(8,128)(2,1)}, bf16[32,1024]{1,0:T(8,128)(2,1)S(1)}, u32[]{:S(2)}, u32[]{:S(2)}) collective-permute-start(bf16[32,1024]{1,0:T(8,128)(2,1)} %param.25), channel_id=1, source_target_pairs={{0,16},{1,17},{2,18},{3,19},{4,20},{5,21},{6,22},{7,23},{8,24},{9,... | collective-permute-start | bytes 196616 | tf_op jit(solution)/shard_map/ppermute | solution.py:72
  10.0 22.3 %collective-permute-start = (bf16[32,1024]{1,0:T(8,128)(2,1)}, bf16[32,1024]{1,0:T(8,128)(2,1)S(1)}, u32[]{:S(2)}, u32[]{:S(2)}) collective-permute-start(bf16[32,1024]{1,0:T(8,128)(2,1)} %param.25), channel_id=1, source_target_pairs={{0,48},{1,49},{2,50},{3,51},{4,52},{5,53},{6,54},{7,55},{8,56},{9,... | collective-permute-start | bytes 196616 | tf_op jit(solution)/shard_map/ppermute | solution.py:73
  20.2 67.4 %all-to-all-start = ((bf16[8,24,3712]{2,1,0:T(8,128)(2,1)}), bf16[8,24,3712]{2,1,0:T(8,128)(2,1)S(1)}, u32[]{:S(2)}, u32[]{:S(2)}) async-start(bf16[8,24,3712]{2,1,0:T(8,128)(2,1)} %bitcast.5), calls=%async_computation | async-start | bytes 2850816 | tf_op jit(solution)/shard_map/all_to_all | solution.py:173
  37.8 11.8 %collective-permute-start.3 = (bf16[4,32,1024]{2,1,0:T(8,128)(2,1)S(1)}, bf16[4,32,1024]{2,1,0:T(8,128)(2,1)S(1)}, u32[]{:S(2)}, u32[]{:S(2)}) collective-permute-start(bf16[4,32,1024]{2,1,0:T(8,128)(2,1)S(1)} %pad_maximum_fusion.3), channel_id=1, source_target_pairs={{0,15},{1,0},{2,1},{3,2},{4,3},{5,4},{6,5},{7,6},{8,7},{9,8},{10,9... | collective-permute-start | bytes 786440 | tf_op jit(solution)/shard_map/ppermute | solution.py:84
  44.7 10.6 %collective-permute-start.10 = (bf16[4,32,1024]{2,1,0:T(8,128)(2,1)S(1)}, bf16[4,32,1024]{2,1,0:T(8,128)(2,1)S(1)}, u32[]{:S(2)}, u32[]{:S(2)}) collective-permute-start(bf16[4,32,1024]{2,1,0:T(8,128)(2,1)S(1)} %pad_maximum_fusion.3), channel_id=1, source_target_pairs={{0,1},{1,2},{2,3},{3,4},{4,5},{5,6},{6,7},{7,8},{8,9},{9,10},{10,1... | collective-permute-start | bytes 786440 | tf_op jit(solution)/shard_map/ppermute | solution.py:81
  49.6 9.7 %collective-permute-start.4 = (bf16[4,32,1024]{2,1,0:T(8,128)(2,1)S(1)}, bf16[4,32,1024]{2,1,0:T(8,128)(2,1)S(1)}, u32[]{:S(2)}, u32[]{:S(2)}) collective-permute-start(bf16[4,32,1024]{2,1,0:T(8,128)(2,1)S(1)} %collective-permute-done.3), channel_id=1, source_target_pairs={{0,15},{1,0},{2,1},{3,2},{4,3},{5,4},{6,5},{7,6},{8,7},{9,8},{10,9... | collective-permute-start | bytes 786440 | tf_op jit(solution)/shard_map/ppermute | solution.py:84
  55.2 9.7 %collective-permute-start.11 = (bf16[4,32,1024]{2,1,0:T(8,128)(2,1)S(1)}, bf16[4,32,1024]{2,1,0:T(8,128)(2,1)S(1)}, u32[]{:S(2)}, u32[]{:S(2)}) collective-permute-start(bf16[4,32,1024]{2,1,0:T(8,128)(2,1)S(1)} %collective-permute-done.10), channel_id=1, source_target_pairs={{0,1},{1,2},{2,3},{3,4},{4,5},{5,6},{6,7},{7,8},{8,9},{9,10},{10,1... | collective-permute-start | bytes 786440 | tf_op jit(solution)/shard_map/ppermute | solution.py:81
  59.3 9.5 %collective-permute-start.5 = (bf16[4,32,1024]{2,1,0:T(8,128)(2,1)S(1)}, bf16[4,32,1024]{2,1,0:T(8,128)(2,1)S(1)}, u32[]{:S(2)}, u32[]{:S(2)}) collective-permute-start(bf16[4,32,1024]{2,1,0:T(8,128)(2,1)S(1)} %collective-permute-done.4), channel_id=1, source_target_pairs={{0,15},{1,0},{2,1},{3,2},{4,3},{5,4},{6,5},{7,6},{8,7},{9,8},{10,9... | collective-permute-start | bytes 786440 | tf_op jit(solution)/shard_map/ppermute | solution.py:84
  65.0 9.5 %collective-permute-start.12 = (bf16[4,32,1024]{2,1,0:T(8,128)(2,1)S(1)}, bf16[4,32,1024]{2,1,0:T(8,128)(2,1)S(1)}, u32[]{:S(2)}, u32[]{:S(2)}) collective-permute-start(bf16[4,32,1024]{2,1,0:T(8,128)(2,1)S(1)} %collective-permute-done.11), channel_id=1, source_target_pairs={{0,1},{1,2},{2,3},{3,4},{4,5},{5,6},{6,7},{7,8},{8,9},{9,10},{10,1... | collective-permute-start | bytes 786440 | tf_op jit(solution)/shard_map/ppermute | solution.py:81
  68.8 9.5 %collective-permute-start.6 = (bf16[4,32,1024]{2,1,0:T(8,128)(2,1)S(1)}, bf16[4,32,1024]{2,1,0:T(8,128)(2,1)}, u32[]{:S(2)}, u32[]{:S(2)}) collective-permute-start(bf16[4,32,1024]{2,1,0:T(8,128)(2,1)S(1)} %collective-permute-done.5), channel_id=1, source_target_pairs={{0,15},{1,0},{2,1},{3,2},{4,3},{5,4},{6,5},{7,6},{8,7},{9,8},{10,9... | collective-permute-start | bytes 786440 | tf_op jit(solution)/shard_map/ppermute | solution.py:84
  74.4 9.6 %collective-permute-start.13 = (bf16[4,32,1024]{2,1,0:T(8,128)(2,1)S(1)}, bf16[4,32,1024]{2,1,0:T(8,128)(2,1)}, u32[]{:S(2)}, u32[]{:S(2)}) collective-permute-start(bf16[4,32,1024]{2,1,0:T(8,128)(2,1)S(1)} %collective-permute-done.12), channel_id=1, source_target_pairs={{0,1},{1,2},{2,3},{3,4},{4,5},{5,6},{6,7},{7,8},{8,9},{9,10},{10,1... | collective-permute-start | bytes 786440 | tf_op jit(solution)/shard_map/ppermute | solution.py:81
  78.3 18.4 %collective-permute-start.7 = (bf16[4,32,1024]{2,1,0:T(8,128)(2,1)}, bf16[4,32,1024]{2,1,0:T(8,128)(2,1)}, u32[]{:S(2)}, u32[]{:S(2)}) collective-permute-start(bf16[4,32,1024]{2,1,0:T(8,128)(2,1)} %collective-permute-done.6), channel_id=1, source_target_pairs={{0,15},{1,0},{2,1},{3,2},{4,3},{5,4},{6,5},{7,6},{8,7},{9,8},{10,9... | collective-permute-start | bytes 786440 | tf_op jit(solution)/shard_map/ppermute | solution.py:84
  84.0 10.0 %collective-permute-start.14 = (bf16[4,32,1024]{2,1,0:T(8,128)(2,1)}, bf16[4,32,1024]{2,1,0:T(8,128)(2,1)}, u32[]{:S(2)}, u32[]{:S(2)}) collective-permute-start(bf16[4,32,1024]{2,1,0:T(8,128)(2,1)} %collective-permute-done.13), channel_id=1, source_target_pairs={{0,1},{1,2},{2,3},{3,4},{4,5},{5,6},{6,7},{7,8},{8,9},{9,10},{10,1... | collective-permute-start | bytes 786440 | tf_op jit(solution)/shard_map/ppermute | solution.py:81
  94.0 11.1 %collective-permute-start.15 = (bf16[4,32,1024]{2,1,0:T(8,128)(2,1)}, bf16[4,32,1024]{2,1,0:T(8,128)(2,1)}, u32[]{:S(2)}, u32[]{:S(2)}) collective-permute-start(bf16[4,32,1024]{2,1,0:T(8,128)(2,1)} %collective-permute-done.14), channel_id=1, source_target_pairs={{0,1},{1,2},{2,3},{3,4},{4,5},{5,6},{6,7},{7,8},{8,9},{9,10},{10,1... | collective-permute-start | bytes 786440 | tf_op jit(solution)/shard_map/ppermute | solution.py:81
  96.6 11.1 %collective-permute-start.8 = (bf16[4,32,1024]{2,1,0:T(8,128)(2,1)}, bf16[4,32,1024]{2,1,0:T(8,128)(2,1)}, u32[]{:S(2)}, u32[]{:S(2)}) collective-permute-start(bf16[4,32,1024]{2,1,0:T(8,128)(2,1)} %collective-permute-done.7), channel_id=1, source_target_pairs={{0,15},{1,0},{2,1},{3,2},{4,3},{5,4},{6,5},{7,6},{8,7},{9,8},{10,9... | collective-permute-start | bytes 786440 | tf_op jit(solution)/shard_map/ppermute | solution.py:84
  105.1 12.5 %collective-permute-start.16 = (bf16[4,32,1024]{2,1,0:T(8,128)(2,1)}, bf16[4,32,1024]{2,1,0:T(8,128)(2,1)S(1)}, u32[]{:S(2)}, u32[]{:S(2)}) collective-permute-start(bf16[4,32,1024]{2,1,0:T(8,128)(2,1)} %collective-permute-done.15), channel_id=1, source_target_pairs={{0,1},{1,2},{2,3},{3,4},{4,5},{5,6},{6,7},{7,8},{8,9},{9,10},{10,1... | collective-permute-start | bytes 786440 | tf_op jit(solution)/shard_map/ppermute | solution.py:81
  107.8 13.5 %collective-permute-start.9 = (bf16[4,32,1024]{2,1,0:T(8,128)(2,1)}, bf16[4,32,1024]{2,1,0:T(8,128)(2,1)S(1)}, u32[]{:S(2)}, u32[]{:S(2)}) collective-permute-start(bf16[4,32,1024]{2,1,0:T(8,128)(2,1)} %collective-permute-done.8), channel_id=1, source_target_pairs={{0,15},{1,0},{2,1},{3,2},{4,3},{5,4},{6,5},{7,6},{8,7},{9,8},{10,9... | collective-permute-start | bytes 786440 | tf_op jit(solution)/shard_map/ppermute | solution.py:84
  151.6 94.7 %all-to-all-start.3 = ((bf16[64,10,1024]{2,1,0:T(8,128)(2,1)}), bf16[64,10,1024]{2,1,0:T(8,128)(2,1)S(1)}, u32[]{:S(2)}, u32[]{:S(2)}) async-start(bf16[64,10,1024]{2,1,0:T(8,128)(2,1)} %get-tuple-element.11), calls=%async_computation.3 | async-start | bytes 4194304 | tf_op jit(solution)/shard_map/all_to_all | solution.py:217
  158.5 97.9 %all-gather.4.cloned.1.call-start = ((), (), s32[]{:S(2)}) async-start(), calls=%async_computation.5 | async-start | bytes 1769472 | tf_op jit(solution)/shard_map/all_gather | solution.py:209
  159.2 101.1 %all-gather.8.cloned.1.call-start = ((), (), s32[]{:S(2)}) async-start(), calls=%async_computation.7 | async-start | bytes 1769472 | tf_op jit(solution)/shard_map/all_gather | solution.py:211
  246.3 97.5 %all-to-all-start.1 = ((bf16[64,10,1024]{2,1,0:T(8,128)(2,1)}), bf16[64,10,1024]{2,1,0:T(8,128)(2,1)}, u32[]{:S(2)}, u32[]{:S(2)}) async-start(bf16[64,10,1024]{2,1,0:T(8,128)(2,1)} %get-tuple-element.10), calls=%async_computation.1 | async-start | bytes 4194304 | tf_op jit(solution)/shard_map/all_to_all | solution.py:217
  255.1 33.9 %all-gather.6.cloned.1.call-start = ((), (), s32[]{:S(2)}) async-start(), calls=%async_computation.6 | async-start | bytes 1769472 | tf_op jit(solution)/shard_map/all_gather | solution.py:210
  343.8 98.8 %all-to-all-start.4 = ((bf16[64,10,1024]{2,1,0:T(8,128)(2,1)}), bf16[64,10,1024]{2,1,0:T(8,128)(2,1)S(1)}, u32[]{:S(2)}, u32[]{:S(2)}) async-start(bf16[64,10,1024]{2,1,0:T(8,128)(2,1)} %reshape.403), calls=%async_computation.4 | async-start | bytes 4194304 | tf_op jit(solution)/shard_map/all_to_all | solution.py:228
  442.5 100.7 %all-to-all-start.2 = ((bf16[64,10,1024]{2,1,0:T(8,128)(2,1)}), bf16[64,10,1024]{2,1,0:T(8,128)(2,1)}, u32[]{:S(2)}, u32[]{:S(2)}) async-start(bf16[64,10,1024]{2,1,0:T(8,128)(2,1)} %reshape.401), calls=%async_computation.2 | async-start | bytes 4194304 | tf_op jit(solution)/shard_map/all_to_all | solution.py:228
  (16 other events, 264.1 us)
Sparse Core Ops, SparseCore 0:
  161.4 31.1 all-gather.3
  194.7 32.3 all-gather.7
  258.1 30.9 all-gather.5

commit v4 on v1

--- a/solution.py
+++ b/solution.py
@@ -68,29 +68,34 @@
     ]
 
 
-def ring_gather(block, rows, cols):
+def ring_gather(block, rows, cols, owners):
+    expert_total = rows * cols
     up = lax.ppermute(block, "expert", ring_pairs(rows, cols, 1, 0))
     down = lax.ppermute(block, "expert", ring_pairs(rows, cols, -1, 0))
     up_two = lax.ppermute(up, "expert", ring_pairs(rows, cols, 1, 0))
     by_row = jnp.stack([block, down, up_two, up])
-    relative = {0: by_row}
-    right = by_row
-    left = by_row
+    walk = [
+        (owner * expert_total + src, owner * expert_total + dst)
+        for owner in range(owners)
+        for src, dst in ring_pairs(rows, cols, 0, 1 if owner % 2 == 0 else -1)
+    ]
     half = cols // 2
-    for step in range(1, half + 1):
-        right = lax.ppermute(right, "expert", ring_pairs(rows, cols, 0, 1))
-        relative[-step % cols] = right
-        if step < half:
-            left = lax.ppermute(left, "expert", ring_pairs(rows, cols, 0, -1))
-            relative[step] = left
-    return jnp.stack([relative[k] for k in range(cols)], axis=1)
+    mine = []
+    current = by_row
+    for step in range(half):
+        current = lax.ppermute(current, ("dp", "expert"), walk)
+        mine.append(current)
+    mine = jnp.stack(mine)
+    partner = lax.ppermute(mine[: half - 1], "dp", [(i, i ^ 1) for i in range(owners)])
+    return jnp.concatenate([by_row[None], mine, partner], axis=0)
 
 
 def project_heads(attended, output_weight):
     expert_total = lax.axis_size("expert")
+    owner_total = lax.axis_size("dp")
     cols = 16
     rows = expert_total // cols
-    if rows != 4 or expert_total % cols:
+    if rows != 4 or expert_total % cols or owner_total % 2:
         return jnp.dot(
             attended,
             lax.all_gather(output_weight, "expert", axis=0, tiled=True),
@@ -99,12 +104,19 @@
     own = lax.axis_index("expert")
     own_row = own // cols
     own_col = own % cols
-    gathered = ring_gather(output_weight, rows, cols)
+    sign = 1 - 2 * (lax.axis_index("dp") % 2)
+    half = cols // 2
+    steps = jnp.arange(1, half + 1, dtype=jnp.int32)
+    offsets = jnp.concatenate(
+        [jnp.zeros((1,), jnp.int32), -sign * steps, sign * steps[: half - 1]]
+    )
+    gathered = ring_gather(output_weight, rows, cols, owner_total)
     block = output_weight.shape[0]
     row_order = (own_row + jnp.arange(rows, dtype=jnp.int32)) % rows
-    col_order = (own_col + jnp.arange(cols, dtype=jnp.int32)) % cols
+    col_order = (own_col + offsets) % cols
     split = attended.reshape(attended.shape[0], rows, cols, block)
-    split = jnp.take(jnp.take(split, row_order, axis=1), col_order, axis=2)
+    split = jnp.take(jnp.take(split, col_order, axis=2), row_order, axis=1)
+    split = jnp.swapaxes(split, 1, 2)
     return jnp.dot(
         split.reshape(attended.shape[0], -1),
         gathered.reshape(rows * cols * block, -1),

time: 480 us -> 487 us (1.015)
  waiting for transfers between devices: 290 us -> 338 us
  starting transfers between devices: 88.3 us -> 53.2 us
  local copies, waits for them, and re-layouts: 52.4 us -> 47 us
    ppermute x15 -> x9, starting transfers between devices: 55.1 us -> 17.2 us  [the longest x8 15.3 us: ring_gather(): current = lax.ppermute(current, ('dp', 'expert'), walk)]
    ppermute x15 -> x9, waiting for transfers between devices: 17.3 us -> 47.8 us  [the longest x8 47.8 us: ring_gather(): current = lax.ppermute(current, ('dp', 'expert'), walk)]
    unnamed x45 -> x28, local copies, waits for them, and re-layouts: 17 us -> 7.9 us
    all_to_all x1, waiting for transfers between devices: 134 us -> 143 us  [local(): lax.all_to_all(out_slots, 'expert', split_axis=0, concat_axis=0, tiled=True)]
    all_to_all x1, waiting for transfers between devices: 132 us -> 140 us  [local(): lax.all_to_all(outgoing, 'expert', split_axis=0, concat_axis=0, tiled=True)]
  transfers between devices with their start and end apart: 24 -> 18, of which waited for: 11 -> 11; matrix products, arithmetic and copies ran while one was open for 7% -> 7% of each run, Pallas kernels for 0% -> 0%
where the time goes in v4:
time: 487 us; the launch traced here: 486 us
  waiting for transfers between devices  338 us (69%)
  starting transfers between devices  53.2 us (11%)
  local copies, waits for them, and re-layouts  47 us (10%)
  matrix products  22.1 us (5%)
  between operations  13.8 us (3%)
  other arithmetic  11.6 us (2%)
    all_to_all x1, waiting for transfers between devices, local(): lax.all_to_all(out_slots, 'expert', split_axis=0, concat_axis=0, tiled=True)  143 us
    all_to_all x1, waiting for transfers between devices, local(): lax.all_to_all(outgoing, 'expert', split_axis=0, concat_axis=0, tiled=True)  140 us
    ppermute x8, waiting for transfers between devices, ring_gather(): current = lax.ppermute(current, ('dp', 'expert'), walk)  47.8 us
    ppermute x8, starting transfers between devices, ring_gather(): current = lax.ppermute(current, ('dp', 'expert'), walk)  15.3 us
    gather x8, local copies, waits for them, and re-layouts, local(): flat_back[copy_index[:, route_slot]].astype(jnp.float32)  11.8 us
    all_to_all x1, starting transfers between devices, local(): lax.all_to_all(outgoing, 'expert', split_axis=0, concat_axis=0, tiled=True)  10 us
    dot_general x1, matrix products, hidden_product(): return jnp.dot(active, down_part, preferred_element_type=jnp.float32)  9.99 us
  transfers between devices with their start and end apart: 18, of which 11 were waited for; matrix products, arithmetic and copies ran while one was open for 7% of the time, Pallas kernels for 0%

profile of v4, /device:TPU:6, one launch (start us, length us, event | category | flops | bytes accessed | tf_op | source)
XLA Modules:
  0.0 485.7 jit_solution(16520847314003922759)
XLA Ops:
  6.5 3.5 collective-permute-start.1
  10.0 3.6 collective-permute-start
  20.2 9.3 %all-to-all-start = ((bf16[8,24,3712]{2,1,0:T(8,128)(2,1)}), bf16[8,24,3712]{2,1,0:T(8,128)(2,1)S(1)}, u32[]{:S(2)}, u32[]{:S(2)}) async-start(bf16[8,24,3712]{2,1,0:T(8,128)(2,1)} %bitcast.5), calls=%async_computation | async-start | bytes 2850816 | tf_op jit(solution)/shard_map/all_to_all | solution.py:185
  32.6 5.4 %collective-permute-done.2 = bf16[32,1024]{1,0:T(8,128)(2,1)S(1)} collective-permute-done((bf16[32,1024]{1,0:T(8,128)(2,1)S(1)}, bf16[32,1024]{1,0:T(8,128)(2,1)S(1)}, u32[]{:S(2)}, u32[]{:S(2)}) %collective-permute-start.2) | collective-permute-done | bytes 65568 | tf_op jit(solution)/shard_map/ppermute | solution.py:75
  40.0 9.2 %collective-permute-done.3 = bf16[4,32,1024]{2,1,0:T(8,128)(2,1)S(1)} collective-permute-done((bf16[4,32,1024]{2,1,0:T(8,128)(2,1)S(1)}, bf16[4,32,1024]{2,1,0:T(8,128)(2,1)S(1)}, u32[]{:S(2)}, u32[]{:S(2)}) %collective-permute-start.3) | collective-permute-done | bytes 262176 | tf_op jit(solution)/shard_map/ppermute | solution.py:86
  51.3 7.4 %collective-permute-done.4 = bf16[4,32,1024]{2,1,0:T(8,128)(2,1)S(1)} collective-permute-done((bf16[4,32,1024]{2,1,0:T(8,128)(2,1)S(1)}, bf16[4,32,1024]{2,1,0:T(8,128)(2,1)S(1)}, u32[]{:S(2)}, u32[]{:S(2)}) %collective-permute-start.4) | collective-permute-done | bytes 262176 | tf_op jit(solution)/shard_map/ppermute | solution.py:86
  62.2 6.0 %collective-permute-done.5 = bf16[4,32,1024]{2,1,0:T(8,128)(2,1)S(1)} collective-permute-done((bf16[4,32,1024]{2,1,0:T(8,128)(2,1)S(1)}, bf16[4,32,1024]{2,1,0:T(8,128)(2,1)S(1)}, u32[]{:S(2)}, u32[]{:S(2)}) %collective-permute-start.5) | collective-permute-done | bytes 262176 | tf_op jit(solution)/shard_map/ppermute | solution.py:86
  71.8 5.8 %collective-permute-done.6 = bf16[4,32,1024]{2,1,0:T(8,128)(2,1)S(1)} collective-permute-done((bf16[4,32,1024]{2,1,0:T(8,128)(2,1)S(1)}, bf16[4,32,1024]{2,1,0:T(8,128)(2,1)S(1)}, u32[]{:S(2)}, u32[]{:S(2)}) %collective-permute-start.6) | collective-permute-done | bytes 262176 | tf_op jit(solution)/shard_map/ppermute | solution.py:86
  84.1 3.0 collective-permute-done.7
  90.3 6.4 %collective-permute-done.8 = bf16[4,32,1024]{2,1,0:T(8,128)(2,1)} collective-permute-done((bf16[4,32,1024]{2,1,0:T(8,128)(2,1)S(1)}, bf16[4,32,1024]{2,1,0:T(8,128)(2,1)}, u32[]{:S(2)}, u32[]{:S(2)}) %collective-permute-start.8) | collective-permute-done | bytes 262176 | tf_op jit(solution)/shard_map/ppermute | solution.py:86
  101.3 5.0 %collective-permute-done.9 = bf16[4,32,1024]{2,1,0:T(8,128)(2,1)S(1)} collective-permute-done((bf16[4,32,1024]{2,1,0:T(8,128)(2,1)}, bf16[4,32,1024]{2,1,0:T(8,128)(2,1)S(1)}, u32[]{:S(2)}, u32[]{:S(2)}) %collective-permute-start.9) | collective-permute-done | bytes 262176 | tf_op jit(solution)/shard_map/ppermute | solution.py:86
  115.2 5.0 %collective-permute-done.10 = bf16[4,32,1024]{2,1,0:T(8,128)(2,1)S(1)} collective-permute-done((bf16[4,32,1024]{2,1,0:T(8,128)(2,1)}, bf16[4,32,1024]{2,1,0:T(8,128)(2,1)S(1)}, u32[]{:S(2)}, u32[]{:S(2)}) %collective-permute-start.10) | collective-permute-done | bytes 262176 | tf_op jit(solution)/shard_map/ppermute | solution.py:86
  120.9 3.0 constant_dynamic-update-slice_fusion
  123.9 3.1 multiply_reduce_fusion.1
  127.9 4.3 gather_fusion.4
  134.5 10.0 %all-to-all-start.1 = ((bf16[64,20,1024]{2,1,0:T(8,128)(2,1)}), bf16[64,20,1024]{2,1,0:T(8,128)(2,1)S(1)}, u32[]{:S(2)}, u32[]{:S(2)}) async-start(bf16[64,20,1024]{2,1,0:T(8,128)(2,1)} %reshape.430), calls=%async_computation.1 | async-start | bytes 6291456 | tf_op jit(solution)/shard_map/all_to_all | solution.py:220
  146.8 139.9 %all-to-all-done.1 = bf16[64,20,1024]{2,1,0:T(8,128)(2,1)S(1)} async-done(((bf16[64,20,1024]{2,1,0:T(8,128)(2,1)}), bf16[64,20,1024]{2,1,0:T(8,128)(2,1)S(1)}, u32[]{:S(2)}, u32[]{:S(2)}) %all-to-all-start.1) | async-done | bytes 2621472 | tf_op jit(solution)/shard_map/all_to_all | solution.py:220
  288.9 6.4 %fusion.4 = f32[1280,768]{1,0:T(8,128)} fusion(bf16[1280,1024]{1,0:T(8,128)(2,1)} %reshape.431, bf16[1,768,1024]{2,1,0:T(8,128)(2,1)} %all-gather.4.cloned.1.call-done), kind=kOutput, calls=%fused_computation.19 | convolution fusion | flops 2013265920 | bytes 8126464 | tf_op jit(solution)/shard_map/dot_general | solution.py:129
  295.4 10.0 %convolution_convert_fusion = bf16[1280,1024]{1,0:T(8,128)(2,1)} fusion(bf16[1,768,1024]{2,1,0:T(8,128)(2,1)} %all-gather.8.cloned.1.call-done, bf16[1280,1024]{1,0:T(8,128)(2,1)S(1)} %copy-done.2, f32[1280,768]{1,0:T(8,128)} %fusion.4, bf16[1,768,1024]{2,1,0:T(8,128)(2,1)} %all-gather.6.cloned.1.call-done), kind=kOutput, calls=%fused_computation.15 | convolution fusion | flops 4033740800 | bytes 12320768 | tf_op jit(solution)/shard_map/dot_general | solution.py:132
  305.4 5.2 %reshape.432 = bf16[64,20,1024]{2,1,0:T(8,128)(2,1)} reshape(bf16[1280,1024]{1,0:T(8,128)(2,1)} %convolution_convert_fusion) | data formatting | bytes 5242880 | tf_op jit(solution)/shard_map/reshape | solution.py:229
  310.5 7.4 %all-to-all-start.2 = ((bf16[64,20,1024]{2,1,0:T(8,128)(2,1)}), bf16[64,20,1024]{2,1,0:T(8,128)(2,1)}, u32[]{:S(2)}, u32[]{:S(2)}) async-start(bf16[64,20,1024]{2,1,0:T(8,128)(2,1)} %reshape.432), calls=%async_computation.2 | async-start | bytes 6291456 | tf_op jit(solution)/shard_map/all_to_all | solution.py:230
  318.1 142.9 %all-to-all-done.2 = bf16[64,20,1024]{2,1,0:T(8,128)(2,1)} async-done(((bf16[64,20,1024]{2,1,0:T(8,128)(2,1)}), bf16[64,20,1024]{2,1,0:T(8,128)(2,1)}, u32[]{:S(2)}, u32[]{:S(2)}) %all-to-all-start.2) | async-done | bytes 2621472 | tf_op jit(solution)/shard_map/all_to_all | solution.py:230
  461.1 3.6 reshape.433
  476.5 2.6 add_convert_fusion.1
  (139 shorter events, 63.8 us)
Async XLA Ops:
  6.5 24.1 %collective-permute-start.1 = (bf16[32,1024]{1,0:T(8,128)(2,1)}, bf16[32,1024]{1,0:T(8,128)(2,1)S(1)}, u32[]{:S(2)}, u32[]{:S(2)}) collective-permute-start(bf16[32,1024]{1,0:T(8,128)(2,1)} %param.25), channel_id=1, source_target_pairs={{0,16},{1,17},{2,18},{3,19},{4,20},{5,21},{6,22},{7,23},{8,24},{9,... | collective-permute-start | bytes 196616 | tf_op jit(solution)/shard_map/ppermute | solution.py:73
  10.0 22.6 %collective-permute-start = (bf16[32,1024]{1,0:T(8,128)(2,1)}, bf16[32,1024]{1,0:T(8,128)(2,1)S(1)}, u32[]{:S(2)}, u32[]{:S(2)}) collective-permute-start(bf16[32,1024]{1,0:T(8,128)(2,1)} %param.25), channel_id=1, source_target_pairs={{0,48},{1,49},{2,50},{3,51},{4,52},{5,53},{6,54},{7,55},{8,56},{9,... | collective-permute-start | bytes 196616 | tf_op jit(solution)/shard_map/ppermute | solution.py:74
  19.0 10.7 %copy-start.5 = (s32[128,8]{0,1:T(8,128)S(1)}, s32[128,8]{0,1:T(8,128)}, u32[]{:S(2)}) copy-start(s32[128,8]{0,1:T(8,128)} %param.27) | copy-start | bytes 12292
  19.0 19.0 %copy-start.4 = (bf16[32,1024]{1,0:T(8,128)(2,1)S(1)}, bf16[32,1024]{1,0:T(8,128)(2,1)}, u32[]{:S(2)}) copy-start(bf16[32,1024]{1,0:T(8,128)(2,1)} %param.25) | copy-start | bytes 196612
  20.2 60.2 %all-to-all-start = ((bf16[8,24,3712]{2,1,0:T(8,128)(2,1)}), bf16[8,24,3712]{2,1,0:T(8,128)(2,1)S(1)}, u32[]{:S(2)}, u32[]{:S(2)}) async-start(bf16[8,24,3712]{2,1,0:T(8,128)(2,1)} %bitcast.5), calls=%async_computation | async-start | bytes 2850816 | tf_op jit(solution)/shard_map/all_to_all | solution.py:185
  30.6 7.4 %collective-permute-start.2 = (bf16[32,1024]{1,0:T(8,128)(2,1)S(1)}, bf16[32,1024]{1,0:T(8,128)(2,1)S(1)}, u32[]{:S(2)}, u32[]{:S(2)}) collective-permute-start(bf16[32,1024]{1,0:T(8,128)(2,1)S(1)} %collective-permute-done.1), channel_id=1, source_target_pairs={{0,16},{1,17},{2,18},{3,19},{4,20},{5,21},{6,22},{7,23},{8,24},{9,... | collective-permute-start | bytes 196616 | tf_op jit(solution)/shard_map/ppermute | solution.py:75
  38.0 11.2 %collective-permute-start.3 = (bf16[4,32,1024]{2,1,0:T(8,128)(2,1)S(1)}, bf16[4,32,1024]{2,1,0:T(8,128)(2,1)S(1)}, u32[]{:S(2)}, u32[]{:S(2)}) collective-permute-start(bf16[4,32,1024]{2,1,0:T(8,128)(2,1)S(1)} %pad_maximum_fusion.2), channel_id=1, source_target_pairs={{0,1},{1,2},{2,3},{3,4},{4,5},{5,6},{6,7},{7,8},{8,9},{9,10},{10,1... | collective-permute-start | bytes 786440 | tf_op jit(solution)/shard_map/ppermute | solution.py:86
  49.2 9.5 %collective-permute-start.4 = (bf16[4,32,1024]{2,1,0:T(8,128)(2,1)S(1)}, bf16[4,32,1024]{2,1,0:T(8,128)(2,1)S(1)}, u32[]{:S(2)}, u32[]{:S(2)}) collective-permute-start(bf16[4,32,1024]{2,1,0:T(8,128)(2,1)S(1)} %collective-permute-done.3), channel_id=1, source_target_pairs={{0,1},{1,2},{2,3},{3,4},{4,5},{5,6},{6,7},{7,8},{8,9},{9,10},{10,1... | collective-permute-start | bytes 786440 | tf_op jit(solution)/shard_map/ppermute | solution.py:86
  58.7 9.5 %collective-permute-start.5 = (bf16[4,32,1024]{2,1,0:T(8,128)(2,1)S(1)}, bf16[4,32,1024]{2,1,0:T(8,128)(2,1)S(1)}, u32[]{:S(2)}, u32[]{:S(2)}) collective-permute-start(bf16[4,32,1024]{2,1,0:T(8,128)(2,1)S(1)} %collective-permute-done.4), channel_id=1, source_target_pairs={{0,1},{1,2},{2,3},{3,4},{4,5},{5,6},{6,7},{7,8},{8,9},{9,10},{10,1... | collective-permute-start | bytes 786440 | tf_op jit(solution)/shard_map/ppermute | solution.py:86
  68.2 9.5 %collective-permute-start.6 = (bf16[4,32,1024]{2,1,0:T(8,128)(2,1)S(1)}, bf16[4,32,1024]{2,1,0:T(8,128)(2,1)S(1)}, u32[]{:S(2)}, u32[]{:S(2)}) collective-permute-start(bf16[4,32,1024]{2,1,0:T(8,128)(2,1)S(1)} %collective-permute-done.5), channel_id=1, source_target_pairs={{0,1},{1,2},{2,3},{3,4},{4,5},{5,6},{6,7},{7,8},{8,9},{9,10},{10,1... | collective-permute-start | bytes 786440 | tf_op jit(solution)/shard_map/ppermute | solution.py:86
  77.6 9.5 %collective-permute-start.7 = (bf16[4,32,1024]{2,1,0:T(8,128)(2,1)S(1)}, bf16[4,32,1024]{2,1,0:T(8,128)(2,1)S(1)}, u32[]{:S(2)}, u32[]{:S(2)}) collective-permute-start(bf16[4,32,1024]{2,1,0:T(8,128)(2,1)S(1)} %collective-permute-done.6), channel_id=1, source_target_pairs={{0,1},{1,2},{2,3},{3,4},{4,5},{5,6},{6,7},{7,8},{8,9},{9,10},{10,1... | collective-permute-start | bytes 786440 | tf_op jit(solution)/shard_map/ppermute | solution.py:86
  84.1 25.1 %copy-start.9 = (f32[128]{0:T(128)S(1)}, f32[128]{0:T(128)}, u32[]{:S(2)}) copy-start(f32[128]{0:T(128)} %param.24) | copy-start | bytes 1540
  87.1 9.6 %collective-permute-start.8 = (bf16[4,32,1024]{2,1,0:T(8,128)(2,1)S(1)}, bf16[4,32,1024]{2,1,0:T(8,128)(2,1)}, u32[]{:S(2)}, u32[]{:S(2)}) collective-permute-start(bf16[4,32,1024]{2,1,0:T(8,128)(2,1)S(1)} %collective-permute-done.7), channel_id=1, source_target_pairs={{0,1},{1,2},{2,3},{3,4},{4,5},{5,6},{6,7},{7,8},{8,9},{9,10},{10,1... | collective-permute-start | bytes 786440 | tf_op jit(solution)/shard_map/ppermute | solution.py:86
  96.7 9.7 %collective-permute-start.9 = (bf16[4,32,1024]{2,1,0:T(8,128)(2,1)}, bf16[4,32,1024]{2,1,0:T(8,128)(2,1)S(1)}, u32[]{:S(2)}, u32[]{:S(2)}) collective-permute-start(bf16[4,32,1024]{2,1,0:T(8,128)(2,1)} %collective-permute-done.8), channel_id=1, source_target_pairs={{0,1},{1,2},{2,3},{3,4},{4,5},{5,6},{6,7},{7,8},{8,9},{9,10},{10,1... | collective-permute-start | bytes 786440 | tf_op jit(solution)/shard_map/ppermute | solution.py:86
  107.2 13.7 %collective-permute-start.11 = (bf16[7,4,32,1024]{3,2,1,0:T(8,128)(2,1)}, bf16[7,4,32,1024]{3,2,1,0:T(8,128)(2,1)}, u32[]{:S(2)}, u32[]{:S(2)}) collective-permute-start(bf16[7,4,32,1024]{3,2,1,0:T(8,128)(2,1)} %get-tuple-element.16), channel_id=1, source_target_pairs={{0,64},{64,0},{128,192},{192,128},{256,320},{320,256},{384,448},{4... | collective-permute-start | bytes 5505032 | tf_op jit(solution)/shard_map/ppermute | solution.py:89
  110.5 9.7 %collective-permute-start.10 = (bf16[4,32,1024]{2,1,0:T(8,128)(2,1)}, bf16[4,32,1024]{2,1,0:T(8,128)(2,1)S(1)}, u32[]{:S(2)}, u32[]{:S(2)}) collective-permute-start(bf16[4,32,1024]{2,1,0:T(8,128)(2,1)} %copy-done.3), channel_id=1, source_target_pairs={{0,1},{1,2},{2,3},{3,4},{4,5},{5,6},{6,7},{7,8},{8,9},{9,10},{10,1... | collective-permute-start | bytes 786440 | tf_op jit(solution)/shard_map/ppermute | solution.py:86
  123.9 3.9 copy-start.7
  134.5 152.1 %all-to-all-start.1 = ((bf16[64,20,1024]{2,1,0:T(8,128)(2,1)}), bf16[64,20,1024]{2,1,0:T(8,128)(2,1)S(1)}, u32[]{:S(2)}, u32[]{:S(2)}) async-start(bf16[64,20,1024]{2,1,0:T(8,128)(2,1)} %reshape.430), calls=%async_computation.1 | async-start | bytes 6291456 | tf_op jit(solution)/shard_map/all_to_all | solution.py:220
  144.6 144.3 %all-gather.4.cloned.1.call-start = ((), (), s32[]{:S(2)}) async-start(), calls=%async_computation.3 | async-start | bytes 1769472 | tf_op jit(solution)/shard_map/all_gather | solution.py:223
  145.3 150.0 %all-gather.8.cloned.1.call-start = ((), (), s32[]{:S(2)}) async-start(), calls=%async_computation.5 | async-start | bytes 1769472 | tf_op jit(solution)/shard_map/all_gather | solution.py:225
  146.1 149.3 %all-gather.6.cloned.1.call-start = ((), (), s32[]{:S(2)}) async-start(), calls=%async_computation.4 | async-start | bytes 1769472 | tf_op jit(solution)/shard_map/all_gather | solution.py:224
  288.9 6.5 %copy-start.2 = (bf16[1280,1024]{1,0:T(8,128)(2,1)S(1)}, bf16[1280,1024]{1,0:T(8,128)(2,1)}, u32[]{:S(2)}) copy-start(bf16[1280,1024]{1,0:T(8,128)(2,1)} %reshape.431) | copy-start | bytes 7864324
  310.5 7.4 %copy-start.6 = (f32[128,8]{0,1:T(8,128)S(1)}, f32[128,8]{0,1:T(8,128)}, u32[]{:S(2)}) copy-start(f32[128,8]{0,1:T(8,128)} %param.28) | copy-start | bytes 12292
  310.5 150.5 %all-to-all-start.2 = ((bf16[64,20,1024]{2,1,0:T(8,128)(2,1)}), bf16[64,20,1024]{2,1,0:T(8,128)(2,1)}, u32[]{:S(2)}, u32[]{:S(2)}) async-start(bf16[64,20,1024]{2,1,0:T(8,128)(2,1)} %reshape.432), calls=%async_computation.2 | async-start | bytes 6291456 | tf_op jit(solution)/shard_map/all_to_all | solution.py:230
  (4 other events, 8.0 us)
Sparse Core Ops, SparseCore 0:
  147.5 31.2 all-gather.3
  180.9 32.2 all-gather.7
  215.4 32.3 all-gather.5

commit v5 on v4

--- a/solution.py
+++ b/solution.py
@@ -215,7 +215,12 @@
     place_ids = jnp.arange(most, dtype=jnp.int32)
     hits = ranked.T[:, :, None] == place_ids[None, None, :]
     source_token = jnp.sum(jnp.where(hits, pack_ids[None, :, None], 0), axis=1)
-    outgoing = normed[source_token.reshape(-1)].reshape(expert_total, most, -1)
+    picks = jnp.transpose(hits, (0, 2, 1)).reshape(-1, row_total).astype(jnp.bfloat16)
+    outgoing = (
+        jnp.dot(picks, normed, preferred_element_type=jnp.float32)
+        .astype(jnp.bfloat16)
+        .reshape(expert_total, most, -1)
+    )
     total_rows = expert_total * most
     received = lax.all_to_all(outgoing, "expert", split_axis=0, concat_axis=0, tiled=True)
     work_rows = received.reshape(total_rows, -1)
@@ -232,11 +237,17 @@
     copy_rank = jnp.sum(jnp.where(routed, rank[:, None, :], 0), axis=2)
     copy_index = routes * most + copy_rank
     gates = route_weight / jnp.sum(route_weight, axis=1, keepdims=True)
+    slot_ids_back = jnp.arange(total_rows, dtype=jnp.int32)
+    spread = jnp.sum(
+        jnp.where(copy_index[:, :, None] == slot_ids_back[None, None, :], gates[:, :, None], 0.0),
+        axis=1,
+    )
     mixture = jnp.zeros(hidden_state.shape, jnp.float32)
-    for route_slot in range(top_total):
-        mixture = mixture + gates[:, route_slot : route_slot + 1] * flat_back[
-            copy_index[:, route_slot]
-        ].astype(jnp.float32)
+    for _ in range(3):
+        leading = lax.reduce_precision(spread, exponent_bits=8, mantissa_bits=7)
+        spread = spread - leading
+        part = leading.astype(jnp.bfloat16)
+        mixture = mixture + jnp.dot(part, flat_back, preferred_element_type=jnp.float32)
     return (hidden_state + mixture).astype(jnp.bfloat16)
 
 

time: 487 us -> 474 us (0.973)
  local copies, waits for them, and re-layouts: 47 us -> 35.8 us
  waiting for transfers between devices: 338 us -> 332 us
  matrix products: 22.1 us -> 27.3 us
    gather x9 -> x0, local copies, waits for them, and re-layouts: 16.1 us -> none  [the longest x8 11.8 us: local(): flat_back[copy_index[:, route_slot]].astype(jnp.float32)]
    unnamed x28 -> x30, local copies, waits for them, and re-layouts: 7.9 us -> 12.2 us
  transfers between devices with their start and end apart: 18 -> 18, of which waited for: 11 -> 11; matrix products, arithmetic and copies ran while one was open for 7% -> 9% of each run, Pallas kernels for 0% -> 0%
where the time goes in v5:
time: 474 us; the launch traced here: 473 us
  waiting for transfers between devices  332 us (70%)
  starting transfers between devices  53.2 us (11%)
  local copies, waits for them, and re-layouts  35.8 us (8%)
  matrix products  27.3 us (6%)
  between operations  13.8 us (3%)
  other arithmetic  10.8 us (2%)
    all_to_all x1, waiting for transfers between devices, local(): lax.all_to_all(out_slots, 'expert', split_axis=0, concat_axis=0, tiled=True)  141 us
    all_to_all x1, waiting for transfers between devices, local(): lax.all_to_all(outgoing, 'expert', split_axis=0, concat_axis=0, tiled=True)  140 us
    ppermute x8, waiting for transfers between devices, ring_gather(): current = lax.ppermute(current, ('dp', 'expert'), walk)  43.5 us
    ppermute x8, starting transfers between devices, ring_gather(): current = lax.ppermute(current, ('dp', 'expert'), walk)  15.3 us
    unnamed x30, local copies, waits for them, and re-layouts  12.2 us
    all_to_all x1, starting transfers between devices, local(): lax.all_to_all(outgoing, 'expert', split_axis=0, concat_axis=0, tiled=True)  10 us
    dot_general x1, matrix products, hidden_product(): return jnp.dot(active, down_part, preferred_element_type=jnp.float32)  10 us
  transfers between devices with their start and end apart: 18, of which 11 were waited for; matrix products, arithmetic and copies ran while one was open for 9% of the time, Pallas kernels for 0%

profile of v5, /device:TPU:6, one launch (start us, length us, event | category | flops | bytes accessed | tf_op | source)
XLA Modules:
  0.0 472.8 jit_solution(17522187536323192893)
XLA Ops:
  6.5 3.5 collective-permute-start.1
  10.0 3.6 collective-permute-start
  20.2 9.3 %all-to-all-start = ((bf16[8,24,3712]{2,1,0:T(8,128)(2,1)}), bf16[8,24,3712]{2,1,0:T(8,128)(2,1)S(1)}, u32[]{:S(2)}, u32[]{:S(2)}) async-start(bf16[8,24,3712]{2,1,0:T(8,128)(2,1)} %bitcast.5), calls=%async_computation | async-start | bytes 2850816 | tf_op jit(solution)/shard_map/all_to_all | solution.py:185
  31.9 5.4 %collective-permute-done.2 = bf16[32,1024]{1,0:T(8,128)(2,1)S(1)} collective-permute-done((bf16[32,1024]{1,0:T(8,128)(2,1)S(1)}, bf16[32,1024]{1,0:T(8,128)(2,1)S(1)}, u32[]{:S(2)}, u32[]{:S(2)}) %collective-permute-start.2) | collective-permute-done | bytes 65568 | tf_op jit(solution)/shard_map/ppermute | solution.py:75
  39.3 9.2 %collective-permute-done.3 = bf16[4,32,1024]{2,1,0:T(8,128)(2,1)S(1)} collective-permute-done((bf16[4,32,1024]{2,1,0:T(8,128)(2,1)S(1)}, bf16[4,32,1024]{2,1,0:T(8,128)(2,1)S(1)}, u32[]{:S(2)}, u32[]{:S(2)}) %collective-permute-start.3) | collective-permute-done | bytes 262176 | tf_op jit(solution)/shard_map/ppermute | solution.py:86
  50.9 7.2 %collective-permute-done.4 = bf16[4,32,1024]{2,1,0:T(8,128)(2,1)} collective-permute-done((bf16[4,32,1024]{2,1,0:T(8,128)(2,1)S(1)}, bf16[4,32,1024]{2,1,0:T(8,128)(2,1)}, u32[]{:S(2)}, u32[]{:S(2)}) %collective-permute-start.4) | collective-permute-done | bytes 262176 | tf_op jit(solution)/shard_map/ppermute | solution.py:86
  61.6 6.2 %collective-permute-done.5 = bf16[4,32,1024]{2,1,0:T(8,128)(2,1)S(1)} collective-permute-done((bf16[4,32,1024]{2,1,0:T(8,128)(2,1)}, bf16[4,32,1024]{2,1,0:T(8,128)(2,1)S(1)}, u32[]{:S(2)}, u32[]{:S(2)}) %collective-permute-start.5) | collective-permute-done | bytes 262176 | tf_op jit(solution)/shard_map/ppermute | solution.py:86
  72.4 5.0 %collective-permute-done.6 = bf16[4,32,1024]{2,1,0:T(8,128)(2,1)} collective-permute-done((bf16[4,32,1024]{2,1,0:T(8,128)(2,1)S(1)}, bf16[4,32,1024]{2,1,0:T(8,128)(2,1)}, u32[]{:S(2)}, u32[]{:S(2)}) %collective-permute-start.6) | collective-permute-done | bytes 262176 | tf_op jit(solution)/shard_map/ppermute | solution.py:86
  90.8 6.2 %collective-permute-done.8 = bf16[4,32,1024]{2,1,0:T(8,128)(2,1)} collective-permute-done((bf16[4,32,1024]{2,1,0:T(8,128)(2,1)}, bf16[4,32,1024]{2,1,0:T(8,128)(2,1)}, u32[]{:S(2)}, u32[]{:S(2)}) %collective-permute-start.8) | collective-permute-done | bytes 262176 | tf_op jit(solution)/shard_map/ppermute | solution.py:86
  102.5 4.1 collective-permute-done.9
  113.8 2.1 convolution_convert_fusion.2
  117.4 4.0 collective-permute-done.10
  123.1 3.0 constant_dynamic-update-slice_fusion
  126.1 3.1 multiply_reduce_fusion.1
  130.9 2.3 reshape.403
  133.2 10.0 %all-to-all-start.1 = ((bf16[64,20,1024]{2,1,0:T(8,128)(2,1)}), bf16[64,20,1024]{2,1,0:T(8,128)(2,1)S(1)}, u32[]{:S(2)}, u32[]{:S(2)}) async-start(bf16[64,20,1024]{2,1,0:T(8,128)(2,1)} %reshape.403), calls=%async_computation.1 | async-start | bytes 6291456 | tf_op jit(solution)/shard_map/all_to_all | solution.py:225
  145.5 139.9 %all-to-all-done.1 = bf16[64,20,1024]{2,1,0:T(8,128)(2,1)S(1)} async-done(((bf16[64,20,1024]{2,1,0:T(8,128)(2,1)}), bf16[64,20,1024]{2,1,0:T(8,128)(2,1)S(1)}, u32[]{:S(2)}, u32[]{:S(2)}) %all-to-all-start.1) | async-done | bytes 2621472 | tf_op jit(solution)/shard_map/all_to_all | solution.py:225
  285.4 2.2 reshape.404
  287.6 6.5 %fusion.4 = f32[1280,768]{1,0:T(8,128)} fusion(bf16[1280,1024]{1,0:T(8,128)(2,1)} %reshape.404, bf16[1,768,1024]{2,1,0:T(8,128)(2,1)} %all-gather.4.cloned.1.call-done), kind=kOutput, calls=%fused_computation.13 | convolution fusion | flops 2013265920 | bytes 8126464 | tf_op jit(solution)/shard_map/dot_general | solution.py:129
  294.1 10.0 %convolution_convert_fusion = bf16[1280,1024]{1,0:T(8,128)(2,1)} fusion(bf16[1,768,1024]{2,1,0:T(8,128)(2,1)} %all-gather.8.cloned.1.call-done, bf16[1280,1024]{1,0:T(8,128)(2,1)S(1)} %copy-done.2, f32[1280,768]{1,0:T(8,128)} %fusion.4, bf16[1,768,1024]{2,1,0:T(8,128)(2,1)} %all-gather.6.cloned.1.call-done), kind=kOutput, calls=%fused_computation.8 | convolution fusion | flops 4033740800 | bytes 12320768 | tf_op jit(solution)/shard_map/dot_general | solution.py:132
  304.1 5.2 %reshape.405 = bf16[64,20,1024]{2,1,0:T(8,128)(2,1)} reshape(bf16[1280,1024]{1,0:T(8,128)(2,1)} %convolution_convert_fusion) | data formatting | bytes 5242880 | tf_op jit(solution)/shard_map/reshape | solution.py:234
  309.3 7.4 %all-to-all-start.2 = ((bf16[64,20,1024]{2,1,0:T(8,128)(2,1)}), bf16[64,20,1024]{2,1,0:T(8,128)(2,1)}, u32[]{:S(2)}, u32[]{:S(2)}) async-start(bf16[64,20,1024]{2,1,0:T(8,128)(2,1)} %reshape.405), calls=%async_computation.2 | async-start | bytes 6291456 | tf_op jit(solution)/shard_map/all_to_all | solution.py:235
  318.6 141.2 %all-to-all-done.2 = bf16[64,20,1024]{2,1,0:T(8,128)(2,1)} async-done(((bf16[64,20,1024]{2,1,0:T(8,128)(2,1)}), bf16[64,20,1024]{2,1,0:T(8,128)(2,1)}, u32[]{:S(2)}, u32[]{:S(2)}) %all-to-all-start.2) | async-done | bytes 2621472 | tf_op jit(solution)/shard_map/all_to_all | solution.py:235
  459.8 3.6 reshape.406
  (130 shorter events, 58.7 us)
Async XLA Ops:
  6.5 23.4 %collective-permute-start.1 = (bf16[32,1024]{1,0:T(8,128)(2,1)}, bf16[32,1024]{1,0:T(8,128)(2,1)S(1)}, u32[]{:S(2)}, u32[]{:S(2)}) collective-permute-start(bf16[32,1024]{1,0:T(8,128)(2,1)} %param.25), channel_id=1, source_target_pairs={{0,16},{1,17},{2,18},{3,19},{4,20},{5,21},{6,22},{7,23},{8,24},{9,... | collective-permute-start | bytes 196616 | tf_op jit(solution)/shard_map/ppermute | solution.py:73
  10.0 21.9 %collective-permute-start = (bf16[32,1024]{1,0:T(8,128)(2,1)}, bf16[32,1024]{1,0:T(8,128)(2,1)S(1)}, u32[]{:S(2)}, u32[]{:S(2)}) collective-permute-start(bf16[32,1024]{1,0:T(8,128)(2,1)} %param.25), channel_id=1, source_target_pairs={{0,48},{1,49},{2,50},{3,51},{4,52},{5,53},{6,54},{7,55},{8,56},{9,... | collective-permute-start | bytes 196616 | tf_op jit(solution)/shard_map/ppermute | solution.py:74
  19.0 10.7 %copy-start.6 = (s32[128,8]{0,1:T(8,128)S(1)}, s32[128,8]{0,1:T(8,128)}, u32[]{:S(2)}) copy-start(s32[128,8]{0,1:T(8,128)} %param.27) | copy-start | bytes 12292
  19.0 18.3 %copy-start.5 = (bf16[32,1024]{1,0:T(8,128)(2,1)S(1)}, bf16[32,1024]{1,0:T(8,128)(2,1)}, u32[]{:S(2)}) copy-start(bf16[32,1024]{1,0:T(8,128)(2,1)} %param.25) | copy-start | bytes 196612
  20.2 60.9 %all-to-all-start = ((bf16[8,24,3712]{2,1,0:T(8,128)(2,1)}), bf16[8,24,3712]{2,1,0:T(8,128)(2,1)S(1)}, u32[]{:S(2)}, u32[]{:S(2)}) async-start(bf16[8,24,3712]{2,1,0:T(8,128)(2,1)} %bitcast.5), calls=%async_computation | async-start | bytes 2850816 | tf_op jit(solution)/shard_map/all_to_all | solution.py:185
  29.9 7.4 %collective-permute-start.2 = (bf16[32,1024]{1,0:T(8,128)(2,1)S(1)}, bf16[32,1024]{1,0:T(8,128)(2,1)S(1)}, u32[]{:S(2)}, u32[]{:S(2)}) collective-permute-start(bf16[32,1024]{1,0:T(8,128)(2,1)S(1)} %collective-permute-done.1), channel_id=1, source_target_pairs={{0,16},{1,17},{2,18},{3,19},{4,20},{5,21},{6,22},{7,23},{8,24},{9,... | collective-permute-start | bytes 196616 | tf_op jit(solution)/shard_map/ppermute | solution.py:75
  37.4 11.2 %collective-permute-start.3 = (bf16[4,32,1024]{2,1,0:T(8,128)(2,1)S(1)}, bf16[4,32,1024]{2,1,0:T(8,128)(2,1)S(1)}, u32[]{:S(2)}, u32[]{:S(2)}) collective-permute-start(bf16[4,32,1024]{2,1,0:T(8,128)(2,1)S(1)} %pad_maximum_fusion.2), channel_id=1, source_target_pairs={{0,1},{1,2},{2,3},{3,4},{4,5},{5,6},{6,7},{7,8},{8,9},{9,10},{10,1... | collective-permute-start | bytes 786440 | tf_op jit(solution)/shard_map/ppermute | solution.py:86
  48.5 9.6 %collective-permute-start.4 = (bf16[4,32,1024]{2,1,0:T(8,128)(2,1)S(1)}, bf16[4,32,1024]{2,1,0:T(8,128)(2,1)}, u32[]{:S(2)}, u32[]{:S(2)}) collective-permute-start(bf16[4,32,1024]{2,1,0:T(8,128)(2,1)S(1)} %collective-permute-done.3), channel_id=1, source_target_pairs={{0,1},{1,2},{2,3},{3,4},{4,5},{5,6},{6,7},{7,8},{8,9},{9,10},{10,1... | collective-permute-start | bytes 786440 | tf_op jit(solution)/shard_map/ppermute | solution.py:86
  58.1 9.7 %collective-permute-start.5 = (bf16[4,32,1024]{2,1,0:T(8,128)(2,1)}, bf16[4,32,1024]{2,1,0:T(8,128)(2,1)S(1)}, u32[]{:S(2)}, u32[]{:S(2)}) collective-permute-start(bf16[4,32,1024]{2,1,0:T(8,128)(2,1)} %collective-permute-done.4), channel_id=1, source_target_pairs={{0,1},{1,2},{2,3},{3,4},{4,5},{5,6},{6,7},{7,8},{8,9},{9,10},{10,1... | collective-permute-start | bytes 786440 | tf_op jit(solution)/shard_map/ppermute | solution.py:86
  67.8 9.6 %collective-permute-start.6 = (bf16[4,32,1024]{2,1,0:T(8,128)(2,1)S(1)}, bf16[4,32,1024]{2,1,0:T(8,128)(2,1)}, u32[]{:S(2)}, u32[]{:S(2)}) collective-permute-start(bf16[4,32,1024]{2,1,0:T(8,128)(2,1)S(1)} %collective-permute-done.5), channel_id=1, source_target_pairs={{0,1},{1,2},{2,3},{3,4},{4,5},{5,6},{6,7},{7,8},{8,9},{9,10},{10,1... | collective-permute-start | bytes 786440 | tf_op jit(solution)/shard_map/ppermute | solution.py:86
  77.4 9.8 %collective-permute-start.7 = (bf16[4,32,1024]{2,1,0:T(8,128)(2,1)}, bf16[4,32,1024]{2,1,0:T(8,128)(2,1)}, u32[]{:S(2)}, u32[]{:S(2)}) collective-permute-start(bf16[4,32,1024]{2,1,0:T(8,128)(2,1)} %collective-permute-done.6), channel_id=1, source_target_pairs={{0,1},{1,2},{2,3},{3,4},{4,5},{5,6},{6,7},{7,8},{8,9},{9,10},{10,1... | collective-permute-start | bytes 786440 | tf_op jit(solution)/shard_map/ppermute | solution.py:86
  85.6 23.8 %copy-start.10 = (f32[128]{0:T(128)S(1)}, f32[128]{0:T(128)}, u32[]{:S(2)}) copy-start(f32[128]{0:T(128)} %param.24) | copy-start | bytes 1540
  87.1 9.8 %collective-permute-start.8 = (bf16[4,32,1024]{2,1,0:T(8,128)(2,1)}, bf16[4,32,1024]{2,1,0:T(8,128)(2,1)}, u32[]{:S(2)}, u32[]{:S(2)}) collective-permute-start(bf16[4,32,1024]{2,1,0:T(8,128)(2,1)} %collective-permute-done.7), channel_id=1, source_target_pairs={{0,1},{1,2},{2,3},{3,4},{4,5},{5,6},{6,7},{7,8},{8,9},{9,10},{10,1... | collective-permute-start | bytes 786440 | tf_op jit(solution)/shard_map/ppermute | solution.py:86
  96.9 9.7 %collective-permute-start.9 = (bf16[4,32,1024]{2,1,0:T(8,128)(2,1)}, bf16[4,32,1024]{2,1,0:T(8,128)(2,1)S(1)}, u32[]{:S(2)}, u32[]{:S(2)}) collective-permute-start(bf16[4,32,1024]{2,1,0:T(8,128)(2,1)} %collective-permute-done.8), channel_id=1, source_target_pairs={{0,1},{1,2},{2,3},{3,4},{4,5},{5,6},{6,7},{7,8},{8,9},{9,10},{10,1... | collective-permute-start | bytes 786440 | tf_op jit(solution)/shard_map/ppermute | solution.py:86
  107.5 15.6 %collective-permute-start.11 = (bf16[7,4,32,1024]{3,2,1,0:T(8,128)(2,1)}, bf16[7,4,32,1024]{3,2,1,0:T(8,128)(2,1)}, u32[]{:S(2)}, u32[]{:S(2)}) collective-permute-start(bf16[7,4,32,1024]{3,2,1,0:T(8,128)(2,1)} %get-tuple-element.16), channel_id=1, source_target_pairs={{0,64},{64,0},{128,192},{192,128},{256,320},{320,256},{384,448},{4... | collective-permute-start | bytes 5505032 | tf_op jit(solution)/shard_map/ppermute | solution.py:89
  111.9 9.6 %collective-permute-start.10 = (bf16[4,32,1024]{2,1,0:T(8,128)(2,1)S(1)}, bf16[4,32,1024]{2,1,0:T(8,128)(2,1)}, u32[]{:S(2)}, u32[]{:S(2)}) collective-permute-start(bf16[4,32,1024]{2,1,0:T(8,128)(2,1)S(1)} %copy-done.4), channel_id=1, source_target_pairs={{0,1},{1,2},{2,3},{3,4},{4,5},{5,6},{6,7},{7,8},{8,9},{9,10},{10,1... | collective-permute-start | bytes 786440 | tf_op jit(solution)/shard_map/ppermute | solution.py:86
  126.1 3.9 copy-start.8
  133.2 152.1 %all-to-all-start.1 = ((bf16[64,20,1024]{2,1,0:T(8,128)(2,1)}), bf16[64,20,1024]{2,1,0:T(8,128)(2,1)S(1)}, u32[]{:S(2)}, u32[]{:S(2)}) async-start(bf16[64,20,1024]{2,1,0:T(8,128)(2,1)} %reshape.403), calls=%async_computation.1 | async-start | bytes 6291456 | tf_op jit(solution)/shard_map/all_to_all | solution.py:225
  143.3 144.3 %all-gather.4.cloned.1.call-start = ((), (), s32[]{:S(2)}) async-start(), calls=%async_computation.3 | async-start | bytes 1769472 | tf_op jit(solution)/shard_map/all_gather | solution.py:228
  144.0 150.1 %all-gather.8.cloned.1.call-start = ((), (), s32[]{:S(2)}) async-start(), calls=%async_computation.5 | async-start | bytes 1769472 | tf_op jit(solution)/shard_map/all_gather | solution.py:230
  144.8 149.3 %all-gather.6.cloned.1.call-start = ((), (), s32[]{:S(2)}) async-start(), calls=%async_computation.4 | async-start | bytes 1769472 | tf_op jit(solution)/shard_map/all_gather | solution.py:229
  287.6 6.5 %copy-start.2 = (bf16[1280,1024]{1,0:T(8,128)(2,1)S(1)}, bf16[1280,1024]{1,0:T(8,128)(2,1)}, u32[]{:S(2)}) copy-start(bf16[1280,1024]{1,0:T(8,128)(2,1)} %reshape.404) | copy-start | bytes 7864324
  309.3 7.4 %copy-start.7 = (f32[128,8]{0,1:T(8,128)S(1)}, f32[128,8]{0,1:T(8,128)}, u32[]{:S(2)}) copy-start(f32[128,8]{0,1:T(8,128)} %param.28) | copy-start | bytes 12292
  309.3 150.5 %all-to-all-start.2 = ((bf16[64,20,1024]{2,1,0:T(8,128)(2,1)}), bf16[64,20,1024]{2,1,0:T(8,128)(2,1)}, u32[]{:S(2)}, u32[]{:S(2)}) async-start(bf16[64,20,1024]{2,1,0:T(8,128)(2,1)} %reshape.405), calls=%async_computation.2 | async-start | bytes 6291456 | tf_op jit(solution)/shard_map/all_to_all | solution.py:235
  (5 other events, 8.1 us)
Sparse Core Ops, SparseCore 0:
  146.2 31.2 all-gather.3
  179.6 32.2 all-gather.7
  214.0 32.3 all-gather.5

commit v6 on v5

--- a/solution.py
+++ b/solution.py
@@ -202,6 +202,14 @@
     identity = slot_of // capacity
     position = slot_of % capacity
     attended = attend(pack_query, pack_key, pack_value, identity, position, query_gain, key_gain)
+    gate_whole, up_whole, down_whole = (
+        lax.all_gather(gate_weight, "dp", axis=1, tiled=True),
+        lax.all_gather(up_weight, "dp", axis=1, tiled=True),
+        lax.all_gather(down_weight, "dp", axis=1, tiled=True),
+    )
+    attended, gate_whole, up_whole, down_whole = lax.optimization_barrier(
+        (attended, gate_whole, up_whole, down_whole)
+    )
     hidden_state = pack_residual.astype(jnp.float32) + project_heads(attended, output_weight)
     normed = rms_scale(hidden_state, post_gain).astype(jnp.bfloat16)
     top_total = routes.shape[1]
@@ -224,11 +232,6 @@
     total_rows = expert_total * most
     received = lax.all_to_all(outgoing, "expert", split_axis=0, concat_axis=0, tiled=True)
     work_rows = received.reshape(total_rows, -1)
-    gate_whole, up_whole, down_whole = (
-        lax.all_gather(gate_weight, "dp", axis=1, tiled=True),
-        lax.all_gather(up_weight, "dp", axis=1, tiled=True),
-        lax.all_gather(down_weight, "dp", axis=1, tiled=True),
-    )
     produced = expert_output(work_rows, gate_whole[0], up_whole[0], down_whole[0])
     produced = produced.astype(jnp.bfloat16)
     out_slots = produced.reshape(expert_total, most, -1)

time: 474 us -> 482 us (1.017)
  blocking collectives: 0 us -> 154 us
  waiting for transfers between devices: 332 us -> 192 us
  starting transfers between devices: 53.2 us -> 42.5 us
    all_to_all x0 -> x1, blocking collectives: none -> 154 us  [local(): lax.all_to_all(outgoing, 'expert', split_axis=0, concat_axis=0, tiled=True)]
    all_to_all x1 -> x0, waiting for transfers between devices: 140 us -> none  [local(): lax.all_to_all(outgoing, 'expert', split_axis=0, concat_axis=0, tiled=True)]
    all_to_all x1 -> x0, starting transfers between devices: 10 us -> none  [local(): lax.all_to_all(outgoing, 'expert', split_axis=0, concat_axis=0, tiled=True)]
    unnamed x30 -> x44, local copies, waits for them, and re-layouts: 12.2 us -> 10.3 us
  transfers between devices with their start and end apart: 18 -> 17, of which waited for: 11 -> 10; matrix products, arithmetic and copies ran while one was open for 9% -> 7% of each run, Pallas kernels for 0% -> 0%
where the time goes in v6:
time: 482 us; the launch traced here: 480 us
  waiting for transfers between devices  192 us (40%)
  blocking collectives  154 us (32%)
  starting transfers between devices  42.5 us (9%)
  local copies, waits for them, and re-layouts  36.3 us (8%)
  matrix products  27.7 us (6%)
  between operations  13.8 us (3%)
  other arithmetic  13.1 us (3%)
    all_to_all x1, blocking collectives, local(): lax.all_to_all(outgoing, 'expert', split_axis=0, concat_axis=0, tiled=True)  154 us
    all_to_all x1, waiting for transfers between devices, local(): lax.all_to_all(out_slots, 'expert', split_axis=0, concat_axis=0, tiled=True)  142 us
    ppermute x8, waiting for transfers between devices, ring_gather(): current = lax.ppermute(current, ('dp', 'expert'), walk)  43.1 us
    ppermute x8, starting transfers between devices, ring_gather(): current = lax.ppermute(current, ('dp', 'expert'), walk)  15.3 us
    unnamed x44, local copies, waits for them, and re-layouts  10.3 us
    dot_general x1, matrix products, hidden_product(): return jnp.dot(active, down_part, preferred_element_type=jnp.float32)  10 us
  transfers between devices with their start and end apart: 17, of which 10 were waited for; matrix products, arithmetic and copies ran while one was open for 7% of the time, Pallas kernels for 0%

profile of v6, /device:TPU:6, one launch (start us, length us, event | category | flops | bytes accessed | tf_op | source)
XLA Modules:
  0.0 479.6 jit_solution(8250339098505976771)
XLA Ops:
  8.0 3.5 collective-permute-start.1
  11.5 3.6 collective-permute-start
  21.7 9.3 %all-to-all-start = ((bf16[8,24,3712]{2,1,0:T(8,128)(2,1)}), bf16[8,24,3712]{2,1,0:T(8,128)(2,1)S(1)}, u32[]{:S(2)}, u32[]{:S(2)}) async-start(bf16[8,24,3712]{2,1,0:T(8,128)(2,1)} %bitcast.5), calls=%async_computation | async-start | bytes 2850816 | tf_op jit(solution)/shard_map/all_to_all | solution.py:185
  34.2 5.4 %collective-permute-done.2 = bf16[32,1024]{1,0:T(8,128)(2,1)S(1)} collective-permute-done((bf16[32,1024]{1,0:T(8,128)(2,1)S(1)}, bf16[32,1024]{1,0:T(8,128)(2,1)S(1)}, u32[]{:S(2)}, u32[]{:S(2)}) %collective-permute-start.2) | collective-permute-done | bytes 65568 | tf_op jit(solution)/shard_map/ppermute | solution.py:75
  42.0 8.8 %collective-permute-done.3 = bf16[4,32,1024]{2,1,0:T(8,128)(2,1)S(1)} collective-permute-done((bf16[4,32,1024]{2,1,0:T(8,128)(2,1)S(1)}, bf16[4,32,1024]{2,1,0:T(8,128)(2,1)S(1)}, u32[]{:S(2)}, u32[]{:S(2)}) %collective-permute-start.3) | collective-permute-done | bytes 262176 | tf_op jit(solution)/shard_map/ppermute | solution.py:86
  54.9 5.4 %collective-permute-done.4 = bf16[4,32,1024]{2,1,0:T(8,128)(2,1)S(1)} collective-permute-done((bf16[4,32,1024]{2,1,0:T(8,128)(2,1)S(1)}, bf16[4,32,1024]{2,1,0:T(8,128)(2,1)S(1)}, u32[]{:S(2)}, u32[]{:S(2)}) %collective-permute-start.4) | collective-permute-done | bytes 262176 | tf_op jit(solution)/shard_map/ppermute | solution.py:86
  64.6 5.1 %collective-permute-done.5 = bf16[4,32,1024]{2,1,0:T(8,128)(2,1)S(1)} collective-permute-done((bf16[4,32,1024]{2,1,0:T(8,128)(2,1)S(1)}, bf16[4,32,1024]{2,1,0:T(8,128)(2,1)S(1)}, u32[]{:S(2)}, u32[]{:S(2)}) %collective-permute-start.5) | collective-permute-done | bytes 262176 | tf_op jit(solution)/shard_map/ppermute | solution.py:86
  73.4 5.9 %collective-permute-done.6 = bf16[4,32,1024]{2,1,0:T(8,128)(2,1)} collective-permute-done((bf16[4,32,1024]{2,1,0:T(8,128)(2,1)S(1)}, bf16[4,32,1024]{2,1,0:T(8,128)(2,1)}, u32[]{:S(2)}, u32[]{:S(2)}) %collective-permute-start.6) | collective-permute-done | bytes 262176 | tf_op jit(solution)/shard_map/ppermute | solution.py:86
  91.6 7.3 %collective-permute-done.8 = bf16[4,32,1024]{2,1,0:T(8,128)(2,1)} collective-permute-done((bf16[4,32,1024]{2,1,0:T(8,128)(2,1)}, bf16[4,32,1024]{2,1,0:T(8,128)(2,1)}, u32[]{:S(2)}, u32[]{:S(2)}) %collective-permute-start.8) | collective-permute-done | bytes 262176 | tf_op jit(solution)/shard_map/ppermute | solution.py:86
  104.4 4.1 collective-permute-done.9
  115.8 2.0 convolution_convert_fusion.2
  117.8 4.8 collective-permute-done.10
  125.0 3.0 constant_dynamic-update-slice_fusion
  128.0 3.1 multiply_reduce_fusion.1
  132.0 2.4 convolution_convert_fusion.1
  134.4 3.5 reshape.411
  137.9 153.9 %all_to_all.15 = bf16[64,20,1024]{2,1,0:T(8,128)(2,1)} all-to-all(bf16[64,20,1024]{2,1,0:T(8,128)(2,1)S(1)} %reshape.411), channel_id=1, replica_groups=mesh['dp'=8,'expert'=64] {'expert'}, dimensions={0} | all-to-all | bytes 5242880 | tf_op jit(solution)/shard_map/all_to_all | solution.py:233
  291.8 3.6 reshape.412
  295.5 5.5 %fusion.4 = f32[1280,768]{1,0:T(8,128)} fusion(bf16[1280,1024]{1,0:T(8,128)(2,1)S(1)} %reshape.412, bf16[1,768,1024]{2,1,0:T(8,128)(2,1)} %all-gather.4.cloned.1.call-done), kind=kOutput, calls=%fused_computation.13 | convolution fusion | flops 2013265920 | bytes 8126464 | tf_op jit(solution)/shard_map/dot_general | solution.py:129
  301.0 10.0 %convolution_convert_fusion = bf16[1280,1024]{1,0:T(8,128)(2,1)} fusion(bf16[1,768,1024]{2,1,0:T(8,128)(2,1)} %all-gather.8.cloned.1.call-done, bf16[1280,1024]{1,0:T(8,128)(2,1)S(1)} %reshape.412, f32[1280,768]{1,0:T(8,128)} %fusion.4, bf16[1,768,1024]{2,1,0:T(8,128)(2,1)} %all-gather.6.cloned.1.call-done), kind=kOutput, calls=%fused_computation.8 | convolution fusion | flops 4033740800 | bytes 12320768 | tf_op jit(solution)/shard_map/dot_general | solution.py:132
  311.0 5.2 %reshape.413 = bf16[64,20,1024]{2,1,0:T(8,128)(2,1)} reshape(bf16[1280,1024]{1,0:T(8,128)(2,1)} %convolution_convert_fusion) | data formatting | bytes 5242880 | tf_op jit(solution)/shard_map/reshape | solution.py:237
  316.2 6.9 %all-to-all-start.2 = ((bf16[64,20,1024]{2,1,0:T(8,128)(2,1)}), bf16[64,20,1024]{2,1,0:T(8,128)(2,1)}, u32[]{:S(2)}, u32[]{:S(2)}) async-start(bf16[64,20,1024]{2,1,0:T(8,128)(2,1)} %reshape.413), calls=%async_computation.2 | async-start | bytes 6291456 | tf_op jit(solution)/shard_map/all_to_all | solution.py:238
  325.0 141.5 %all-to-all-done.2 = bf16[64,20,1024]{2,1,0:T(8,128)(2,1)} async-done(((bf16[64,20,1024]{2,1,0:T(8,128)(2,1)}), bf16[64,20,1024]{2,1,0:T(8,128)(2,1)}, u32[]{:S(2)}, u32[]{:S(2)}) %all-to-all-start.2) | async-done | bytes 2621472 | tf_op jit(solution)/shard_map/all_to_all | solution.py:238
  466.6 3.6 reshape.414
  (143 shorter events, 58.2 us)
Async XLA Ops:
  6.5 116.8 %all-gather.4.cloned.1.call-start = ((), (), s32[]{:S(2)}) async-start(), calls=%async_computation.3 | async-start | bytes 1769472 | tf_op jit(solution)/shard_map/all_gather | solution.py:206
  7.3 116.0 %all-gather.6.cloned.1.call-start = ((), (), s32[]{:S(2)}) async-start(), calls=%async_computation.4 | async-start | bytes 1769472 | tf_op jit(solution)/shard_map/all_gather | solution.py:207
  8.0 24.2 %collective-permute-start.1 = (bf16[32,1024]{1,0:T(8,128)(2,1)}, bf16[32,1024]{1,0:T(8,128)(2,1)S(1)}, u32[]{:S(2)}, u32[]{:S(2)}) collective-permute-start(bf16[32,1024]{1,0:T(8,128)(2,1)} %param.25), channel_id=1, source_target_pairs={{0,16},{1,17},{2,18},{3,19},{4,20},{5,21},{6,22},{7,23},{8,24},{9,... | collective-permute-start | bytes 196616 | tf_op jit(solution)/shard_map/ppermute | solution.py:73
  11.5 22.6 %collective-permute-start = (bf16[32,1024]{1,0:T(8,128)(2,1)}, bf16[32,1024]{1,0:T(8,128)(2,1)S(1)}, u32[]{:S(2)}, u32[]{:S(2)}) collective-permute-start(bf16[32,1024]{1,0:T(8,128)(2,1)} %param.25), channel_id=1, source_target_pairs={{0,48},{1,49},{2,50},{3,51},{4,52},{5,53},{6,54},{7,55},{8,56},{9,... | collective-permute-start | bytes 196616 | tf_op jit(solution)/shard_map/ppermute | solution.py:74
  20.5 11.4 %copy-start.7 = (s32[128,8]{0,1:T(8,128)S(1)}, s32[128,8]{0,1:T(8,128)}, u32[]{:S(2)}) copy-start(s32[128,8]{0,1:T(8,128)} %param.27) | copy-start | bytes 12292
  20.5 19.1 %copy-start.4 = (bf16[32,1024]{1,0:T(8,128)(2,1)S(1)}, bf16[32,1024]{1,0:T(8,128)(2,1)}, u32[]{:S(2)}) copy-start(bf16[32,1024]{1,0:T(8,128)(2,1)} %param.25) | copy-start | bytes 196612
  21.7 61.3 %all-to-all-start = ((bf16[8,24,3712]{2,1,0:T(8,128)(2,1)}), bf16[8,24,3712]{2,1,0:T(8,128)(2,1)S(1)}, u32[]{:S(2)}, u32[]{:S(2)}) async-start(bf16[8,24,3712]{2,1,0:T(8,128)(2,1)} %bitcast.5), calls=%async_computation | async-start | bytes 2850816 | tf_op jit(solution)/shard_map/all_to_all | solution.py:185
  31.1 92.2 %all-gather.8.cloned.1.call-start = ((), (), s32[]{:S(2)}) async-start(), calls=%async_computation.5 | async-start | bytes 1769472 | tf_op jit(solution)/shard_map/all_gather | solution.py:208
  32.1 21.3 %copy-start.2 = (s32[128,64]{0,1:T(8,128)}, s32[128,64]{0,1:T(8,128)S(1)}, u32[]{:S(2)}) copy-start(s32[128,64]{0,1:T(8,128)S(1)} %fusion.29) | copy-start | bytes 98308
  32.2 7.4 %collective-permute-start.2 = (bf16[32,1024]{1,0:T(8,128)(2,1)S(1)}, bf16[32,1024]{1,0:T(8,128)(2,1)S(1)}, u32[]{:S(2)}, u32[]{:S(2)}) collective-permute-start(bf16[32,1024]{1,0:T(8,128)(2,1)S(1)} %collective-permute-done.1), channel_id=1, source_target_pairs={{0,16},{1,17},{2,18},{3,19},{4,20},{5,21},{6,22},{7,23},{8,24},{9,... | collective-permute-start | bytes 196616 | tf_op jit(solution)/shard_map/ppermute | solution.py:75
  34.2 18.7 %copy-start.5 = (bf16[32,1024]{1,0:T(8,128)(2,1)}, bf16[32,1024]{1,0:T(8,128)(2,1)S(1)}, u32[]{:S(2)}) copy-start(bf16[32,1024]{1,0:T(8,128)(2,1)S(1)} %collective-permute-done) | copy-start | bytes 196612
  39.6 13.2 %copy-start.6 = (bf16[32,1024]{1,0:T(8,128)(2,1)}, bf16[32,1024]{1,0:T(8,128)(2,1)S(1)}, u32[]{:S(2)}) copy-start(bf16[32,1024]{1,0:T(8,128)(2,1)S(1)} %collective-permute-done.2) | copy-start | bytes 196612
  39.6 11.2 %collective-permute-start.3 = (bf16[4,32,1024]{2,1,0:T(8,128)(2,1)S(1)}, bf16[4,32,1024]{2,1,0:T(8,128)(2,1)S(1)}, u32[]{:S(2)}, u32[]{:S(2)}) collective-permute-start(bf16[4,32,1024]{2,1,0:T(8,128)(2,1)S(1)} %pad_maximum_fusion.2), channel_id=1, source_target_pairs={{0,1},{1,2},{2,3},{3,4},{4,5},{5,6},{6,7},{7,8},{8,9},{9,10},{10,1... | collective-permute-start | bytes 786440 | tf_op jit(solution)/shard_map/ppermute | solution.py:86
  50.8 9.5 %collective-permute-start.4 = (bf16[4,32,1024]{2,1,0:T(8,128)(2,1)S(1)}, bf16[4,32,1024]{2,1,0:T(8,128)(2,1)S(1)}, u32[]{:S(2)}, u32[]{:S(2)}) collective-permute-start(bf16[4,32,1024]{2,1,0:T(8,128)(2,1)S(1)} %collective-permute-done.3), channel_id=1, source_target_pairs={{0,1},{1,2},{2,3},{3,4},{4,5},{5,6},{6,7},{7,8},{8,9},{9,10},{10,1... | collective-permute-start | bytes 786440 | tf_op jit(solution)/shard_map/ppermute | solution.py:86
  60.3 9.5 %collective-permute-start.5 = (bf16[4,32,1024]{2,1,0:T(8,128)(2,1)S(1)}, bf16[4,32,1024]{2,1,0:T(8,128)(2,1)S(1)}, u32[]{:S(2)}, u32[]{:S(2)}) collective-permute-start(bf16[4,32,1024]{2,1,0:T(8,128)(2,1)S(1)} %collective-permute-done.4), channel_id=1, source_target_pairs={{0,1},{1,2},{2,3},{3,4},{4,5},{5,6},{6,7},{7,8},{8,9},{9,10},{10,1... | collective-permute-start | bytes 786440 | tf_op jit(solution)/shard_map/ppermute | solution.py:86
  69.7 9.6 %collective-permute-start.6 = (bf16[4,32,1024]{2,1,0:T(8,128)(2,1)S(1)}, bf16[4,32,1024]{2,1,0:T(8,128)(2,1)}, u32[]{:S(2)}, u32[]{:S(2)}) collective-permute-start(bf16[4,32,1024]{2,1,0:T(8,128)(2,1)S(1)} %collective-permute-done.5), channel_id=1, source_target_pairs={{0,1},{1,2},{2,3},{3,4},{4,5},{5,6},{6,7},{7,8},{8,9},{9,10},{10,1... | collective-permute-start | bytes 786440 | tf_op jit(solution)/shard_map/ppermute | solution.py:86
  79.3 9.8 %collective-permute-start.7 = (bf16[4,32,1024]{2,1,0:T(8,128)(2,1)}, bf16[4,32,1024]{2,1,0:T(8,128)(2,1)}, u32[]{:S(2)}, u32[]{:S(2)}) collective-permute-start(bf16[4,32,1024]{2,1,0:T(8,128)(2,1)} %collective-permute-done.6), channel_id=1, source_target_pairs={{0,1},{1,2},{2,3},{3,4},{4,5},{5,6},{6,7},{7,8},{8,9},{9,10},{10,1... | collective-permute-start | bytes 786440 | tf_op jit(solution)/shard_map/ppermute | solution.py:86
  87.2 24.1 %copy-start.17 = (f32[128]{0:T(128)S(1)}, f32[128]{0:T(128)}, u32[]{:S(2)}) copy-start(f32[128]{0:T(128)} %param.24) | copy-start | bytes 1540
  89.1 9.8 %collective-permute-start.8 = (bf16[4,32,1024]{2,1,0:T(8,128)(2,1)}, bf16[4,32,1024]{2,1,0:T(8,128)(2,1)}, u32[]{:S(2)}, u32[]{:S(2)}) collective-permute-start(bf16[4,32,1024]{2,1,0:T(8,128)(2,1)} %collective-permute-done.7), channel_id=1, source_target_pairs={{0,1},{1,2},{2,3},{3,4},{4,5},{5,6},{6,7},{7,8},{8,9},{9,10},{10,1... | collective-permute-start | bytes 786440 | tf_op jit(solution)/shard_map/ppermute | solution.py:86
  98.9 9.7 %collective-permute-start.9 = (bf16[4,32,1024]{2,1,0:T(8,128)(2,1)}, bf16[4,32,1024]{2,1,0:T(8,128)(2,1)S(1)}, u32[]{:S(2)}, u32[]{:S(2)}) collective-permute-start(bf16[4,32,1024]{2,1,0:T(8,128)(2,1)} %collective-permute-done.8), channel_id=1, source_target_pairs={{0,1},{1,2},{2,3},{3,4},{4,5},{5,6},{6,7},{7,8},{8,9},{9,10},{10,1... | collective-permute-start | bytes 786440 | tf_op jit(solution)/shard_map/ppermute | solution.py:86
  109.4 15.6 %collective-permute-start.11 = (bf16[7,4,32,1024]{3,2,1,0:T(8,128)(2,1)}, bf16[7,4,32,1024]{3,2,1,0:T(8,128)(2,1)}, u32[]{:S(2)}, u32[]{:S(2)}) collective-permute-start(bf16[7,4,32,1024]{3,2,1,0:T(8,128)(2,1)} %get-tuple-element.24), channel_id=1, source_target_pairs={{0,64},{64,0},{128,192},{192,128},{256,320},{320,256},{384,448},{4... | collective-permute-start | bytes 5505032 | tf_op jit(solution)/shard_map/ppermute | solution.py:89
  113.1 9.5 %collective-permute-start.10 = (bf16[4,32,1024]{2,1,0:T(8,128)(2,1)S(1)}, bf16[4,32,1024]{2,1,0:T(8,128)(2,1)S(1)}, u32[]{:S(2)}, u32[]{:S(2)}) collective-permute-start(bf16[4,32,1024]{2,1,0:T(8,128)(2,1)S(1)} %collective-permute-done.9), channel_id=1, source_target_pairs={{0,1},{1,2},{2,3},{3,4},{4,5},{5,6},{6,7},{7,8},{8,9},{9,10},{10,1... | collective-permute-start | bytes 786440 | tf_op jit(solution)/shard_map/ppermute | solution.py:86
  316.2 7.1 %copy-start.8 = (s32[128,8]{0,1:T(8,128)S(1)}, s32[128,8]{0,1:T(8,128)}, u32[]{:S(2)}) copy-start(s32[128,8]{0,1:T(8,128)} %param.27) | copy-start | bytes 12292
  316.2 150.4 %all-to-all-start.2 = ((bf16[64,20,1024]{2,1,0:T(8,128)(2,1)}), bf16[64,20,1024]{2,1,0:T(8,128)(2,1)}, u32[]{:S(2)}, u32[]{:S(2)}) async-start(bf16[64,20,1024]{2,1,0:T(8,128)(2,1)} %reshape.413), calls=%async_computation.2 | async-start | bytes 6291456 | tf_op jit(solution)/shard_map/all_to_all | solution.py:238
  (11 other events, 43.5 us)
Sparse Core Ops, SparseCore 0:
  9.5 41.1 all-gather.3
  52.7 30.1 all-gather.5
  85.0 32.1 all-gather.7

commit v7 on v5

--- a/solution.py
+++ b/solution.py
@@ -134,6 +134,24 @@
 
 def expert_output(work_rows, gate_part, up_part, down_part):
     return hidden_product(work_rows, gate_part, up_part, down_part)
+
+
+def expert_exchange(slots):
+    expert_total = lax.axis_size("expert")
+    cols = 16
+    rows = expert_total // cols
+    if rows * cols != expert_total:
+        return lax.all_to_all(slots, "expert", split_axis=0, concat_axis=0, tiled=True)
+    grid = slots.reshape(rows, cols, *slots.shape[1:])
+    along_row = [[r * cols + c for c in range(cols)] for r in range(rows)]
+    along_col = [[r * cols + c for r in range(rows)] for c in range(cols)]
+    grid = lax.all_to_all(
+        grid, "expert", split_axis=1, concat_axis=1, tiled=True, axis_index_groups=along_row
+    )
+    grid = lax.all_to_all(
+        grid, "expert", split_axis=0, concat_axis=0, tiled=True, axis_index_groups=along_col
+    )
+    return grid.reshape(slots.shape)
 
 
 def local(
@@ -222,7 +240,7 @@
         .reshape(expert_total, most, -1)
     )
     total_rows = expert_total * most
-    received = lax.all_to_all(outgoing, "expert", split_axis=0, concat_axis=0, tiled=True)
+    received = expert_exchange(outgoing)
     work_rows = received.reshape(total_rows, -1)
     gate_whole, up_whole, down_whole = (
         lax.all_gather(gate_weight, "dp", axis=1, tiled=True),
@@ -232,7 +250,7 @@
     produced = expert_output(work_rows, gate_whole[0], up_whole[0], down_whole[0])
     produced = produced.astype(jnp.bfloat16)
     out_slots = produced.reshape(expert_total, most, -1)
-    returned = lax.all_to_all(out_slots, "expert", split_axis=0, concat_axis=0, tiled=True)
+    returned = expert_exchange(out_slots)
     flat_back = returned.reshape(total_rows, -1)
     copy_rank = jnp.sum(jnp.where(routed, rank[:, None, :], 0), axis=2)
     copy_index = routes * most + copy_rank

time: 474 us -> 503 us (1.061)
  blocking collectives: 0 us -> 161 us
  waiting for transfers between devices: 332 us -> 185 us
  local copies, waits for them, and re-layouts: 35.8 us -> 48.9 us
    all_to_all x0 -> x2, blocking collectives: none -> 161 us  [the longest x1 130 us: expert_exchange(): lax.all_to_all(grid, 'expert', split_axis=1, concat_axis=1, tiled=True, a...]
    all_to_all x2, waiting for transfers between devices: 281 us -> 138 us  [the longest x1 113 us: expert_exchange(): lax.all_to_all(grid, 'expert', split_axis=1, concat_axis=1, tiled=True, a...]
    another operation x2 -> x8, local copies, waits for them, and re-layouts: 1.32 us -> 19 us  [the longest x4 12.9 us: expert_exchange(): grid = slots.reshape(rows, cols, *slots.shape[1:])]
    reshape x4 -> x0, local copies, waits for them, and re-layouts: 13.4 us -> none  [the longest x1 5.18 us: local(): out_slots = produced.reshape(expert_total, most, -1)]
    all_to_all x0 -> x4, local copies, waits for them, and re-layouts: none -> 9.04 us  [the longest x2 4.66 us: expert_exchange(): lax.all_to_all(grid, 'expert', split_axis=0, concat_axis=0, tiled=True, a...]
    unnamed x30 -> x46, local copies, waits for them, and re-layouts: 12.2 us -> 10.4 us
where the time goes in v7:
time: 503 us; the launch traced here: 501 us
  waiting for transfers between devices  185 us (37%)
  blocking collectives  161 us (32%)
  local copies, waits for them, and re-layouts  48.9 us (10%)
  starting transfers between devices  48.5 us (10%)
  matrix products  28.7 us (6%)
  other arithmetic  14.3 us (3%)
  between operations  13.8 us (3%)
    all_to_all x1, blocking collectives, expert_exchange(): lax.all_to_all(grid, 'expert', split_axis=1, concat_axis=1, tiled=True, a...  130 us
    all_to_all x1, waiting for transfers between devices, expert_exchange(): lax.all_to_all(grid, 'expert', split_axis=1, concat_axis=1, tiled=True, a...  113 us
    ppermute x8, waiting for transfers between devices, ring_gather(): current = lax.ppermute(current, ('dp', 'expert'), walk)  40.9 us
    all_to_all x1, blocking collectives, expert_exchange(): lax.all_to_all(grid, 'expert', split_axis=0, concat_axis=0, tiled=True, a...  31.5 us
    all_to_all x1, waiting for transfers between devices, expert_exchange(): lax.all_to_all(grid, 'expert', split_axis=0, concat_axis=0, tiled=True, a...  24.1 us
    ppermute x8, starting transfers between devices, ring_gather(): current = lax.ppermute(current, ('dp', 'expert'), walk)  15.5 us
    another operation x4, local copies, waits for them, and re-layouts, expert_exchange(): grid = slots.reshape(rows, cols, *slots.shape[1:])  12.9 us
    unnamed x46, local copies, waits for them, and re-layouts  10.4 us
  transfers between devices with their start and end apart: 18, of which 11 were waited for; matrix products, arithmetic and copies ran while one was open for 9% of the time, Pallas kernels for 0%

profile of v7, /device:TPU:6, one launch (start us, length us, event | category | flops | bytes accessed | tf_op | source)
XLA Modules:
  0.0 500.7 jit_solution(15630298285537753146)
XLA Ops:
  6.5 3.5 collective-permute-start.1
  10.0 3.6 collective-permute-start
  20.2 9.3 %all-to-all-start = ((bf16[8,24,3712]{2,1,0:T(8,128)(2,1)}), bf16[8,24,3712]{2,1,0:T(8,128)(2,1)S(1)}, u32[]{:S(2)}, u32[]{:S(2)}) async-start(bf16[8,24,3712]{2,1,0:T(8,128)(2,1)} %bitcast.5), calls=%async_computation | async-start | bytes 2850816 | tf_op jit(solution)/shard_map/all_to_all | solution.py:203
  33.0 4.9 collective-permute-done.2
  40.5 8.7 %collective-permute-done.3 = bf16[4,32,1024]{2,1,0:T(8,128)(2,1)S(1)} collective-permute-done((bf16[4,32,1024]{2,1,0:T(8,128)(2,1)S(1)}, bf16[4,32,1024]{2,1,0:T(8,128)(2,1)S(1)}, u32[]{:S(2)}, u32[]{:S(2)}) %collective-permute-start.3) | collective-permute-done | bytes 262176 | tf_op jit(solution)/shard_map/ppermute | solution.py:86
  53.8 4.8 collective-permute-done.4
  63.0 5.1 %collective-permute-done.5 = bf16[4,32,1024]{2,1,0:T(8,128)(2,1)S(1)} collective-permute-done((bf16[4,32,1024]{2,1,0:T(8,128)(2,1)S(1)}, bf16[4,32,1024]{2,1,0:T(8,128)(2,1)S(1)}, u32[]{:S(2)}, u32[]{:S(2)}) %collective-permute-start.5) | collective-permute-done | bytes 262176 | tf_op jit(solution)/shard_map/ppermute | solution.py:86
  71.7 5.9 %collective-permute-done.6 = bf16[4,32,1024]{2,1,0:T(8,128)(2,1)} collective-permute-done((bf16[4,32,1024]{2,1,0:T(8,128)(2,1)S(1)}, bf16[4,32,1024]{2,1,0:T(8,128)(2,1)}, u32[]{:S(2)}, u32[]{:S(2)}) %collective-permute-start.6) | collective-permute-done | bytes 262176 | tf_op jit(solution)/shard_map/ppermute | solution.py:86
  90.6 6.6 %collective-permute-done.8 = bf16[4,32,1024]{2,1,0:T(8,128)(2,1)} collective-permute-done((bf16[4,32,1024]{2,1,0:T(8,128)(2,1)}, bf16[4,32,1024]{2,1,0:T(8,128)(2,1)}, u32[]{:S(2)}, u32[]{:S(2)}) %collective-permute-start.8) | collective-permute-done | bytes 262176 | tf_op jit(solution)/shard_map/ppermute | solution.py:86
  102.8 4.1 collective-permute-done.9
  118.0 3.5 collective-permute-done.10
  131.6 3.5 reshape_reshape.16
  135.1 3.7 copy.91
  138.8 8.9 %all-to-all-start.1 = ((bf16[4,16,20,1024]{3,0,2,1:T(4,128)(2,1)}), bf16[4,16,20,1024]{3,0,2,1:T(4,128)(2,1)S(1)}, u32[]{:S(2)}, u32[]{:S(2)}) async-start(bf16[4,16,20,1024]{3,0,2,1:T(4,128)(2,1)} %copy.91), calls=%async_computation.1 | async-start | bytes 5242880 | tf_op jit(solution)/shard_map/all_to_all | solution.py:148
  149.9 113.4 %all-to-all-done.1 = bf16[4,16,20,1024]{3,0,2,1:T(4,128)(2,1)S(1)} async-done(((bf16[4,16,20,1024]{3,0,2,1:T(4,128)(2,1)}), bf16[4,16,20,1024]{3,0,2,1:T(4,128)(2,1)S(1)}, u32[]{:S(2)}, u32[]{:S(2)}) %all-to-all-start.1) | async-done | bytes 2621472 | tf_op jit(solution)/shard_map/all_to_all | solution.py:148
  264.8 31.5 %all_to_all.25 = bf16[4,16,20,1024]{3,1,2,0:T(8,128)(2,1)S(1)} all-to-all(bf16[4,16,20,1024]{3,1,2,0:T(8,128)(2,1)S(1)} %copy.92), channel_id=1, replica_groups={{0,16,32,48},{1,17,33,49},{2,18,34,50},{3,19,35,51},{4,20,36,52},{5,21,..., dimensions={0} | all-to-all | bytes 5242880 | tf_op jit(solution)/shard_map/all_to_all | solution.py:151
  300.1 6.4 %fusion.4 = f32[1280,768]{1,0:T(8,128)} fusion(bf16[1280,1024]{1,0:T(8,128)(2,1)} %reshape_reshape.17, bf16[1,768,1024]{2,1,0:T(8,128)(2,1)} %all-gather.4.cloned.1.call-done), kind=kOutput, calls=%fused_computation.13 | convolution fusion | flops 2013265920 | bytes 8126464 | tf_op jit(solution)/shard_map/dot_general | solution.py:129
  306.5 10.0 %convolution_convert_fusion = bf16[1280,1024]{1,0:T(8,128)(2,1)} fusion(bf16[1,768,1024]{2,1,0:T(8,128)(2,1)} %all-gather.8.cloned.1.call-done, bf16[1280,1024]{1,0:T(8,128)(2,1)S(1)} %copy-done.2, f32[1280,768]{1,0:T(8,128)} %fusion.4, bf16[1,768,1024]{2,1,0:T(8,128)(2,1)} %all-gather.6.cloned.1.call-done), kind=kOutput, calls=%fused_computation.8 | convolution fusion | flops 4033740800 | bytes 12320768 | tf_op jit(solution)/shard_map/dot_general | solution.py:132
  316.6 3.5 reshape_reshape.18
  322.3 129.5 %all_to_all.26 = bf16[4,16,20,1024]{3,0,2,1:T(4,128)(2,1)S(1)} all-to-all(bf16[4,16,20,1024]{3,0,2,1:T(4,128)(2,1)S(1)} %copy.94), channel_id=1, replica_groups={{0,1,2,3,4,5,6,7,8,9,10,11,12,13,14,15},{16,17,18,19,20,21,22,23,24,25,..., dimensions={1} | all-to-all | bytes 5242880 | tf_op jit(solution)/shard_map/all_to_all | solution.py:148
  454.8 3.8 all-to-all-start.4
  460.5 24.1 %all-to-all-done.4 = bf16[4,16,20,1024]{3,1,2,0:T(8,128)(2,1)S(1)} async-done(((bf16[4,16,20,1024]{3,1,2,0:T(8,128)(2,1)}), bf16[4,16,20,1024]{3,1,2,0:T(8,128)(2,1)S(1)}, u32[]{:S(2)}, u32[]{:S(2)}) %all-to-all-start.4) | async-done | bytes 2621472 | tf_op jit(solution)/shard_map/all_to_all | solution.py:151
  484.6 3.2 copy.96
  487.7 3.6 reshape_reshape.19
  (154 shorter events, 81.8 us)
Async XLA Ops:
  6.5 24.0 %collective-permute-start.1 = (bf16[32,1024]{1,0:T(8,128)(2,1)}, bf16[32,1024]{1,0:T(8,128)(2,1)S(1)}, u32[]{:S(2)}, u32[]{:S(2)}) collective-permute-start(bf16[32,1024]{1,0:T(8,128)(2,1)} %param.25), channel_id=1, source_target_pairs={{0,16},{1,17},{2,18},{3,19},{4,20},{5,21},{6,22},{7,23},{8,24},{9,... | collective-permute-start | bytes 196616 | tf_op jit(solution)/shard_map/ppermute | solution.py:73
  10.0 23.0 %collective-permute-start = (bf16[32,1024]{1,0:T(8,128)(2,1)}, bf16[32,1024]{1,0:T(8,128)(2,1)S(1)}, u32[]{:S(2)}, u32[]{:S(2)}) collective-permute-start(bf16[32,1024]{1,0:T(8,128)(2,1)} %param.25), channel_id=1, source_target_pairs={{0,48},{1,49},{2,50},{3,51},{4,52},{5,53},{6,54},{7,55},{8,56},{9,... | collective-permute-start | bytes 196616 | tf_op jit(solution)/shard_map/ppermute | solution.py:74
  19.0 11.2 %copy-start.9 = (s32[128,8]{0,1:T(8,128)S(1)}, s32[128,8]{0,1:T(8,128)}, u32[]{:S(2)}) copy-start(s32[128,8]{0,1:T(8,128)} %param.27) | copy-start | bytes 12292
  19.0 18.9 %copy-start.5 = (bf16[32,1024]{1,0:T(8,128)(2,1)S(1)}, bf16[32,1024]{1,0:T(8,128)(2,1)}, u32[]{:S(2)}) copy-start(bf16[32,1024]{1,0:T(8,128)(2,1)} %param.25) | copy-start | bytes 196612
  20.2 61.2 %all-to-all-start = ((bf16[8,24,3712]{2,1,0:T(8,128)(2,1)}), bf16[8,24,3712]{2,1,0:T(8,128)(2,1)S(1)}, u32[]{:S(2)}, u32[]{:S(2)}) async-start(bf16[8,24,3712]{2,1,0:T(8,128)(2,1)} %bitcast.5), calls=%async_computation | async-start | bytes 2850816 | tf_op jit(solution)/shard_map/all_to_all | solution.py:203
  30.5 20.7 %copy-start.3 = (s32[128,64]{0,1:T(8,128)}, s32[128,64]{0,1:T(8,128)S(1)}, u32[]{:S(2)}) copy-start(s32[128,64]{0,1:T(8,128)S(1)} %fusion.29) | copy-start | bytes 98308
  30.5 21.2 %copy-start.6 = (bf16[32,1024]{1,0:T(8,128)(2,1)}, bf16[32,1024]{1,0:T(8,128)(2,1)S(1)}, u32[]{:S(2)}) copy-start(bf16[32,1024]{1,0:T(8,128)(2,1)S(1)} %collective-permute-done.1) | copy-start | bytes 196612
  30.5 7.4 %collective-permute-start.2 = (bf16[32,1024]{1,0:T(8,128)(2,1)S(1)}, bf16[32,1024]{1,0:T(8,128)(2,1)S(1)}, u32[]{:S(2)}, u32[]{:S(2)}) collective-permute-start(bf16[32,1024]{1,0:T(8,128)(2,1)S(1)} %collective-permute-done.1), channel_id=1, source_target_pairs={{0,16},{1,17},{2,18},{3,19},{4,20},{5,21},{6,22},{7,23},{8,24},{9,... | collective-permute-start | bytes 196616 | tf_op jit(solution)/shard_map/ppermute | solution.py:75
  33.0 18.8 %copy-start.7 = (bf16[32,1024]{1,0:T(8,128)(2,1)}, bf16[32,1024]{1,0:T(8,128)(2,1)S(1)}, u32[]{:S(2)}) copy-start(bf16[32,1024]{1,0:T(8,128)(2,1)S(1)} %collective-permute-done) | copy-start | bytes 196612
  37.9 11.2 %collective-permute-start.3 = (bf16[4,32,1024]{2,1,0:T(8,128)(2,1)S(1)}, bf16[4,32,1024]{2,1,0:T(8,128)(2,1)S(1)}, u32[]{:S(2)}, u32[]{:S(2)}) collective-permute-start(bf16[4,32,1024]{2,1,0:T(8,128)(2,1)S(1)} %pad_maximum_fusion.2), channel_id=1, source_target_pairs={{0,1},{1,2},{2,3},{3,4},{4,5},{5,6},{6,7},{7,8},{8,9},{9,10},{10,1... | collective-permute-start | bytes 786440 | tf_op jit(solution)/shard_map/ppermute | solution.py:86
  49.1 9.5 %collective-permute-start.4 = (bf16[4,32,1024]{2,1,0:T(8,128)(2,1)S(1)}, bf16[4,32,1024]{2,1,0:T(8,128)(2,1)S(1)}, u32[]{:S(2)}, u32[]{:S(2)}) collective-permute-start(bf16[4,32,1024]{2,1,0:T(8,128)(2,1)S(1)} %collective-permute-done.3), channel_id=1, source_target_pairs={{0,1},{1,2},{2,3},{3,4},{4,5},{5,6},{6,7},{7,8},{8,9},{9,10},{10,1... | collective-permute-start | bytes 786440 | tf_op jit(solution)/shard_map/ppermute | solution.py:86
  58.6 9.5 %collective-permute-start.5 = (bf16[4,32,1024]{2,1,0:T(8,128)(2,1)S(1)}, bf16[4,32,1024]{2,1,0:T(8,128)(2,1)S(1)}, u32[]{:S(2)}, u32[]{:S(2)}) collective-permute-start(bf16[4,32,1024]{2,1,0:T(8,128)(2,1)S(1)} %collective-permute-done.4), channel_id=1, source_target_pairs={{0,1},{1,2},{2,3},{3,4},{4,5},{5,6},{6,7},{7,8},{8,9},{9,10},{10,1... | collective-permute-start | bytes 786440 | tf_op jit(solution)/shard_map/ppermute | solution.py:86
  68.1 9.6 %collective-permute-start.6 = (bf16[4,32,1024]{2,1,0:T(8,128)(2,1)S(1)}, bf16[4,32,1024]{2,1,0:T(8,128)(2,1)}, u32[]{:S(2)}, u32[]{:S(2)}) collective-permute-start(bf16[4,32,1024]{2,1,0:T(8,128)(2,1)S(1)} %collective-permute-done.5), channel_id=1, source_target_pairs={{0,1},{1,2},{2,3},{3,4},{4,5},{5,6},{6,7},{7,8},{8,9},{9,10},{10,1... | collective-permute-start | bytes 786440 | tf_op jit(solution)/shard_map/ppermute | solution.py:86
  77.6 9.8 %collective-permute-start.7 = (bf16[4,32,1024]{2,1,0:T(8,128)(2,1)}, bf16[4,32,1024]{2,1,0:T(8,128)(2,1)}, u32[]{:S(2)}, u32[]{:S(2)}) collective-permute-start(bf16[4,32,1024]{2,1,0:T(8,128)(2,1)} %collective-permute-done.6), channel_id=1, source_target_pairs={{0,1},{1,2},{2,3},{3,4},{4,5},{5,6},{6,7},{7,8},{8,9},{9,10},{10,1... | collective-permute-start | bytes 786440 | tf_op jit(solution)/shard_map/ppermute | solution.py:86
  85.1 24.6 %copy-start.17 = (f32[128]{0:T(128)S(1)}, f32[128]{0:T(128)}, u32[]{:S(2)}) copy-start(f32[128]{0:T(128)} %param.24) | copy-start | bytes 1540
  87.4 9.8 %collective-permute-start.8 = (bf16[4,32,1024]{2,1,0:T(8,128)(2,1)}, bf16[4,32,1024]{2,1,0:T(8,128)(2,1)}, u32[]{:S(2)}, u32[]{:S(2)}) collective-permute-start(bf16[4,32,1024]{2,1,0:T(8,128)(2,1)} %collective-permute-done.7), channel_id=1, source_target_pairs={{0,1},{1,2},{2,3},{3,4},{4,5},{5,6},{6,7},{7,8},{8,9},{9,10},{10,1... | collective-permute-start | bytes 786440 | tf_op jit(solution)/shard_map/ppermute | solution.py:86
  97.2 9.7 %collective-permute-start.9 = (bf16[4,32,1024]{2,1,0:T(8,128)(2,1)}, bf16[4,32,1024]{2,1,0:T(8,128)(2,1)S(1)}, u32[]{:S(2)}, u32[]{:S(2)}) collective-permute-start(bf16[4,32,1024]{2,1,0:T(8,128)(2,1)} %collective-permute-done.8), channel_id=1, source_target_pairs={{0,1},{1,2},{2,3},{3,4},{4,5},{5,6},{6,7},{7,8},{8,9},{9,10},{10,1... | collective-permute-start | bytes 786440 | tf_op jit(solution)/shard_map/ppermute | solution.py:86
  107.7 14.5 %collective-permute-start.11 = (bf16[7,4,32,1024]{3,2,1,0:T(8,128)(2,1)}, bf16[7,4,32,1024]{3,2,1,0:T(8,128)(2,1)}, u32[]{:S(2)}, u32[]{:S(2)}) collective-permute-start(bf16[7,4,32,1024]{3,2,1,0:T(8,128)(2,1)} %get-tuple-element.16), channel_id=1, source_target_pairs={{0,64},{64,0},{128,192},{192,128},{256,320},{320,256},{384,448},{4... | collective-permute-start | bytes 5505032 | tf_op jit(solution)/shard_map/ppermute | solution.py:89
  112.1 9.5 %collective-permute-start.10 = (bf16[4,32,1024]{2,1,0:T(8,128)(2,1)S(1)}, bf16[4,32,1024]{2,1,0:T(8,128)(2,1)S(1)}, u32[]{:S(2)}, u32[]{:S(2)}) collective-permute-start(bf16[4,32,1024]{2,1,0:T(8,128)(2,1)S(1)} %collective-permute-done.9), channel_id=1, source_target_pairs={{0,1},{1,2},{2,3},{3,4},{4,5},{5,6},{6,7},{7,8},{8,9},{9,10},{10,1... | collective-permute-start | bytes 786440 | tf_op jit(solution)/shard_map/ppermute | solution.py:86
  138.8 124.6 %all-to-all-start.1 = ((bf16[4,16,20,1024]{3,0,2,1:T(4,128)(2,1)}), bf16[4,16,20,1024]{3,0,2,1:T(4,128)(2,1)S(1)}, u32[]{:S(2)}, u32[]{:S(2)}) async-start(bf16[4,16,20,1024]{3,0,2,1:T(4,128)(2,1)} %copy.91), calls=%async_computation.1 | async-start | bytes 5242880 | tf_op jit(solution)/shard_map/all_to_all | solution.py:148
  147.7 152.4 %all-gather.4.cloned.1.call-start = ((), (), s32[]{:S(2)}) async-start(), calls=%async_computation.5 | async-start | bytes 1769472 | tf_op jit(solution)/shard_map/all_gather | solution.py:246
  148.4 158.1 %all-gather.8.cloned.1.call-start = ((), (), s32[]{:S(2)}) async-start(), calls=%async_computation.7 | async-start | bytes 1769472 | tf_op jit(solution)/shard_map/all_gather | solution.py:248
  149.2 157.4 %all-gather.6.cloned.1.call-start = ((), (), s32[]{:S(2)}) async-start(), calls=%async_computation.6 | async-start | bytes 1769472 | tf_op jit(solution)/shard_map/all_gather | solution.py:247
  454.8 29.8 %all-to-all-start.4 = ((bf16[4,16,20,1024]{3,1,2,0:T(8,128)(2,1)}), bf16[4,16,20,1024]{3,1,2,0:T(8,128)(2,1)S(1)}, u32[]{:S(2)}, u32[]{:S(2)}) async-start(bf16[4,16,20,1024]{3,1,2,0:T(8,128)(2,1)} %copy.95), calls=%async_computation.4 | async-start | bytes 5242880 | tf_op jit(solution)/shard_map/all_to_all | solution.py:151
  (13 other events, 42.4 us)
Sparse Core Ops, SparseCore 0:
  150.6 29.1 all-gather.3
  182.0 32.3 all-gather.7
  216.5 32.2 all-gather.5

commit v8 on v5

--- a/solution.py
+++ b/solution.py
@@ -87,7 +87,7 @@
         mine.append(current)
     mine = jnp.stack(mine)
     partner = lax.ppermute(mine[: half - 1], "dp", [(i, i ^ 1) for i in range(owners)])
-    return jnp.concatenate([by_row[None], mine, partner], axis=0)
+    return by_row[None], mine, partner
 
 
 def project_heads(attended, output_weight):
@@ -117,11 +117,17 @@
     split = attended.reshape(attended.shape[0], rows, cols, block)
     split = jnp.take(jnp.take(split, col_order, axis=2), row_order, axis=1)
     split = jnp.swapaxes(split, 1, 2)
-    return jnp.dot(
-        split.reshape(attended.shape[0], -1),
-        gathered.reshape(rows * cols * block, -1),
-        preferred_element_type=jnp.float32,
-    )
+    projected = jnp.zeros((attended.shape[0], output_weight.shape[1]), jnp.float32)
+    first = 0
+    for pieces in gathered:
+        last = first + pieces.shape[0]
+        projected = projected + jnp.dot(
+            split[:, first:last].reshape(attended.shape[0], -1),
+            pieces.reshape(-1, output_weight.shape[1]),
+            preferred_element_type=jnp.float32,
+        )
+        first = last
+    return projected
 
 
 def hidden_product(block, gate_part, up_part, down_part):

time: 474 us -> 473 us (level)
    unnamed x30 -> x56, local copies, waits for them, and re-layouts: 12.2 us -> 10.2 us
  transfers between devices with their start and end apart: 18 -> 18, of which waited for: 11 -> 11; matrix products, arithmetic and copies ran while one was open for 9% -> 8% of each run, Pallas kernels for 0% -> 0%
where the time goes in v8:
time: 473 us; the launch traced here: 472 us
  waiting for transfers between devices  335 us (71%)
  starting transfers between devices  53.4 us (11%)
  local copies, waits for them, and re-layouts  31.5 us (7%)
  matrix products  25.8 us (5%)
  between operations  13.9 us (3%)
  other arithmetic  12.3 us (3%)
    all_to_all x1, waiting for transfers between devices, local(): lax.all_to_all(out_slots, 'expert', split_axis=0, concat_axis=0, tiled=True)  141 us
    all_to_all x1, waiting for transfers between devices, local(): lax.all_to_all(outgoing, 'expert', split_axis=0, concat_axis=0, tiled=True)  140 us
    ppermute x8, waiting for transfers between devices, ring_gather(): current = lax.ppermute(current, ('dp', 'expert'), walk)  46.6 us
    ppermute x8, starting transfers between devices, ring_gather(): current = lax.ppermute(current, ('dp', 'expert'), walk)  15.3 us
    unnamed x56, local copies, waits for them, and re-layouts  10.2 us
    all_to_all x1, starting transfers between devices, local(): lax.all_to_all(outgoing, 'expert', split_axis=0, concat_axis=0, tiled=True)  10 us
    dot_general x1, matrix products, hidden_product(): return jnp.dot(active, down_part, preferred_element_type=jnp.float32)  10 us
    all_to_all x1, starting transfers between devices, local(): lax.all_to_all(outgoing_pack.reshape(owner_total, capacity, -1), 'dp', sp...  9.47 us
  transfers between devices with their start and end apart: 18, of which 11 were waited for; matrix products, arithmetic and copies ran while one was open for 8% of the time, Pallas kernels for 0%

profile of v8, /device:TPU:6, one launch (start us, length us, event | category | flops | bytes accessed | tf_op | source)
XLA Modules:
  0.0 471.8 jit_solution(14147809949098280699)
XLA Ops:
  6.5 3.5 collective-permute-start.1
  10.0 3.6 collective-permute-start
  20.2 9.5 %all-to-all-start = ((bf16[8,24,3712]{2,1,0:T(8,128)(2,1)}), bf16[8,24,3712]{2,1,0:T(8,128)(2,1)S(1)}, u32[]{:S(2)}, u32[]{:S(2)}) async-start(bf16[8,24,3712]{2,1,0:T(8,128)(2,1)} %bitcast.5), calls=%async_computation | async-start | bytes 2850816 | tf_op jit(solution)/shard_map/all_to_all | solution.py:191
  30.6 1.9 collective-permute-start.2
  32.5 5.4 %collective-permute-done.2 = bf16[32,1024]{1,0:T(8,128)(2,1)S(1)} collective-permute-done((bf16[32,1024]{1,0:T(8,128)(2,1)S(1)}, bf16[32,1024]{1,0:T(8,128)(2,1)S(1)}, u32[]{:S(2)}, u32[]{:S(2)}) %collective-permute-start.2) | collective-permute-done | bytes 65568 | tf_op jit(solution)/shard_map/ppermute | solution.py:75
  40.6 9.2 %collective-permute-done.3 = bf16[4,32,1024]{2,1,0:T(8,128)(2,1)S(1)} collective-permute-done((bf16[4,32,1024]{2,1,0:T(8,128)(2,1)S(1)}, bf16[4,32,1024]{2,1,0:T(8,128)(2,1)S(1)}, u32[]{:S(2)}, u32[]{:S(2)}) %collective-permute-start.3) | collective-permute-done | bytes 262176 | tf_op jit(solution)/shard_map/ppermute | solution.py:86
  53.1 6.3 %collective-permute-done.4 = bf16[4,32,1024]{2,1,0:T(8,128)(2,1)S(1)} collective-permute-done((bf16[4,32,1024]{2,1,0:T(8,128)(2,1)S(1)}, bf16[4,32,1024]{2,1,0:T(8,128)(2,1)S(1)}, u32[]{:S(2)}, u32[]{:S(2)}) %collective-permute-start.4) | collective-permute-done | bytes 262176 | tf_op jit(solution)/shard_map/ppermute | solution.py:86
  64.4 4.4 collective-permute-done.5
  72.4 6.0 %collective-permute-done.6 = bf16[4,32,1024]{2,1,0:T(8,128)(2,1)} collective-permute-done((bf16[4,32,1024]{2,1,0:T(8,128)(2,1)S(1)}, bf16[4,32,1024]{2,1,0:T(8,128)(2,1)}, u32[]{:S(2)}, u32[]{:S(2)}) %collective-permute-start.6) | collective-permute-done | bytes 262176 | tf_op jit(solution)/shard_map/ppermute | solution.py:86
  90.7 7.1 %collective-permute-done.8 = bf16[4,32,1024]{2,1,0:T(8,128)(2,1)S(1)} collective-permute-done((bf16[4,32,1024]{2,1,0:T(8,128)(2,1)}, bf16[4,32,1024]{2,1,0:T(8,128)(2,1)S(1)}, u32[]{:S(2)}, u32[]{:S(2)}) %collective-permute-start.8) | collective-permute-done | bytes 262176 | tf_op jit(solution)/shard_map/ppermute | solution.py:86
  102.4 4.8 %collective-permute-done.9 = bf16[4,32,1024]{2,1,0:T(8,128)(2,1)S(1)} collective-permute-done((bf16[4,32,1024]{2,1,0:T(8,128)(2,1)S(1)}, bf16[4,32,1024]{2,1,0:T(8,128)(2,1)S(1)}, u32[]{:S(2)}, u32[]{:S(2)}) %collective-permute-start.9) | collective-permute-done | bytes 262176 | tf_op jit(solution)/shard_map/ppermute | solution.py:86
  116.1 7.1 %collective-permute-done.10 = bf16[4,32,1024]{2,1,0:T(8,128)(2,1)S(1)} collective-permute-done((bf16[4,32,1024]{2,1,0:T(8,128)(2,1)S(1)}, bf16[4,32,1024]{2,1,0:T(8,128)(2,1)S(1)}, u32[]{:S(2)}, u32[]{:S(2)}) %collective-permute-start.10) | collective-permute-done | bytes 262176 | tf_op jit(solution)/shard_map/ppermute | solution.py:86
  123.9 2.0 convolution_bitcast_fusion
  125.9 2.2 multiply_reduce_fusion.1
  129.9 2.3 reshape.409
  132.3 10.0 %all-to-all-start.1 = ((bf16[64,20,1024]{2,1,0:T(8,128)(2,1)}), bf16[64,20,1024]{2,1,0:T(8,128)(2,1)S(1)}, u32[]{:S(2)}, u32[]{:S(2)}) async-start(bf16[64,20,1024]{2,1,0:T(8,128)(2,1)} %reshape.409), calls=%async_computation.1 | async-start | bytes 6291456 | tf_op jit(solution)/shard_map/all_to_all | solution.py:231
  144.5 139.9 %all-to-all-done.1 = bf16[64,20,1024]{2,1,0:T(8,128)(2,1)S(1)} async-done(((bf16[64,20,1024]{2,1,0:T(8,128)(2,1)}), bf16[64,20,1024]{2,1,0:T(8,128)(2,1)S(1)}, u32[]{:S(2)}, u32[]{:S(2)}) %all-to-all-start.1) | async-done | bytes 2621472 | tf_op jit(solution)/shard_map/all_to_all | solution.py:231
  284.4 2.2 reshape.410
  286.6 6.4 %fusion.4 = f32[1280,768]{1,0:T(8,128)} fusion(bf16[1280,1024]{1,0:T(8,128)(2,1)} %reshape.410, bf16[1,768,1024]{2,1,0:T(8,128)(2,1)} %all-gather.4.cloned.1.call-done), kind=kOutput, calls=%fused_computation.13 | convolution fusion | flops 2013265920 | bytes 8126464 | tf_op jit(solution)/shard_map/dot_general | solution.py:135
  293.1 10.0 %convolution_convert_fusion = bf16[1280,1024]{1,0:T(8,128)(2,1)} fusion(bf16[1,768,1024]{2,1,0:T(8,128)(2,1)} %all-gather.8.cloned.1.call-done, bf16[1280,1024]{1,0:T(8,128)(2,1)S(1)} %copy-done.3, f32[1280,768]{1,0:T(8,128)} %fusion.4, bf16[1,768,1024]{2,1,0:T(8,128)(2,1)} %all-gather.6.cloned.1.call-done), kind=kOutput, calls=%fused_computation.8 | convolution fusion | flops 4033740800 | bytes 12320768 | tf_op jit(solution)/shard_map/dot_general | solution.py:138
  303.1 5.1 %reshape.411 = bf16[64,20,1024]{2,1,0:T(8,128)(2,1)} reshape(bf16[1280,1024]{1,0:T(8,128)(2,1)} %convolution_convert_fusion) | data formatting | bytes 5242880 | tf_op jit(solution)/shard_map/reshape | solution.py:240
  308.3 7.4 %all-to-all-start.2 = ((bf16[64,20,1024]{2,1,0:T(8,128)(2,1)}), bf16[64,20,1024]{2,1,0:T(8,128)(2,1)}, u32[]{:S(2)}, u32[]{:S(2)}) async-start(bf16[64,20,1024]{2,1,0:T(8,128)(2,1)} %reshape.411), calls=%async_computation.2 | async-start | bytes 6291456 | tf_op jit(solution)/shard_map/all_to_all | solution.py:241
  317.6 141.2 %all-to-all-done.2 = bf16[64,20,1024]{2,1,0:T(8,128)(2,1)} async-done(((bf16[64,20,1024]{2,1,0:T(8,128)(2,1)}), bf16[64,20,1024]{2,1,0:T(8,128)(2,1)}, u32[]{:S(2)}, u32[]{:S(2)}) %all-to-all-start.2) | async-done | bytes 2621472 | tf_op jit(solution)/shard_map/all_to_all | solution.py:241
  458.8 3.6 reshape.412
  (158 shorter events, 56.6 us)
Async XLA Ops:
  6.5 24.0 %collective-permute-start.1 = (bf16[32,1024]{1,0:T(8,128)(2,1)}, bf16[32,1024]{1,0:T(8,128)(2,1)S(1)}, u32[]{:S(2)}, u32[]{:S(2)}) collective-permute-start(bf16[32,1024]{1,0:T(8,128)(2,1)} %param.25), channel_id=1, source_target_pairs={{0,16},{1,17},{2,18},{3,19},{4,20},{5,21},{6,22},{7,23},{8,24},{9,... | collective-permute-start | bytes 196616 | tf_op jit(solution)/shard_map/ppermute | solution.py:73
  10.0 22.5 %collective-permute-start = (bf16[32,1024]{1,0:T(8,128)(2,1)}, bf16[32,1024]{1,0:T(8,128)(2,1)S(1)}, u32[]{:S(2)}, u32[]{:S(2)}) collective-permute-start(bf16[32,1024]{1,0:T(8,128)(2,1)} %param.25), channel_id=1, source_target_pairs={{0,48},{1,49},{2,50},{3,51},{4,52},{5,53},{6,54},{7,55},{8,56},{9,... | collective-permute-start | bytes 196616 | tf_op jit(solution)/shard_map/ppermute | solution.py:74
  20.2 10.1 %copy-start.11 = (s32[128,8]{0,1:T(8,128)S(1)}, s32[128,8]{0,1:T(8,128)}, u32[]{:S(2)}) copy-start(s32[128,8]{0,1:T(8,128)} %param.27) | copy-start | bytes 12292
  20.2 17.7 %copy-start.10 = (bf16[32,1024]{1,0:T(8,128)(2,1)S(1)}, bf16[32,1024]{1,0:T(8,128)(2,1)}, u32[]{:S(2)}) copy-start(bf16[32,1024]{1,0:T(8,128)(2,1)} %param.25) | copy-start | bytes 196612
  20.2 61.9 %all-to-all-start = ((bf16[8,24,3712]{2,1,0:T(8,128)(2,1)}), bf16[8,24,3712]{2,1,0:T(8,128)(2,1)S(1)}, u32[]{:S(2)}, u32[]{:S(2)}) async-start(bf16[8,24,3712]{2,1,0:T(8,128)(2,1)} %bitcast.5), calls=%async_computation | async-start | bytes 2850816 | tf_op jit(solution)/shard_map/all_to_all | solution.py:191
  30.5 30.7 %copy-start.6 = (s32[128,64]{0,1:T(8,128)}, s32[128,64]{0,1:T(8,128)S(1)}, u32[]{:S(2)}) copy-start(s32[128,64]{0,1:T(8,128)S(1)} %fusion.31) | copy-start | bytes 98308
  30.6 7.4 %collective-permute-start.2 = (bf16[32,1024]{1,0:T(8,128)(2,1)S(1)}, bf16[32,1024]{1,0:T(8,128)(2,1)S(1)}, u32[]{:S(2)}, u32[]{:S(2)}) collective-permute-start(bf16[32,1024]{1,0:T(8,128)(2,1)S(1)} %collective-permute-done.1), channel_id=1, source_target_pairs={{0,16},{1,17},{2,18},{3,19},{4,20},{5,21},{6,22},{7,23},{8,24},{9,... | collective-permute-start | bytes 196616 | tf_op jit(solution)/shard_map/ppermute | solution.py:75
  38.7 11.2 %collective-permute-start.3 = (bf16[4,32,1024]{2,1,0:T(8,128)(2,1)S(1)}, bf16[4,32,1024]{2,1,0:T(8,128)(2,1)S(1)}, u32[]{:S(2)}, u32[]{:S(2)}) collective-permute-start(bf16[4,32,1024]{2,1,0:T(8,128)(2,1)S(1)} %pad_maximum_fusion.2), channel_id=1, source_target_pairs={{0,1},{1,2},{2,3},{3,4},{4,5},{5,6},{6,7},{7,8},{8,9},{9,10},{10,1... | collective-permute-start | bytes 786440 | tf_op jit(solution)/shard_map/ppermute | solution.py:86
  49.9 9.5 %collective-permute-start.4 = (bf16[4,32,1024]{2,1,0:T(8,128)(2,1)S(1)}, bf16[4,32,1024]{2,1,0:T(8,128)(2,1)S(1)}, u32[]{:S(2)}, u32[]{:S(2)}) collective-permute-start(bf16[4,32,1024]{2,1,0:T(8,128)(2,1)S(1)} %collective-permute-done.3), channel_id=1, source_target_pairs={{0,1},{1,2},{2,3},{3,4},{4,5},{5,6},{6,7},{7,8},{8,9},{9,10},{10,1... | collective-permute-start | bytes 786440 | tf_op jit(solution)/shard_map/ppermute | solution.py:86
  59.3 9.5 %collective-permute-start.5 = (bf16[4,32,1024]{2,1,0:T(8,128)(2,1)S(1)}, bf16[4,32,1024]{2,1,0:T(8,128)(2,1)S(1)}, u32[]{:S(2)}, u32[]{:S(2)}) collective-permute-start(bf16[4,32,1024]{2,1,0:T(8,128)(2,1)S(1)} %collective-permute-done.4), channel_id=1, source_target_pairs={{0,1},{1,2},{2,3},{3,4},{4,5},{5,6},{6,7},{7,8},{8,9},{9,10},{10,1... | collective-permute-start | bytes 786440 | tf_op jit(solution)/shard_map/ppermute | solution.py:86
  68.8 9.6 %collective-permute-start.6 = (bf16[4,32,1024]{2,1,0:T(8,128)(2,1)S(1)}, bf16[4,32,1024]{2,1,0:T(8,128)(2,1)}, u32[]{:S(2)}, u32[]{:S(2)}) collective-permute-start(bf16[4,32,1024]{2,1,0:T(8,128)(2,1)S(1)} %collective-permute-done.5), channel_id=1, source_target_pairs={{0,1},{1,2},{2,3},{3,4},{4,5},{5,6},{6,7},{7,8},{8,9},{9,10},{10,1... | collective-permute-start | bytes 786440 | tf_op jit(solution)/shard_map/ppermute | solution.py:86
  78.4 9.8 %collective-permute-start.7 = (bf16[4,32,1024]{2,1,0:T(8,128)(2,1)}, bf16[4,32,1024]{2,1,0:T(8,128)(2,1)}, u32[]{:S(2)}, u32[]{:S(2)}) collective-permute-start(bf16[4,32,1024]{2,1,0:T(8,128)(2,1)} %collective-permute-done.6), channel_id=1, source_target_pairs={{0,1},{1,2},{2,3},{3,4},{4,5},{5,6},{6,7},{7,8},{8,9},{9,10},{10,1... | collective-permute-start | bytes 786440 | tf_op jit(solution)/shard_map/ppermute | solution.py:86
  88.2 9.7 %collective-permute-start.8 = (bf16[4,32,1024]{2,1,0:T(8,128)(2,1)}, bf16[4,32,1024]{2,1,0:T(8,128)(2,1)S(1)}, u32[]{:S(2)}, u32[]{:S(2)}) collective-permute-start(bf16[4,32,1024]{2,1,0:T(8,128)(2,1)} %collective-permute-done.7), channel_id=1, source_target_pairs={{0,1},{1,2},{2,3},{3,4},{4,5},{5,6},{6,7},{7,8},{8,9},{9,10},{10,1... | collective-permute-start | bytes 786440 | tf_op jit(solution)/shard_map/ppermute | solution.py:86
  90.3 19.8 %copy-start.15 = (s32[128]{0:T(128)S(1)}, s32[128]{0:T(128)}, u32[]{:S(2)}) copy-start(s32[128]{0:T(128)} %get-tuple-element.9) | copy-start | bytes 1540
  90.3 19.8 %copy-start.16 = (s32[128]{0:T(128)S(1)}, s32[128]{0:T(128)}, u32[]{:S(2)}) copy-start(s32[128]{0:T(128)} %get-tuple-element.32) | copy-start | bytes 1540
  97.8 9.5 %collective-permute-start.9 = (bf16[4,32,1024]{2,1,0:T(8,128)(2,1)S(1)}, bf16[4,32,1024]{2,1,0:T(8,128)(2,1)S(1)}, u32[]{:S(2)}, u32[]{:S(2)}) collective-permute-start(bf16[4,32,1024]{2,1,0:T(8,128)(2,1)S(1)} %collective-permute-done.8), channel_id=1, source_target_pairs={{0,1},{1,2},{2,3},{3,4},{4,5},{5,6},{6,7},{7,8},{8,9},{9,10},{10,1... | collective-permute-start | bytes 786440 | tf_op jit(solution)/shard_map/ppermute | solution.py:86
  108.2 15.8 %collective-permute-start.11 = (bf16[7,4,32,1024]{3,2,1,0:T(8,128)(2,1)}, bf16[7,4,32,1024]{3,2,1,0:T(8,128)(2,1)}, u32[]{:S(2)}, u32[]{:S(2)}) collective-permute-start(bf16[7,4,32,1024]{3,2,1,0:T(8,128)(2,1)} %get-tuple-element.15), channel_id=1, source_target_pairs={{0,64},{64,0},{128,192},{192,128},{256,320},{320,256},{384,448},{4... | collective-permute-start | bytes 5505032 | tf_op jit(solution)/shard_map/ppermute | solution.py:89
  113.7 9.5 %collective-permute-start.10 = (bf16[4,32,1024]{2,1,0:T(8,128)(2,1)S(1)}, bf16[4,32,1024]{2,1,0:T(8,128)(2,1)S(1)}, u32[]{:S(2)}, u32[]{:S(2)}) collective-permute-start(bf16[4,32,1024]{2,1,0:T(8,128)(2,1)S(1)} %copy-done.9), channel_id=1, source_target_pairs={{0,1},{1,2},{2,3},{3,4},{4,5},{5,6},{6,7},{7,8},{8,9},{9,10},{10,1... | collective-permute-start | bytes 786440 | tf_op jit(solution)/shard_map/ppermute | solution.py:86
  132.3 152.2 %all-to-all-start.1 = ((bf16[64,20,1024]{2,1,0:T(8,128)(2,1)}), bf16[64,20,1024]{2,1,0:T(8,128)(2,1)S(1)}, u32[]{:S(2)}, u32[]{:S(2)}) async-start(bf16[64,20,1024]{2,1,0:T(8,128)(2,1)} %reshape.409), calls=%async_computation.1 | async-start | bytes 6291456 | tf_op jit(solution)/shard_map/all_to_all | solution.py:231
  142.3 144.3 %all-gather.4.cloned.1.call-start = ((), (), s32[]{:S(2)}) async-start(), calls=%async_computation.3 | async-start | bytes 1769472 | tf_op jit(solution)/shard_map/all_gather | solution.py:234
  143.0 150.0 %all-gather.6.cloned.1.call-start = ((), (), s32[]{:S(2)}) async-start(), calls=%async_computation.4 | async-start | bytes 1769472 | tf_op jit(solution)/shard_map/all_gather | solution.py:235
  143.8 149.3 %all-gather.8.cloned.1.call-start = ((), (), s32[]{:S(2)}) async-start(), calls=%async_computation.5 | async-start | bytes 1769472 | tf_op jit(solution)/shard_map/all_gather | solution.py:236
  308.3 7.6 %copy-start.14 = (f32[128,8]{0,1:T(8,128)S(1)}, f32[128,8]{0,1:T(8,128)}, u32[]{:S(2)}) copy-start(f32[128,8]{0,1:T(8,128)} %param.28) | copy-start | bytes 12292
  308.3 150.5 %all-to-all-start.2 = ((bf16[64,20,1024]{2,1,0:T(8,128)(2,1)}), bf16[64,20,1024]{2,1,0:T(8,128)(2,1)}, u32[]{:S(2)}, u32[]{:S(2)}) async-start(bf16[64,20,1024]{2,1,0:T(8,128)(2,1)} %reshape.411), calls=%async_computation.2 | async-start | bytes 6291456 | tf_op jit(solution)/shard_map/all_to_all | solution.py:241
  (18 other events, 52.2 us)
Sparse Core Ops, SparseCore 0:
  145.2 31.2 all-gather.3
  178.6 32.2 all-gather.5
  213.1 32.3 all-gather.7

commit v9 on v8

--- a/solution.py
+++ b/solution.py
@@ -74,17 +74,21 @@
     down = lax.ppermute(block, "expert", ring_pairs(rows, cols, -1, 0))
     up_two = lax.ppermute(up, "expert", ring_pairs(rows, cols, 1, 0))
     by_row = jnp.stack([block, down, up_two, up])
-    walk = [
-        (owner * expert_total + src, owner * expert_total + dst)
-        for owner in range(owners)
-        for src, dst in ring_pairs(rows, cols, 0, 1 if owner % 2 == 0 else -1)
-    ]
+    def walk(stride):
+        return [
+            (owner * expert_total + src, owner * expert_total + dst)
+            for owner in range(owners)
+            for src, dst in ring_pairs(rows, cols, 0, stride if owner % 2 == 0 else -stride)
+        ]
+
     half = cols // 2
-    mine = []
-    current = by_row
-    for step in range(half):
-        current = lax.ppermute(current, ("dp", "expert"), walk)
-        mine.append(current)
+    odd = lax.ppermute(by_row, ("dp", "expert"), walk(1))
+    even = lax.ppermute(by_row, ("dp", "expert"), walk(2))
+    mine = [odd, even]
+    for _ in range(half // 2 - 1):
+        odd = lax.ppermute(odd, ("dp", "expert"), walk(2))
+        even = lax.ppermute(even, ("dp", "expert"), walk(2))
+        mine += [odd, even]
     mine = jnp.stack(mine)
     partner = lax.ppermute(mine[: half - 1], "dp", [(i, i ^ 1) for i in range(owners)])
     return by_row[None], mine, partner

time: 473 us -> 455 us (0.962)
  waiting for transfers between devices: 335 us -> 307 us
  starting transfers between devices: 53.4 us -> 64.1 us
    ppermute x8, waiting for transfers between devices: 46.6 us -> 21 us  [the longest x3 7.42 us: ring_gather(): even = lax.ppermute(even, ('dp', 'expert'), walk(2))]
    ppermute x8, starting transfers between devices: 15.3 us -> 21.4 us  [the longest x3 8.58 us: ring_gather(): even = lax.ppermute(even, ('dp', 'expert'), walk(2))]
    unnamed x56 -> x54, local copies, waits for them, and re-layouts: 10.2 us -> 8.2 us
where the time goes in v9:
time: 455 us; the launch traced here: 453 us
  waiting for transfers between devices  307 us (67%)
  starting transfers between devices  64.1 us (14%)
  local copies, waits for them, and re-layouts  30.1 us (7%)
  matrix products  25.9 us (6%)
  between operations  13.9 us (3%)
  other arithmetic  12.1 us (3%)
    all_to_all x1, waiting for transfers between devices, local(): lax.all_to_all(out_slots, 'expert', split_axis=0, concat_axis=0, tiled=True)  141 us
    all_to_all x1, waiting for transfers between devices, local(): lax.all_to_all(outgoing, 'expert', split_axis=0, concat_axis=0, tiled=True)  138 us
    all_to_all x1, starting transfers between devices, local(): lax.all_to_all(outgoing, 'expert', split_axis=0, concat_axis=0, tiled=True)  14 us
    dot_general x1, matrix products, hidden_product(): return jnp.dot(active, down_part, preferred_element_type=jnp.float32)  10 us
    all_to_all x1, starting transfers between devices, local(): lax.all_to_all(outgoing_pack.reshape(owner_total, capacity, -1), 'dp', sp...  9.47 us
  transfers between devices with their start and end apart: 18, of which 11 were waited for; matrix products, arithmetic and copies ran while one was open for 8% of the time, Pallas kernels for 0%

profile of v9, /device:TPU:6, one launch (start us, length us, event | category | flops | bytes accessed | tf_op | source)
XLA Modules:
  0.0 453.4 jit_solution(17091335603697589033)
XLA Ops:
  6.5 3.5 collective-permute-start.1
  10.0 3.6 collective-permute-start
  20.2 9.5 %all-to-all-start = ((bf16[8,24,3712]{2,1,0:T(8,128)(2,1)}), bf16[8,24,3712]{2,1,0:T(8,128)(2,1)S(1)}, u32[]{:S(2)}, u32[]{:S(2)}) async-start(bf16[8,24,3712]{2,1,0:T(8,128)(2,1)} %bitcast.5), calls=%async_computation | async-start | bytes 2850816 | tf_op jit(solution)/shard_map/all_to_all | solution.py:195
  33.5 4.9 %collective-permute-done.2 = bf16[32,1024]{1,0:T(8,128)(2,1)S(1)} collective-permute-done((bf16[32,1024]{1,0:T(8,128)(2,1)S(1)}, bf16[32,1024]{1,0:T(8,128)(2,1)S(1)}, u32[]{:S(2)}, u32[]{:S(2)}) %collective-permute-start.2) | collective-permute-done | bytes 65568 | tf_op jit(solution)/shard_map/ppermute | solution.py:75
  40.5 2.5 collective-permute-start.4
  45.9 3.8 collective-permute-done.3
  49.7 2.6 collective-permute-start.5
  52.3 3.3 collective-permute-done.4
  59.3 3.7 collective-permute-done.5
  66.9 3.7 collective-permute-start.8
  72.3 2.3 collective-permute-done.7
  74.6 3.9 collective-permute-start.9
  79.9 3.0 collective-permute-start.10
  88.0 4.0 collective-permute-done.10
  104.5 2.2 multiply_reduce_fusion.1
  108.5 2.3 reshape.409
  110.8 14.0 %all-to-all-start.1 = ((bf16[64,20,1024]{2,1,0:T(8,128)(2,1)}), bf16[64,20,1024]{2,1,0:T(8,128)(2,1)S(1)}, u32[]{:S(2)}, u32[]{:S(2)}) async-start(bf16[64,20,1024]{2,1,0:T(8,128)(2,1)} %reshape.409), calls=%async_computation.1 | async-start | bytes 6291456 | tf_op jit(solution)/shard_map/all_to_all | solution.py:235
  127.1 138.5 %all-to-all-done.1 = bf16[64,20,1024]{2,1,0:T(8,128)(2,1)S(1)} async-done(((bf16[64,20,1024]{2,1,0:T(8,128)(2,1)}), bf16[64,20,1024]{2,1,0:T(8,128)(2,1)S(1)}, u32[]{:S(2)}, u32[]{:S(2)}) %all-to-all-start.1) | async-done | bytes 2621472 | tf_op jit(solution)/shard_map/all_to_all | solution.py:235
  267.8 6.4 %fusion.4 = f32[1280,768]{1,0:T(8,128)} fusion(bf16[1280,1024]{1,0:T(8,128)(2,1)} %reshape.410, bf16[1,768,1024]{2,1,0:T(8,128)(2,1)} %all-gather.4.cloned.1.call-done), kind=kOutput, calls=%fused_computation.13 | convolution fusion | flops 2013265920 | bytes 8126464 | tf_op jit(solution)/shard_map/dot_general | solution.py:139
  274.2 10.0 %convolution_convert_fusion = bf16[1280,1024]{1,0:T(8,128)(2,1)} fusion(bf16[1,768,1024]{2,1,0:T(8,128)(2,1)} %all-gather.8.cloned.1.call-done, bf16[1280,1024]{1,0:T(8,128)(2,1)S(1)} %copy-done.3, f32[1280,768]{1,0:T(8,128)} %fusion.4, bf16[1,768,1024]{2,1,0:T(8,128)(2,1)} %all-gather.6.cloned.1.call-done), kind=kOutput, calls=%fused_computation.8 | convolution fusion | flops 4033740800 | bytes 12320768 | tf_op jit(solution)/shard_map/dot_general | solution.py:142
  284.3 5.2 %reshape.411 = bf16[64,20,1024]{2,1,0:T(8,128)(2,1)} reshape(bf16[1280,1024]{1,0:T(8,128)(2,1)} %convolution_convert_fusion) | data formatting | bytes 5242880 | tf_op jit(solution)/shard_map/reshape | solution.py:244
  289.4 8.0 %all-to-all-start.2 = ((bf16[64,20,1024]{2,1,0:T(8,128)(2,1)}), bf16[64,20,1024]{2,1,0:T(8,128)(2,1)}, u32[]{:S(2)}, u32[]{:S(2)}) async-start(bf16[64,20,1024]{2,1,0:T(8,128)(2,1)} %reshape.411), calls=%async_computation.2 | async-start | bytes 6291456 | tf_op jit(solution)/shard_map/all_to_all | solution.py:245
  299.4 141.0 %all-to-all-done.2 = bf16[64,20,1024]{2,1,0:T(8,128)(2,1)} async-done(((bf16[64,20,1024]{2,1,0:T(8,128)(2,1)}), bf16[64,20,1024]{2,1,0:T(8,128)(2,1)}, u32[]{:S(2)}, u32[]{:S(2)}) %all-to-all-start.2) | async-done | bytes 2621472 | tf_op jit(solution)/shard_map/all_to_all | solution.py:245
  440.4 3.6 reshape.412
  (156 shorter events, 54.0 us)
Async XLA Ops:
  6.5 24.6 %collective-permute-start.1 = (bf16[32,1024]{1,0:T(8,128)(2,1)}, bf16[32,1024]{1,0:T(8,128)(2,1)S(1)}, u32[]{:S(2)}, u32[]{:S(2)}) collective-permute-start(bf16[32,1024]{1,0:T(8,128)(2,1)} %param.25), channel_id=1, source_target_pairs={{0,16},{1,17},{2,18},{3,19},{4,20},{5,21},{6,22},{7,23},{8,24},{9,... | collective-permute-start | bytes 196616 | tf_op jit(solution)/shard_map/ppermute | solution.py:73
  10.0 23.5 %collective-permute-start = (bf16[32,1024]{1,0:T(8,128)(2,1)}, bf16[32,1024]{1,0:T(8,128)(2,1)S(1)}, u32[]{:S(2)}, u32[]{:S(2)}) collective-permute-start(bf16[32,1024]{1,0:T(8,128)(2,1)} %param.25), channel_id=1, source_target_pairs={{0,48},{1,49},{2,50},{3,51},{4,52},{5,53},{6,54},{7,55},{8,56},{9,... | collective-permute-start | bytes 196616 | tf_op jit(solution)/shard_map/ppermute | solution.py:74
  20.2 10.0 %copy-start.10 = (s32[128,8]{0,1:T(8,128)S(1)}, s32[128,8]{0,1:T(8,128)}, u32[]{:S(2)}) copy-start(s32[128,8]{0,1:T(8,128)} %param.27) | copy-start | bytes 12292
  20.2 18.3 %copy-start.9 = (bf16[32,1024]{1,0:T(8,128)(2,1)S(1)}, bf16[32,1024]{1,0:T(8,128)(2,1)}, u32[]{:S(2)}) copy-start(bf16[32,1024]{1,0:T(8,128)(2,1)} %param.25) | copy-start | bytes 196612
  20.2 72.5 %all-to-all-start = ((bf16[8,24,3712]{2,1,0:T(8,128)(2,1)}), bf16[8,24,3712]{2,1,0:T(8,128)(2,1)S(1)}, u32[]{:S(2)}, u32[]{:S(2)}) async-start(bf16[8,24,3712]{2,1,0:T(8,128)(2,1)} %bitcast.5), calls=%async_computation | async-start | bytes 2850816 | tf_op jit(solution)/shard_map/all_to_all | solution.py:195
  31.1 7.4 %collective-permute-start.2 = (bf16[32,1024]{1,0:T(8,128)(2,1)S(1)}, bf16[32,1024]{1,0:T(8,128)(2,1)S(1)}, u32[]{:S(2)}, u32[]{:S(2)}) collective-permute-start(bf16[32,1024]{1,0:T(8,128)(2,1)S(1)} %collective-permute-done.1), channel_id=1, source_target_pairs={{0,16},{1,17},{2,18},{3,19},{4,20},{5,21},{6,22},{7,23},{8,24},{9,... | collective-permute-start | bytes 196616 | tf_op jit(solution)/shard_map/ppermute | solution.py:75
  38.5 32.9 %copy-start.4 = (bf16[4,32,1024]{2,1,0:T(8,128)(2,1)}, bf16[4,32,1024]{2,1,0:T(8,128)(2,1)S(1)}, u32[]{:S(2)}) copy-start(bf16[4,32,1024]{2,1,0:T(8,128)(2,1)S(1)} %pad_maximum_fusion.2) | copy-start | bytes 786436
  38.5 11.2 %collective-permute-start.3 = (bf16[4,32,1024]{2,1,0:T(8,128)(2,1)S(1)}, bf16[4,32,1024]{2,1,0:T(8,128)(2,1)S(1)}, u32[]{:S(2)}, u32[]{:S(2)}) collective-permute-start(bf16[4,32,1024]{2,1,0:T(8,128)(2,1)S(1)} %pad_maximum_fusion.2), channel_id=1, source_target_pairs={{0,1},{1,2},{2,3},{3,4},{4,5},{5,6},{6,7},{7,8},{8,9},{9,10},{10,1... | collective-permute-start | bytes 786440 | tf_op jit(solution)/shard_map/ppermute | solution.py:85
  40.5 15.2 %collective-permute-start.4 = (bf16[4,32,1024]{2,1,0:T(8,128)(2,1)S(1)}, bf16[4,32,1024]{2,1,0:T(8,128)(2,1)S(1)}, u32[]{:S(2)}, u32[]{:S(2)}) collective-permute-start(bf16[4,32,1024]{2,1,0:T(8,128)(2,1)S(1)} %pad_maximum_fusion.2), channel_id=1, source_target_pairs={{0,2},{1,3},{2,4},{3,5},{4,6},{5,7},{6,8},{7,9},{8,10},{9,11},{10,... | collective-permute-start | bytes 786440 | tf_op jit(solution)/shard_map/ppermute | solution.py:86
  49.7 13.2 %collective-permute-start.5 = (bf16[4,32,1024]{2,1,0:T(8,128)(2,1)S(1)}, bf16[4,32,1024]{2,1,0:T(8,128)(2,1)S(1)}, u32[]{:S(2)}, u32[]{:S(2)}) collective-permute-start(bf16[4,32,1024]{2,1,0:T(8,128)(2,1)S(1)} %collective-permute-done.3), channel_id=1, source_target_pairs={{0,2},{1,3},{2,4},{3,5},{4,6},{5,7},{6,8},{7,9},{8,10},{9,11},{10,... | collective-permute-start | bytes 786440 | tf_op jit(solution)/shard_map/ppermute | solution.py:89
  55.7 11.3 %collective-permute-start.6 = (bf16[4,32,1024]{2,1,0:T(8,128)(2,1)S(1)}, bf16[4,32,1024]{2,1,0:T(8,128)(2,1)S(1)}, u32[]{:S(2)}, u32[]{:S(2)}) collective-permute-start(bf16[4,32,1024]{2,1,0:T(8,128)(2,1)S(1)} %collective-permute-done.4), channel_id=1, source_target_pairs={{0,2},{1,3},{2,4},{3,5},{4,6},{5,7},{6,8},{7,9},{8,10},{9,11},{10,... | collective-permute-start | bytes 786440 | tf_op jit(solution)/shard_map/ppermute | solution.py:90
  63.0 11.7 %collective-permute-start.7 = (bf16[4,32,1024]{2,1,0:T(8,128)(2,1)S(1)}, bf16[4,32,1024]{2,1,0:T(8,128)(2,1)S(1)}, u32[]{:S(2)}, u32[]{:S(2)}) collective-permute-start(bf16[4,32,1024]{2,1,0:T(8,128)(2,1)S(1)} %collective-permute-done.5), channel_id=1, source_target_pairs={{0,2},{1,3},{2,4},{3,5},{4,6},{5,7},{6,8},{7,9},{8,10},{9,11},{10,... | collective-permute-start | bytes 786440 | tf_op jit(solution)/shard_map/ppermute | solution.py:89
  66.9 13.0 %collective-permute-start.8 = (bf16[4,32,1024]{2,1,0:T(8,128)(2,1)S(1)}, bf16[4,32,1024]{2,1,0:T(8,128)(2,1)S(1)}, u32[]{:S(2)}, u32[]{:S(2)}) collective-permute-start(bf16[4,32,1024]{2,1,0:T(8,128)(2,1)S(1)} %collective-permute-done.6), channel_id=1, source_target_pairs={{0,2},{1,3},{2,4},{3,5},{4,6},{5,7},{6,8},{7,9},{8,10},{9,11},{10,... | collective-permute-start | bytes 786440 | tf_op jit(solution)/shard_map/ppermute | solution.py:90
  74.6 10.5 %collective-permute-start.9 = (bf16[4,32,1024]{2,1,0:T(8,128)(2,1)S(1)}, bf16[4,32,1024]{2,1,0:T(8,128)(2,1)S(1)}, u32[]{:S(2)}, u32[]{:S(2)}) collective-permute-start(bf16[4,32,1024]{2,1,0:T(8,128)(2,1)S(1)} %collective-permute-done.7), channel_id=1, source_target_pairs={{0,2},{1,3},{2,4},{3,5},{4,6},{5,7},{6,8},{7,9},{8,10},{9,11},{10,... | collective-permute-start | bytes 786440 | tf_op jit(solution)/shard_map/ppermute | solution.py:89
  79.9 12.1 %collective-permute-start.10 = (bf16[4,32,1024]{2,1,0:T(8,128)(2,1)S(1)}, bf16[4,32,1024]{2,1,0:T(8,128)(2,1)S(1)}, u32[]{:S(2)}, u32[]{:S(2)}) collective-permute-start(bf16[4,32,1024]{2,1,0:T(8,128)(2,1)S(1)} %collective-permute-done.8), channel_id=1, source_target_pairs={{0,2},{1,3},{2,4},{3,5},{4,6},{5,7},{6,8},{7,9},{8,10},{9,11},{10,... | collective-permute-start | bytes 786440 | tf_op jit(solution)/shard_map/ppermute | solution.py:90
  86.0 16.5 %collective-permute-start.11 = (bf16[7,4,32,1024]{3,2,1,0:T(8,128)(2,1)}, bf16[7,4,32,1024]{3,2,1,0:T(8,128)(2,1)}, u32[]{:S(2)}, u32[]{:S(2)}) collective-permute-start(bf16[7,4,32,1024]{3,2,1,0:T(8,128)(2,1)} %get-tuple-element.15), channel_id=1, source_target_pairs={{0,64},{64,0},{128,192},{192,128},{256,320},{320,256},{384,448},{4... | collective-permute-start | bytes 5505032 | tf_op jit(solution)/shard_map/ppermute | solution.py:93
  110.8 154.7 %all-to-all-start.1 = ((bf16[64,20,1024]{2,1,0:T(8,128)(2,1)}), bf16[64,20,1024]{2,1,0:T(8,128)(2,1)S(1)}, u32[]{:S(2)}, u32[]{:S(2)}) async-start(bf16[64,20,1024]{2,1,0:T(8,128)(2,1)} %reshape.409), calls=%async_computation.1 | async-start | bytes 6291456 | tf_op jit(solution)/shard_map/all_to_all | solution.py:235
  124.8 142.9 %all-gather.4.cloned.1.call-start = ((), (), s32[]{:S(2)}) async-start(), calls=%async_computation.3 | async-start | bytes 1769472 | tf_op jit(solution)/shard_map/all_gather | solution.py:238
  125.6 148.6 %all-gather.6.cloned.1.call-start = ((), (), s32[]{:S(2)}) async-start(), calls=%async_computation.4 | async-start | bytes 1769472 | tf_op jit(solution)/shard_map/all_gather | solution.py:239
  126.3 147.9 %all-gather.8.cloned.1.call-start = ((), (), s32[]{:S(2)}) async-start(), calls=%async_computation.5 | async-start | bytes 1769472 | tf_op jit(solution)/shard_map/all_gather | solution.py:240
  289.4 8.0 %copy-start.7 = (s32[128,64]{0,1:T(8,128)S(1)}, s32[128,64]{0,1:T(8,128)}, u32[]{:S(2)}) copy-start(s32[128,64]{0,1:T(8,128)} %copy-done.6) | copy-start | bytes 98308
  289.4 8.0 %copy-start.11 = (s32[128,8]{0,1:T(8,128)S(1)}, s32[128,8]{0,1:T(8,128)}, u32[]{:S(2)}) copy-start(s32[128,8]{0,1:T(8,128)} %param.27) | copy-start | bytes 12292
  289.4 8.2 %copy-start.13 = (f32[128,8]{0,1:T(8,128)S(1)}, f32[128,8]{0,1:T(8,128)}, u32[]{:S(2)}) copy-start(f32[128,8]{0,1:T(8,128)} %param.28) | copy-start | bytes 12292
  289.4 151.0 %all-to-all-start.2 = ((bf16[64,20,1024]{2,1,0:T(8,128)(2,1)}), bf16[64,20,1024]{2,1,0:T(8,128)(2,1)}, u32[]{:S(2)}, u32[]{:S(2)}) async-start(bf16[64,20,1024]{2,1,0:T(8,128)(2,1)} %reshape.411), calls=%async_computation.2 | async-start | bytes 6291456 | tf_op jit(solution)/shard_map/all_to_all | solution.py:245
  (17 other events, 30.5 us)
Sparse Core Ops, SparseCore 0:
  127.8 31.2 all-gather.3
  161.2 32.2 all-gather.5
  195.6 32.3 all-gather.7

commit v10 on v9

--- a/solution.py
+++ b/solution.py
@@ -72,7 +72,7 @@
     expert_total = rows * cols
     up = lax.ppermute(block, "expert", ring_pairs(rows, cols, 1, 0))
     down = lax.ppermute(block, "expert", ring_pairs(rows, cols, -1, 0))
-    up_two = lax.ppermute(up, "expert", ring_pairs(rows, cols, 1, 0))
+    up_two = lax.ppermute(block, "expert", ring_pairs(rows, cols, 2, 0))
     by_row = jnp.stack([block, down, up_two, up])
     def walk(stride):
         return [

time: 455 us -> 453 us (level)
  waiting for transfers between devices: 307 us -> 302 us
    ppermute x1, waiting for transfers between devices: 4.94 us -> 0.01 us  [ring_gather(): up_two = lax.ppermute(block, 'expert', ring_pairs(rows, cols, 2, 0))]
  transfers between devices with their start and end apart: 18 -> 18, of which waited for: 11 -> 10; matrix products, arithmetic and copies ran while one was open for 8% -> 8% of each run, Pallas kernels for 0% -> 0%
where the time goes in v10:
time: 453 us; the launch traced here: 452 us
  waiting for transfers between devices  302 us (67%)
  starting transfers between devices  67.6 us (15%)
  local copies, waits for them, and re-layouts  30.1 us (7%)
  matrix products  25.9 us (6%)
  between operations  13.9 us (3%)
  other arithmetic  12.1 us (3%)
    all_to_all x1, waiting for transfers between devices, local(): lax.all_to_all(out_slots, 'expert', split_axis=0, concat_axis=0, tiled=True)  141 us
    all_to_all x1, waiting for transfers between devices, local(): lax.all_to_all(outgoing, 'expert', split_axis=0, concat_axis=0, tiled=True)  139 us
    all_to_all x1, starting transfers between devices, local(): lax.all_to_all(outgoing, 'expert', split_axis=0, concat_axis=0, tiled=True)  15.6 us
    dot_general x1, matrix products, hidden_product(): return jnp.dot(active, down_part, preferred_element_type=jnp.float32)  10 us
  transfers between devices with their start and end apart: 18, of which 10 were waited for; matrix products, arithmetic and copies ran while one was open for 8% of the time, Pallas kernels for 0%

profile of v10, /device:TPU:6, one launch (start us, length us, event | category | flops | bytes accessed | tf_op | source)
XLA Modules:
  0.0 451.6 jit_solution(5051493309914958047)
XLA Ops:
  6.5 4.9 %collective-permute-start = (bf16[32,1024]{1,0:T(8,128)(2,1)}, bf16[32,1024]{1,0:T(8,128)(2,1)S(1)}, u32[]{:S(2)}, u32[]{:S(2)}) collective-permute-start(bf16[32,1024]{1,0:T(8,128)(2,1)} %param.25), channel_id=1, source_target_pairs={{0,48},{1,49},{2,50},{3,51},{4,52},{5,53},{6,54},{7,55},{8,56},{9,... | collective-permute-start | bytes 196616 | tf_op jit(solution)/shard_map/ppermute | solution.py:74
  11.5 2.5 collective-permute-start.1
  14.0 2.9 collective-permute-start.2
  23.5 6.9 %all-to-all-start = ((bf16[8,24,3712]{2,1,0:T(8,128)(2,1)}), bf16[8,24,3712]{2,1,0:T(8,128)(2,1)S(1)}, u32[]{:S(2)}, u32[]{:S(2)}) async-start(bf16[8,24,3712]{2,1,0:T(8,128)(2,1)} %bitcast.5), calls=%async_computation | async-start | bytes 2850816 | tf_op jit(solution)/shard_map/all_to_all | solution.py:195
  34.3 5.1 %collective-permute-start.4 = (bf16[4,32,1024]{2,1,0:T(8,128)(2,1)S(1)}, bf16[4,32,1024]{2,1,0:T(8,128)(2,1)S(1)}, u32[]{:S(2)}, u32[]{:S(2)}) collective-permute-start(bf16[4,32,1024]{2,1,0:T(8,128)(2,1)S(1)} %pad_maximum_fusion.2), channel_id=1, source_target_pairs={{0,2},{1,3},{2,4},{3,5},{4,6},{5,7},{6,8},{7,9},{8,10},{9,11},{10,... | collective-permute-start | bytes 786440 | tf_op jit(solution)/shard_map/ppermute | solution.py:86
  42.4 3.8 collective-permute-done.3
  46.2 2.6 collective-permute-start.5
  48.8 3.3 collective-permute-done.4
  55.7 3.7 collective-permute-done.5
  63.4 3.7 collective-permute-start.8
  68.8 2.3 collective-permute-done.7
  71.1 3.9 collective-permute-start.9
  76.3 3.0 collective-permute-start.10
  82.5 2.5 collective-permute-start.11
  85.0 3.5 collective-permute-done.10
  105.0 2.3 reshape.409
  107.3 15.6 %all-to-all-start.1 = ((bf16[64,20,1024]{2,1,0:T(8,128)(2,1)}), bf16[64,20,1024]{2,1,0:T(8,128)(2,1)S(1)}, u32[]{:S(2)}, u32[]{:S(2)}) async-start(bf16[64,20,1024]{2,1,0:T(8,128)(2,1)} %reshape.409), calls=%async_computation.1 | async-start | bytes 6291456 | tf_op jit(solution)/shard_map/all_to_all | solution.py:235
  125.2 138.6 %all-to-all-done.1 = bf16[64,20,1024]{2,1,0:T(8,128)(2,1)S(1)} async-done(((bf16[64,20,1024]{2,1,0:T(8,128)(2,1)}), bf16[64,20,1024]{2,1,0:T(8,128)(2,1)S(1)}, u32[]{:S(2)}, u32[]{:S(2)}) %all-to-all-start.1) | async-done | bytes 2621472 | tf_op jit(solution)/shard_map/all_to_all | solution.py:235
  265.9 6.4 %fusion.4 = f32[1280,768]{1,0:T(8,128)} fusion(bf16[1280,1024]{1,0:T(8,128)(2,1)} %reshape.410, bf16[1,768,1024]{2,1,0:T(8,128)(2,1)} %all-gather.4.cloned.1.call-done), kind=kOutput, calls=%fused_computation.13 | convolution fusion | flops 2013265920 | bytes 8126464 | tf_op jit(solution)/shard_map/dot_general | solution.py:139
  272.4 10.0 %convolution_convert_fusion = bf16[1280,1024]{1,0:T(8,128)(2,1)} fusion(bf16[1,768,1024]{2,1,0:T(8,128)(2,1)} %all-gather.8.cloned.1.call-done, bf16[1280,1024]{1,0:T(8,128)(2,1)S(1)} %copy-done.3, f32[1280,768]{1,0:T(8,128)} %fusion.4, bf16[1,768,1024]{2,1,0:T(8,128)(2,1)} %all-gather.6.cloned.1.call-done), kind=kOutput, calls=%fused_computation.8 | convolution fusion | flops 4033740800 | bytes 12320768 | tf_op jit(solution)/shard_map/dot_general | solution.py:142
  282.4 5.2 %reshape.411 = bf16[64,20,1024]{2,1,0:T(8,128)(2,1)} reshape(bf16[1280,1024]{1,0:T(8,128)(2,1)} %convolution_convert_fusion) | data formatting | bytes 5242880 | tf_op jit(solution)/shard_map/reshape | solution.py:244
  287.6 8.0 %all-to-all-start.2 = ((bf16[64,20,1024]{2,1,0:T(8,128)(2,1)}), bf16[64,20,1024]{2,1,0:T(8,128)(2,1)}, u32[]{:S(2)}, u32[]{:S(2)}) async-start(bf16[64,20,1024]{2,1,0:T(8,128)(2,1)} %reshape.411), calls=%async_computation.2 | async-start | bytes 6291456 | tf_op jit(solution)/shard_map/all_to_all | solution.py:245
  297.5 141.1 %all-to-all-done.2 = bf16[64,20,1024]{2,1,0:T(8,128)(2,1)} async-done(((bf16[64,20,1024]{2,1,0:T(8,128)(2,1)}), bf16[64,20,1024]{2,1,0:T(8,128)(2,1)}, u32[]{:S(2)}, u32[]{:S(2)}) %all-to-all-start.2) | async-done | bytes 2621472 | tf_op jit(solution)/shard_map/all_to_all | solution.py:245
  438.7 3.6 reshape.412
  (156 shorter events, 52.4 us)
Async XLA Ops:
  6.5 25.8 %collective-permute-start = (bf16[32,1024]{1,0:T(8,128)(2,1)}, bf16[32,1024]{1,0:T(8,128)(2,1)S(1)}, u32[]{:S(2)}, u32[]{:S(2)}) collective-permute-start(bf16[32,1024]{1,0:T(8,128)(2,1)} %param.25), channel_id=1, source_target_pairs={{0,48},{1,49},{2,50},{3,51},{4,52},{5,53},{6,54},{7,55},{8,56},{9,... | collective-permute-start | bytes 196616 | tf_op jit(solution)/shard_map/ppermute | solution.py:74
  11.5 20.9 %collective-permute-start.1 = (bf16[32,1024]{1,0:T(8,128)(2,1)}, bf16[32,1024]{1,0:T(8,128)(2,1)S(1)}, u32[]{:S(2)}, u32[]{:S(2)}) collective-permute-start(bf16[32,1024]{1,0:T(8,128)(2,1)} %param.25), channel_id=1, source_target_pairs={{0,32},{1,33},{2,34},{3,35},{4,36},{5,37},{6,38},{7,39},{8,40},{9,... | collective-permute-start | bytes 196616 | tf_op jit(solution)/shard_map/ppermute | solution.py:75
  14.0 18.3 %collective-permute-start.2 = (bf16[32,1024]{1,0:T(8,128)(2,1)}, bf16[32,1024]{1,0:T(8,128)(2,1)S(1)}, u32[]{:S(2)}, u32[]{:S(2)}) collective-permute-start(bf16[32,1024]{1,0:T(8,128)(2,1)} %param.25), channel_id=1, source_target_pairs={{0,16},{1,17},{2,18},{3,19},{4,20},{5,21},{6,22},{7,23},{8,24},{9,... | collective-permute-start | bytes 196616 | tf_op jit(solution)/shard_map/ppermute | solution.py:73
  23.5 7.5 %copy-start.10 = (s32[128,8]{0,1:T(8,128)S(1)}, s32[128,8]{0,1:T(8,128)}, u32[]{:S(2)}) copy-start(s32[128,8]{0,1:T(8,128)} %param.27) | copy-start | bytes 12292
  23.5 8.8 %copy-start.9 = (bf16[32,1024]{1,0:T(8,128)(2,1)S(1)}, bf16[32,1024]{1,0:T(8,128)(2,1)}, u32[]{:S(2)}) copy-start(bf16[32,1024]{1,0:T(8,128)(2,1)} %param.25) | copy-start | bytes 196612
  23.5 65.7 %all-to-all-start = ((bf16[8,24,3712]{2,1,0:T(8,128)(2,1)}), bf16[8,24,3712]{2,1,0:T(8,128)(2,1)S(1)}, u32[]{:S(2)}, u32[]{:S(2)}) async-start(bf16[8,24,3712]{2,1,0:T(8,128)(2,1)} %bitcast.5), calls=%async_computation | async-start | bytes 2850816 | tf_op jit(solution)/shard_map/all_to_all | solution.py:195
  32.4 35.5 %copy-start.4 = (bf16[4,32,1024]{2,1,0:T(8,128)(2,1)}, bf16[4,32,1024]{2,1,0:T(8,128)(2,1)S(1)}, u32[]{:S(2)}) copy-start(bf16[4,32,1024]{2,1,0:T(8,128)(2,1)S(1)} %pad_maximum_fusion.2) | copy-start | bytes 786436
  32.4 13.8 %collective-permute-start.3 = (bf16[4,32,1024]{2,1,0:T(8,128)(2,1)S(1)}, bf16[4,32,1024]{2,1,0:T(8,128)(2,1)S(1)}, u32[]{:S(2)}, u32[]{:S(2)}) collective-permute-start(bf16[4,32,1024]{2,1,0:T(8,128)(2,1)S(1)} %pad_maximum_fusion.2), channel_id=1, source_target_pairs={{0,1},{1,2},{2,3},{3,4},{4,5},{5,6},{6,7},{7,8},{8,9},{9,10},{10,1... | collective-permute-start | bytes 786440 | tf_op jit(solution)/shard_map/ppermute | solution.py:85
  34.3 17.8 %collective-permute-start.4 = (bf16[4,32,1024]{2,1,0:T(8,128)(2,1)S(1)}, bf16[4,32,1024]{2,1,0:T(8,128)(2,1)S(1)}, u32[]{:S(2)}, u32[]{:S(2)}) collective-permute-start(bf16[4,32,1024]{2,1,0:T(8,128)(2,1)S(1)} %pad_maximum_fusion.2), channel_id=1, source_target_pairs={{0,2},{1,3},{2,4},{3,5},{4,6},{5,7},{6,8},{7,9},{8,10},{9,11},{10,... | collective-permute-start | bytes 786440 | tf_op jit(solution)/shard_map/ppermute | solution.py:86
  46.2 13.2 %collective-permute-start.5 = (bf16[4,32,1024]{2,1,0:T(8,128)(2,1)S(1)}, bf16[4,32,1024]{2,1,0:T(8,128)(2,1)S(1)}, u32[]{:S(2)}, u32[]{:S(2)}) collective-permute-start(bf16[4,32,1024]{2,1,0:T(8,128)(2,1)S(1)} %collective-permute-done.3), channel_id=1, source_target_pairs={{0,2},{1,3},{2,4},{3,5},{4,6},{5,7},{6,8},{7,9},{8,10},{9,11},{10,... | collective-permute-start | bytes 786440 | tf_op jit(solution)/shard_map/ppermute | solution.py:89
  52.1 11.2 %collective-permute-start.6 = (bf16[4,32,1024]{2,1,0:T(8,128)(2,1)S(1)}, bf16[4,32,1024]{2,1,0:T(8,128)(2,1)S(1)}, u32[]{:S(2)}, u32[]{:S(2)}) collective-permute-start(bf16[4,32,1024]{2,1,0:T(8,128)(2,1)S(1)} %collective-permute-done.4), channel_id=1, source_target_pairs={{0,2},{1,3},{2,4},{3,5},{4,6},{5,7},{6,8},{7,9},{8,10},{9,11},{10,... | collective-permute-start | bytes 786440 | tf_op jit(solution)/shard_map/ppermute | solution.py:90
  59.4 11.7 %collective-permute-start.7 = (bf16[4,32,1024]{2,1,0:T(8,128)(2,1)S(1)}, bf16[4,32,1024]{2,1,0:T(8,128)(2,1)S(1)}, u32[]{:S(2)}, u32[]{:S(2)}) collective-permute-start(bf16[4,32,1024]{2,1,0:T(8,128)(2,1)S(1)} %collective-permute-done.5), channel_id=1, source_target_pairs={{0,2},{1,3},{2,4},{3,5},{4,6},{5,7},{6,8},{7,9},{8,10},{9,11},{10,... | collective-permute-start | bytes 786440 | tf_op jit(solution)/shard_map/ppermute | solution.py:89
  63.4 13.0 %collective-permute-start.8 = (bf16[4,32,1024]{2,1,0:T(8,128)(2,1)S(1)}, bf16[4,32,1024]{2,1,0:T(8,128)(2,1)S(1)}, u32[]{:S(2)}, u32[]{:S(2)}) collective-permute-start(bf16[4,32,1024]{2,1,0:T(8,128)(2,1)S(1)} %collective-permute-done.6), channel_id=1, source_target_pairs={{0,2},{1,3},{2,4},{3,5},{4,6},{5,7},{6,8},{7,9},{8,10},{9,11},{10,... | collective-permute-start | bytes 786440 | tf_op jit(solution)/shard_map/ppermute | solution.py:90
  71.1 10.5 %collective-permute-start.9 = (bf16[4,32,1024]{2,1,0:T(8,128)(2,1)S(1)}, bf16[4,32,1024]{2,1,0:T(8,128)(2,1)S(1)}, u32[]{:S(2)}, u32[]{:S(2)}) collective-permute-start(bf16[4,32,1024]{2,1,0:T(8,128)(2,1)S(1)} %collective-permute-done.7), channel_id=1, source_target_pairs={{0,2},{1,3},{2,4},{3,5},{4,6},{5,7},{6,8},{7,9},{8,10},{9,11},{10,... | collective-permute-start | bytes 786440 | tf_op jit(solution)/shard_map/ppermute | solution.py:89
  76.3 12.1 %collective-permute-start.10 = (bf16[4,32,1024]{2,1,0:T(8,128)(2,1)S(1)}, bf16[4,32,1024]{2,1,0:T(8,128)(2,1)S(1)}, u32[]{:S(2)}, u32[]{:S(2)}) collective-permute-start(bf16[4,32,1024]{2,1,0:T(8,128)(2,1)S(1)} %collective-permute-done.8), channel_id=1, source_target_pairs={{0,2},{1,3},{2,4},{3,5},{4,6},{5,7},{6,8},{7,9},{8,10},{9,11},{10,... | collective-permute-start | bytes 786440 | tf_op jit(solution)/shard_map/ppermute | solution.py:90
  82.5 16.5 %collective-permute-start.11 = (bf16[7,4,32,1024]{3,2,1,0:T(8,128)(2,1)}, bf16[7,4,32,1024]{3,2,1,0:T(8,128)(2,1)}, u32[]{:S(2)}, u32[]{:S(2)}) collective-permute-start(bf16[7,4,32,1024]{3,2,1,0:T(8,128)(2,1)} %get-tuple-element.15), channel_id=1, source_target_pairs={{0,64},{64,0},{128,192},{192,128},{256,320},{320,256},{384,448},{4... | collective-permute-start | bytes 5505032 | tf_op jit(solution)/shard_map/ppermute | solution.py:93
  107.3 156.4 %all-to-all-start.1 = ((bf16[64,20,1024]{2,1,0:T(8,128)(2,1)}), bf16[64,20,1024]{2,1,0:T(8,128)(2,1)S(1)}, u32[]{:S(2)}, u32[]{:S(2)}) async-start(bf16[64,20,1024]{2,1,0:T(8,128)(2,1)} %reshape.409), calls=%async_computation.1 | async-start | bytes 6291456 | tf_op jit(solution)/shard_map/all_to_all | solution.py:235
  123.0 143.0 %all-gather.4.cloned.1.call-start = ((), (), s32[]{:S(2)}) async-start(), calls=%async_computation.3 | async-start | bytes 1769472 | tf_op jit(solution)/shard_map/all_gather | solution.py:238
  123.7 148.7 %all-gather.6.cloned.1.call-start = ((), (), s32[]{:S(2)}) async-start(), calls=%async_computation.4 | async-start | bytes 1769472 | tf_op jit(solution)/shard_map/all_gather | solution.py:239
  124.4 148.0 %all-gather.8.cloned.1.call-start = ((), (), s32[]{:S(2)}) async-start(), calls=%async_computation.5 | async-start | bytes 1769472 | tf_op jit(solution)/shard_map/all_gather | solution.py:240
  287.6 8.0 %copy-start.7 = (s32[128,64]{0,1:T(8,128)S(1)}, s32[128,64]{0,1:T(8,128)}, u32[]{:S(2)}) copy-start(s32[128,64]{0,1:T(8,128)} %copy-done.6) | copy-start | bytes 98308
  287.6 8.0 %copy-start.11 = (s32[128,8]{0,1:T(8,128)S(1)}, s32[128,8]{0,1:T(8,128)}, u32[]{:S(2)}) copy-start(s32[128,8]{0,1:T(8,128)} %param.27) | copy-start | bytes 12292
  287.6 8.2 %copy-start.13 = (f32[128,8]{0,1:T(8,128)S(1)}, f32[128,8]{0,1:T(8,128)}, u32[]{:S(2)}) copy-start(f32[128,8]{0,1:T(8,128)} %param.28) | copy-start | bytes 12292
  287.6 151.1 %all-to-all-start.2 = ((bf16[64,20,1024]{2,1,0:T(8,128)(2,1)}), bf16[64,20,1024]{2,1,0:T(8,128)(2,1)}, u32[]{:S(2)}, u32[]{:S(2)}) async-start(bf16[64,20,1024]{2,1,0:T(8,128)(2,1)} %reshape.411), calls=%async_computation.2 | async-start | bytes 6291456 | tf_op jit(solution)/shard_map/all_to_all | solution.py:245
  (17 other events, 30.5 us)
Sparse Core Ops, SparseCore 0:
  125.9 31.2 all-gather.3
  159.3 32.2 all-gather.5
  193.7 32.3 all-gather.7

commit v11 on v10

--- a/solution.py
+++ b/solution.py
@@ -82,13 +82,20 @@
         ]
 
     half = cols // 2
-    odd = lax.ppermute(by_row, ("dp", "expert"), walk(1))
-    even = lax.ppermute(by_row, ("dp", "expert"), walk(2))
-    mine = [odd, even]
-    for _ in range(half // 2 - 1):
-        odd = lax.ppermute(odd, ("dp", "expert"), walk(2))
-        even = lax.ppermute(even, ("dp", "expert"), walk(2))
-        mine += [odd, even]
+    stride = 3
+    chains = [lax.ppermute(by_row, ("dp", "expert"), walk(s)) for s in range(1, stride + 1)]
+    found = {s: chains[s - 1] for s in range(1, stride + 1)}
+    reach = stride
+    while reach < half:
+        chains = [
+            lax.ppermute(chain, ("dp", "expert"), walk(stride))
+            for s, chain in enumerate(chains, start=reach + 1)
+            if s <= half
+        ]
+        for s, chain in enumerate(chains, start=reach + 1):
+            found[s] = chain
+        reach += stride
+    mine = [found[s] for s in range(1, half + 1)]
     mine = jnp.stack(mine)
     partner = lax.ppermute(mine[: half - 1], "dp", [(i, i ^ 1) for i in range(owners)])
     return by_row[None], mine, partner

time: 453 us -> 466 us (1.029)
  starting transfers between devices: 67.6 us -> 81.8 us
    ppermute x8, starting transfers between devices: 24 us -> 41.9 us  [the longest x5 27.1 us: ring_gather(): lax.ppermute(chain, ('dp', 'expert'), walk(stride))]
  transfers between devices with their start and end apart: 18 -> 18, of which waited for: 10 -> 6; matrix products, arithmetic and copies ran while one was open for 8% -> 8% of each run, Pallas kernels for 0% -> 0%
where the time goes in v11:
time: 466 us; the launch traced here: 464 us
  waiting for transfers between devices  300 us (64%)
  starting transfers between devices  81.8 us (18%)
  local copies, waits for them, and re-layouts  30.1 us (6%)
  matrix products  25.9 us (6%)
  between operations  13.9 us (3%)
  other arithmetic  12.1 us (3%)
    all_to_all x1, waiting for transfers between devices, local(): lax.all_to_all(out_slots, 'expert', split_axis=0, concat_axis=0, tiled=True)  141 us
    all_to_all x1, waiting for transfers between devices, local(): lax.all_to_all(outgoing, 'expert', split_axis=0, concat_axis=0, tiled=True)  141 us
    ppermute x5, starting transfers between devices, ring_gather(): lax.ppermute(chain, ('dp', 'expert'), walk(stride))  27.1 us
    ppermute x5, waiting for transfers between devices, ring_gather(): lax.ppermute(chain, ('dp', 'expert'), walk(stride))  16.3 us
    ppermute x3, starting transfers between devices, ring_gather(): lax.ppermute(by_row, ('dp', 'expert'), walk(s))  14.8 us
    all_to_all x1, starting transfers between devices, local(): lax.all_to_all(outgoing, 'expert', split_axis=0, concat_axis=0, tiled=True)  13.3 us
    dot_general x1, matrix products, hidden_product(): return jnp.dot(active, down_part, preferred_element_type=jnp.float32)  10 us
  transfers between devices with their start and end apart: 18, of which 6 were waited for; matrix products, arithmetic and copies ran while one was open for 8% of the time, Pallas kernels for 0%

profile of v11, /device:TPU:6, one launch (start us, length us, event | category | flops | bytes accessed | tf_op | source)
XLA Modules:
  0.0 464.3 jit_solution(222978595203538010)
XLA Ops:
  6.5 4.9 %collective-permute-start = (bf16[32,1024]{1,0:T(8,128)(2,1)}, bf16[32,1024]{1,0:T(8,128)(2,1)S(1)}, u32[]{:S(2)}, u32[]{:S(2)}) collective-permute-start(bf16[32,1024]{1,0:T(8,128)(2,1)} %param.25), channel_id=1, source_target_pairs={{0,48},{1,49},{2,50},{3,51},{4,52},{5,53},{6,54},{7,55},{8,56},{9,... | collective-permute-start | bytes 196616 | tf_op jit(solution)/shard_map/ppermute | solution.py:74
  11.5 2.5 collective-permute-start.1
  14.0 2.9 collective-permute-start.2
  23.5 6.9 %all-to-all-start = ((bf16[8,24,3712]{2,1,0:T(8,128)(2,1)}), bf16[8,24,3712]{2,1,0:T(8,128)(2,1)S(1)}, u32[]{:S(2)}, u32[]{:S(2)}) async-start(bf16[8,24,3712]{2,1,0:T(8,128)(2,1)} %bitcast.5), calls=%async_computation | async-start | bytes 2850816 | tf_op jit(solution)/shard_map/all_to_all | solution.py:202
  34.3 5.1 %collective-permute-start.4 = (bf16[4,32,1024]{2,1,0:T(8,128)(2,1)S(1)}, bf16[4,32,1024]{2,1,0:T(8,128)(2,1)S(1)}, u32[]{:S(2)}, u32[]{:S(2)}) collective-permute-start(bf16[4,32,1024]{2,1,0:T(8,128)(2,1)S(1)} %pad_maximum_fusion.2), channel_id=1, source_target_pairs={{0,2},{1,3},{2,4},{3,5},{4,6},{5,7},{6,8},{7,9},{8,10},{9,11},{10,... | collective-permute-start | bytes 786440 | tf_op jit(solution)/shard_map/ppermute | solution.py:86
  40.1 7.7 %collective-permute-start.5 = (bf16[4,32,1024]{2,1,0:T(8,128)(2,1)S(1)}, bf16[4,32,1024]{2,1,0:T(8,128)(2,1)S(1)}, u32[]{:S(2)}, u32[]{:S(2)}) collective-permute-start(bf16[4,32,1024]{2,1,0:T(8,128)(2,1)S(1)} %pad_maximum_fusion.2), channel_id=1, source_target_pairs={{0,3},{1,4},{2,5},{3,6},{4,7},{5,8},{6,9},{7,10},{8,11},{9,12},{10... | collective-permute-start | bytes 786440 | tf_op jit(solution)/shard_map/ppermute | solution.py:86
  50.1 6.8 %collective-permute-start.6 = (bf16[4,32,1024]{2,1,0:T(8,128)(2,1)S(1)}, bf16[4,32,1024]{2,1,0:T(8,128)(2,1)S(1)}, u32[]{:S(2)}, u32[]{:S(2)}) collective-permute-start(bf16[4,32,1024]{2,1,0:T(8,128)(2,1)S(1)} %collective-permute-done.3), channel_id=1, source_target_pairs={{0,3},{1,4},{2,5},{3,6},{4,7},{5,8},{6,9},{7,10},{8,11},{9,12},{10... | collective-permute-start | bytes 786440 | tf_op jit(solution)/shard_map/ppermute | solution.py:91
  57.0 3.8 collective-permute-start.7
  61.7 3.8 collective-permute-start.8
  68.1 5.8 %collective-permute-start.9 = (bf16[4,32,1024]{2,1,0:T(8,128)(2,1)S(1)}, bf16[4,32,1024]{2,1,0:T(8,128)(2,1)S(1)}, u32[]{:S(2)}, u32[]{:S(2)}) collective-permute-start(bf16[4,32,1024]{2,1,0:T(8,128)(2,1)S(1)} %collective-permute-done.6), channel_id=1, source_target_pairs={{0,3},{1,4},{2,5},{3,6},{4,7},{5,8},{6,9},{7,10},{8,11},{9,12},{10... | collective-permute-start | bytes 786440 | tf_op jit(solution)/shard_map/ppermute | solution.py:91
  74.0 6.8 %collective-permute-start.10 = (bf16[4,32,1024]{2,1,0:T(8,128)(2,1)S(1)}, bf16[4,32,1024]{2,1,0:T(8,128)(2,1)S(1)}, u32[]{:S(2)}, u32[]{:S(2)}) collective-permute-start(bf16[4,32,1024]{2,1,0:T(8,128)(2,1)S(1)} %collective-permute-done.7), channel_id=1, source_target_pairs={{0,3},{1,4},{2,5},{3,6},{4,7},{5,8},{6,9},{7,10},{8,11},{9,12},{10... | collective-permute-start | bytes 786440 | tf_op jit(solution)/shard_map/ppermute | solution.py:91
  82.5 3.5 collective-permute-done.8
  86.9 9.7 %collective-permute-done.9 = bf16[4,32,1024]{2,1,0:T(8,128)(2,1)S(1)} collective-permute-done((bf16[4,32,1024]{2,1,0:T(8,128)(2,1)S(1)}, bf16[4,32,1024]{2,1,0:T(8,128)(2,1)S(1)}, u32[]{:S(2)}, u32[]{:S(2)}) %collective-permute-start.9) | collective-permute-done | bytes 262176 | tf_op jit(solution)/shard_map/ppermute | solution.py:91
  99.4 2.2 collective-permute-done.10
  114.2 2.2 multiply_reduce_fusion.1
  118.2 2.3 reshape.409
  120.5 13.3 %all-to-all-start.1 = ((bf16[64,20,1024]{2,1,0:T(8,128)(2,1)}), bf16[64,20,1024]{2,1,0:T(8,128)(2,1)S(1)}, u32[]{:S(2)}, u32[]{:S(2)}) async-start(bf16[64,20,1024]{2,1,0:T(8,128)(2,1)} %reshape.409), calls=%async_computation.1 | async-start | bytes 6291456 | tf_op jit(solution)/shard_map/all_to_all | solution.py:242
  136.0 140.9 %all-to-all-done.1 = bf16[64,20,1024]{2,1,0:T(8,128)(2,1)S(1)} async-done(((bf16[64,20,1024]{2,1,0:T(8,128)(2,1)}), bf16[64,20,1024]{2,1,0:T(8,128)(2,1)S(1)}, u32[]{:S(2)}, u32[]{:S(2)}) %all-to-all-start.1) | async-done | bytes 2621472 | tf_op jit(solution)/shard_map/all_to_all | solution.py:242
  279.2 6.4 %fusion.4 = f32[1280,768]{1,0:T(8,128)} fusion(bf16[1280,1024]{1,0:T(8,128)(2,1)} %reshape.410, bf16[1,768,1024]{2,1,0:T(8,128)(2,1)} %all-gather.4.cloned.1.call-done), kind=kOutput, calls=%fused_computation.13 | convolution fusion | flops 2013265920 | bytes 8126464 | tf_op jit(solution)/shard_map/dot_general | solution.py:146
  285.6 10.0 %convolution_convert_fusion = bf16[1280,1024]{1,0:T(8,128)(2,1)} fusion(bf16[1,768,1024]{2,1,0:T(8,128)(2,1)} %all-gather.8.cloned.1.call-done, bf16[1280,1024]{1,0:T(8,128)(2,1)S(1)} %copy-done.3, f32[1280,768]{1,0:T(8,128)} %fusion.4, bf16[1,768,1024]{2,1,0:T(8,128)(2,1)} %all-gather.6.cloned.1.call-done), kind=kOutput, calls=%fused_computation.8 | convolution fusion | flops 4033740800 | bytes 12320768 | tf_op jit(solution)/shard_map/dot_general | solution.py:149
  295.6 5.2 %reshape.411 = bf16[64,20,1024]{2,1,0:T(8,128)(2,1)} reshape(bf16[1280,1024]{1,0:T(8,128)(2,1)} %convolution_convert_fusion) | data formatting | bytes 5242880 | tf_op jit(solution)/shard_map/reshape | solution.py:251
  300.8 7.2 %all-to-all-start.2 = ((bf16[64,20,1024]{2,1,0:T(8,128)(2,1)}), bf16[64,20,1024]{2,1,0:T(8,128)(2,1)}, u32[]{:S(2)}, u32[]{:S(2)}) async-start(bf16[64,20,1024]{2,1,0:T(8,128)(2,1)} %reshape.411), calls=%async_computation.2 | async-start | bytes 6291456 | tf_op jit(solution)/shard_map/all_to_all | solution.py:252
  310.0 141.3 %all-to-all-done.2 = bf16[64,20,1024]{2,1,0:T(8,128)(2,1)} async-done(((bf16[64,20,1024]{2,1,0:T(8,128)(2,1)}), bf16[64,20,1024]{2,1,0:T(8,128)(2,1)}, u32[]{:S(2)}, u32[]{:S(2)}) %all-to-all-start.2) | async-done | bytes 2621472 | tf_op jit(solution)/shard_map/all_to_all | solution.py:252
  451.3 3.6 reshape.412
  (156 shorter events, 45.1 us)
Async XLA Ops:
  6.5 25.8 %collective-permute-start = (bf16[32,1024]{1,0:T(8,128)(2,1)}, bf16[32,1024]{1,0:T(8,128)(2,1)S(1)}, u32[]{:S(2)}, u32[]{:S(2)}) collective-permute-start(bf16[32,1024]{1,0:T(8,128)(2,1)} %param.25), channel_id=1, source_target_pairs={{0,48},{1,49},{2,50},{3,51},{4,52},{5,53},{6,54},{7,55},{8,56},{9,... | collective-permute-start | bytes 196616 | tf_op jit(solution)/shard_map/ppermute | solution.py:74
  11.5 20.9 %collective-permute-start.1 = (bf16[32,1024]{1,0:T(8,128)(2,1)}, bf16[32,1024]{1,0:T(8,128)(2,1)S(1)}, u32[]{:S(2)}, u32[]{:S(2)}) collective-permute-start(bf16[32,1024]{1,0:T(8,128)(2,1)} %param.25), channel_id=1, source_target_pairs={{0,32},{1,33},{2,34},{3,35},{4,36},{5,37},{6,38},{7,39},{8,40},{9,... | collective-permute-start | bytes 196616 | tf_op jit(solution)/shard_map/ppermute | solution.py:75
  14.0 18.3 %collective-permute-start.2 = (bf16[32,1024]{1,0:T(8,128)(2,1)}, bf16[32,1024]{1,0:T(8,128)(2,1)S(1)}, u32[]{:S(2)}, u32[]{:S(2)}) collective-permute-start(bf16[32,1024]{1,0:T(8,128)(2,1)} %param.25), channel_id=1, source_target_pairs={{0,16},{1,17},{2,18},{3,19},{4,20},{5,21},{6,22},{7,23},{8,24},{9,... | collective-permute-start | bytes 196616 | tf_op jit(solution)/shard_map/ppermute | solution.py:73
  23.5 7.5 %copy-start.10 = (s32[128,8]{0,1:T(8,128)S(1)}, s32[128,8]{0,1:T(8,128)}, u32[]{:S(2)}) copy-start(s32[128,8]{0,1:T(8,128)} %param.27) | copy-start | bytes 12292
  23.5 8.8 %copy-start.9 = (bf16[32,1024]{1,0:T(8,128)(2,1)S(1)}, bf16[32,1024]{1,0:T(8,128)(2,1)}, u32[]{:S(2)}) copy-start(bf16[32,1024]{1,0:T(8,128)(2,1)} %param.25) | copy-start | bytes 196612
  23.5 78.9 %all-to-all-start = ((bf16[8,24,3712]{2,1,0:T(8,128)(2,1)}), bf16[8,24,3712]{2,1,0:T(8,128)(2,1)S(1)}, u32[]{:S(2)}, u32[]{:S(2)}) async-start(bf16[8,24,3712]{2,1,0:T(8,128)(2,1)} %bitcast.5), calls=%async_computation | async-start | bytes 2850816 | tf_op jit(solution)/shard_map/all_to_all | solution.py:202
  32.4 34.9 %copy-start.4 = (bf16[4,32,1024]{2,1,0:T(8,128)(2,1)}, bf16[4,32,1024]{2,1,0:T(8,128)(2,1)S(1)}, u32[]{:S(2)}) copy-start(bf16[4,32,1024]{2,1,0:T(8,128)(2,1)S(1)} %pad_maximum_fusion.2) | copy-start | bytes 786436
  32.4 17.7 %collective-permute-start.3 = (bf16[4,32,1024]{2,1,0:T(8,128)(2,1)S(1)}, bf16[4,32,1024]{2,1,0:T(8,128)(2,1)S(1)}, u32[]{:S(2)}, u32[]{:S(2)}) collective-permute-start(bf16[4,32,1024]{2,1,0:T(8,128)(2,1)S(1)} %pad_maximum_fusion.2), channel_id=1, source_target_pairs={{0,1},{1,2},{2,3},{3,4},{4,5},{5,6},{6,7},{7,8},{8,9},{9,10},{10,1... | collective-permute-start | bytes 786440 | tf_op jit(solution)/shard_map/ppermute | solution.py:86
  34.3 22.7 %collective-permute-start.4 = (bf16[4,32,1024]{2,1,0:T(8,128)(2,1)S(1)}, bf16[4,32,1024]{2,1,0:T(8,128)(2,1)S(1)}, u32[]{:S(2)}, u32[]{:S(2)}) collective-permute-start(bf16[4,32,1024]{2,1,0:T(8,128)(2,1)S(1)} %pad_maximum_fusion.2), channel_id=1, source_target_pairs={{0,2},{1,3},{2,4},{3,5},{4,6},{5,7},{6,8},{7,9},{8,10},{9,11},{10,... | collective-permute-start | bytes 786440 | tf_op jit(solution)/shard_map/ppermute | solution.py:86
  40.1 21.6 %collective-permute-start.5 = (bf16[4,32,1024]{2,1,0:T(8,128)(2,1)S(1)}, bf16[4,32,1024]{2,1,0:T(8,128)(2,1)S(1)}, u32[]{:S(2)}, u32[]{:S(2)}) collective-permute-start(bf16[4,32,1024]{2,1,0:T(8,128)(2,1)S(1)} %pad_maximum_fusion.2), channel_id=1, source_target_pairs={{0,3},{1,4},{2,5},{3,6},{4,7},{5,8},{6,9},{7,10},{8,11},{9,12},{10... | collective-permute-start | bytes 786440 | tf_op jit(solution)/shard_map/ppermute | solution.py:86
  50.1 18.0 %collective-permute-start.6 = (bf16[4,32,1024]{2,1,0:T(8,128)(2,1)S(1)}, bf16[4,32,1024]{2,1,0:T(8,128)(2,1)S(1)}, u32[]{:S(2)}, u32[]{:S(2)}) collective-permute-start(bf16[4,32,1024]{2,1,0:T(8,128)(2,1)S(1)} %collective-permute-done.3), channel_id=1, source_target_pairs={{0,3},{1,4},{2,5},{3,6},{4,7},{5,8},{6,9},{7,10},{8,11},{9,12},{10... | collective-permute-start | bytes 786440 | tf_op jit(solution)/shard_map/ppermute | solution.py:91
  57.0 16.9 %collective-permute-start.7 = (bf16[4,32,1024]{2,1,0:T(8,128)(2,1)S(1)}, bf16[4,32,1024]{2,1,0:T(8,128)(2,1)S(1)}, u32[]{:S(2)}, u32[]{:S(2)}) collective-permute-start(bf16[4,32,1024]{2,1,0:T(8,128)(2,1)S(1)} %collective-permute-done.4), channel_id=1, source_target_pairs={{0,3},{1,4},{2,5},{3,6},{4,7},{5,8},{6,9},{7,10},{8,11},{9,12},{10... | collective-permute-start | bytes 786440 | tf_op jit(solution)/shard_map/ppermute | solution.py:91
  61.7 24.3 %collective-permute-start.8 = (bf16[4,32,1024]{2,1,0:T(8,128)(2,1)S(1)}, bf16[4,32,1024]{2,1,0:T(8,128)(2,1)S(1)}, u32[]{:S(2)}, u32[]{:S(2)}) collective-permute-start(bf16[4,32,1024]{2,1,0:T(8,128)(2,1)S(1)} %collective-permute-done.5), channel_id=1, source_target_pairs={{0,3},{1,4},{2,5},{3,6},{4,7},{5,8},{6,9},{7,10},{8,11},{9,12},{10... | collective-permute-start | bytes 786440 | tf_op jit(solution)/shard_map/ppermute | solution.py:91
  68.1 28.5 %collective-permute-start.9 = (bf16[4,32,1024]{2,1,0:T(8,128)(2,1)S(1)}, bf16[4,32,1024]{2,1,0:T(8,128)(2,1)S(1)}, u32[]{:S(2)}, u32[]{:S(2)}) collective-permute-start(bf16[4,32,1024]{2,1,0:T(8,128)(2,1)S(1)} %collective-permute-done.6), channel_id=1, source_target_pairs={{0,3},{1,4},{2,5},{3,6},{4,7},{5,8},{6,9},{7,10},{8,11},{9,12},{10... | collective-permute-start | bytes 786440 | tf_op jit(solution)/shard_map/ppermute | solution.py:91
  74.0 27.7 %collective-permute-start.10 = (bf16[4,32,1024]{2,1,0:T(8,128)(2,1)S(1)}, bf16[4,32,1024]{2,1,0:T(8,128)(2,1)S(1)}, u32[]{:S(2)}, u32[]{:S(2)}) collective-permute-start(bf16[4,32,1024]{2,1,0:T(8,128)(2,1)S(1)} %collective-permute-done.7), channel_id=1, source_target_pairs={{0,3},{1,4},{2,5},{3,6},{4,7},{5,8},{6,9},{7,10},{8,11},{9,12},{10... | collective-permute-start | bytes 786440 | tf_op jit(solution)/shard_map/ppermute | solution.py:91
  97.5 14.7 %collective-permute-start.11 = (bf16[7,4,32,1024]{3,2,1,0:T(8,128)(2,1)}, bf16[7,4,32,1024]{3,2,1,0:T(8,128)(2,1)}, u32[]{:S(2)}, u32[]{:S(2)}) collective-permute-start(bf16[7,4,32,1024]{3,2,1,0:T(8,128)(2,1)} %get-tuple-element.15), channel_id=1, source_target_pairs={{0,64},{64,0},{128,192},{192,128},{256,320},{320,256},{384,448},{4... | collective-permute-start | bytes 5505032 | tf_op jit(solution)/shard_map/ppermute | solution.py:100
  120.5 156.4 %all-to-all-start.1 = ((bf16[64,20,1024]{2,1,0:T(8,128)(2,1)}), bf16[64,20,1024]{2,1,0:T(8,128)(2,1)S(1)}, u32[]{:S(2)}, u32[]{:S(2)}) async-start(bf16[64,20,1024]{2,1,0:T(8,128)(2,1)} %reshape.409), calls=%async_computation.1 | async-start | bytes 6291456 | tf_op jit(solution)/shard_map/all_to_all | solution.py:242
  133.8 145.3 %all-gather.4.cloned.1.call-start = ((), (), s32[]{:S(2)}) async-start(), calls=%async_computation.3 | async-start | bytes 1769472 | tf_op jit(solution)/shard_map/all_gather | solution.py:245
  134.6 151.0 %all-gather.6.cloned.1.call-start = ((), (), s32[]{:S(2)}) async-start(), calls=%async_computation.4 | async-start | bytes 1769472 | tf_op jit(solution)/shard_map/all_gather | solution.py:246
  135.3 150.3 %all-gather.8.cloned.1.call-start = ((), (), s32[]{:S(2)}) async-start(), calls=%async_computation.5 | async-start | bytes 1769472 | tf_op jit(solution)/shard_map/all_gather | solution.py:247
  300.8 7.2 %copy-start.7 = (s32[128,64]{0,1:T(8,128)S(1)}, s32[128,64]{0,1:T(8,128)}, u32[]{:S(2)}) copy-start(s32[128,64]{0,1:T(8,128)} %copy-done.6) | copy-start | bytes 98308
  300.8 7.2 %copy-start.11 = (s32[128,8]{0,1:T(8,128)S(1)}, s32[128,8]{0,1:T(8,128)}, u32[]{:S(2)}) copy-start(s32[128,8]{0,1:T(8,128)} %param.27) | copy-start | bytes 12292
  300.8 7.4 %copy-start.13 = (f32[128,8]{0,1:T(8,128)S(1)}, f32[128,8]{0,1:T(8,128)}, u32[]{:S(2)}) copy-start(f32[128,8]{0,1:T(8,128)} %param.28) | copy-start | bytes 12292
  300.8 150.5 %all-to-all-start.2 = ((bf16[64,20,1024]{2,1,0:T(8,128)(2,1)}), bf16[64,20,1024]{2,1,0:T(8,128)(2,1)}, u32[]{:S(2)}, u32[]{:S(2)}) async-start(bf16[64,20,1024]{2,1,0:T(8,128)(2,1)} %reshape.411), calls=%async_computation.2 | async-start | bytes 6291456 | tf_op jit(solution)/shard_map/all_to_all | solution.py:252
  (17 other events, 30.5 us)
Sparse Core Ops, SparseCore 0:
  136.7 31.2 all-gather.3
  170.2 32.2 all-gather.5
  204.6 32.3 all-gather.7
